TPU v7x, 128 devices: a whole 4x4x4 slice. The times are simulated.
128 devices in a mesh: head: 8 (over y, core), blk: 16 (over x, z).
Axes of the slice: x: 4, y: 4, z: 4, core: 2. Of those that a mesh axis runs over, the one named last changes fastest.
Arguments:
- states: bfloat16 [16384, 4096], P('blk', 'head'), may hold values from -6 to 6
- qkv_weight: bfloat16 [3, 4096, 4096], P(None, None, 'head'), may hold values from -1 to 1
- norm_gains: bfloat16 [2, 4096], P(None, 'head'), may hold values from 0.5 to 2
- kv_cache: bfloat16 [2, 640, 64, 4096], P(None, 'blk', None, 'head'), may hold values from -300 to 300
- cached_len: int32 [8], replicated, may hold values from 1 to 4096, as said below
- old_table: int32 [8, 64], replicated, may hold values from -1 to 639, as said below
- new_table: int32 [8, 32], replicated, may hold values from 0 to 639, as said below
Outputs:
- attended: bfloat16 [16384, 4096], P('blk', 'head')
- updated_cache: bfloat16 [2, 640, 64, 4096], P(None, 'blk', None, 'head')
Inputs may be any that keep to these rules, and one draw needn't show every extreme that they name: `cached_len`: one request has exactly 4096 cached tokens. old_table[r, b] is d * 40 plus a local slot for the blocks b of request r below the ceiling of cached_len[r] / 64, and -1 beyond; block b of request r lies on blk index d = (o + b) mod 16, where o is the index of its block 0. New block j of request r lies on blk index (p + j // 2) mod 16, where p is the index of its block 0; no slot appears twice in old_table and new_table together.
All inputs are finite; a program needn't handle non-finite values.
Results may differ from a plain program's by a relative error of at most 0.014.
The roundings to bfloat16 on the way count: a program that leaves them out, or rounds other values in their place, can miss the bound.
Values may be sent and summed in bfloat16 or wider, within the bound.
No kernel may reach another device: no remote copies, remote signals or barrier semaphores. Data moves between devices by JAX's collectives and lax.ppermute only.
A program may use at most 192 MiB of HBM per device.

v0:
```python
import jax
import jax.numpy as jnp
from jax import lax
from jax.sharding import PartitionSpec as P

D = 4096
HS = 128


rope_base = 500000.0
norm_eps = 1e-06


def swapped(block, axis, apart):
    count = lax.axis_size(axis)
    route = []
    for low in range(count):
        high = low | 1 << apart
        if high != low and high < count:
            route += [(low, high), (high, low)]
    return lax.ppermute(block, axis, route)


def rotate(values, positions, head_size):
    half_size = head_size // 2
    frequency = rope_base ** (-jnp.arange(half_size, dtype=jnp.float32) * 2.0 / head_size)
    angles = positions.astype(jnp.float32)[:, None] * frequency[None, :]
    cosine = jnp.cos(angles)[:, None, :]
    sine_part = jnp.sin(angles)[:, None, :]
    first_half = values[..., :half_size]
    second = values[..., half_size:]
    return jnp.concatenate(
        [first_half * cosine - second * sine_part, second * cosine + first_half * sine_part],
        axis=-1,
    )


def body(states, qkv_weight, norm_gains, kv_cache, cached_len, old_table, new_table):
    tok_rows = states.shape[0]
    half_rows = tok_rows // 2
    local_width = qkv_weight.shape[2]
    local_heads = local_width // HS
    groups = lax.axis_size("blk")
    slot_count = kv_cache.shape[1]
    block_len = kv_cache.shape[2]
    requests = cached_len.shape[0]
    group_size = groups // requests
    per_dev = old_table.shape[1] // groups
    my_index = lax.axis_index("blk")
    request = my_index // group_size
    member = my_index % group_size
    late_block = 2 * group_size - 1 - member
    projected = jnp.einsum(
        "tc,jcw->tjw",
        lax.all_gather(states, "head", axis=1, tiled=True),
        qkv_weight,
        preferred_element_type=jnp.float32,
    )
    queries = projected[:, 0]
    key_new = projected[:, 1]
    value_new = projected[:, 2]
    query_sq, key_sq = lax.psum(
        (jnp.sum(queries * queries, axis=1), jnp.sum(key_new * key_new, axis=1)), "head"
    )
    gains = norm_gains.astype(jnp.float32)
    queries = queries * lax.rsqrt(query_sq / D + norm_eps)[:, None] * gains[0]
    key_new = key_new * lax.rsqrt(key_sq / D + norm_eps)[:, None] * gains[1]
    half_ids = jnp.arange(half_rows, dtype=jnp.int32)
    token_offset = jnp.concatenate(
        [member * half_rows + half_ids, late_block * half_rows + half_ids]
    )
    positions = cached_len[request] + token_offset
    queries = (
        rotate(queries.reshape(tok_rows, local_heads, HS), positions, HS)
        .reshape(tok_rows, local_width)
        .astype(jnp.bfloat16)
    )
    key_new = (
        rotate(key_new.reshape(tok_rows, local_heads, HS), positions, HS)
        .reshape(tok_rows, local_width)
        .astype(jnp.bfloat16)
    )
    value_new = value_new.astype(jnp.bfloat16)
    fresh_kv = jnp.stack([key_new, value_new])
    blocks_dev = tok_rows // block_len
    half_blocks = blocks_dev // 2
    new_count = new_table.shape[1]
    fresh_blocks = fresh_kv.reshape(2, blocks_dev, block_len, local_width)
    targets = jnp.arange(groups, dtype=jnp.int32)
    pair_index = jnp.arange(2, dtype=jnp.int32)
    new_home = new_table[:, 0] // slot_count
    wanted_out = 2 * ((targets - new_home[request]) % groups)[:, None] + pair_index[None, :]
    out_half = wanted_out // half_blocks
    local_index = jnp.where(
        out_half == member,
        wanted_out - member * half_blocks,
        wanted_out - late_block * half_blocks + half_blocks,
    )
    usable = (out_half == member) | (out_half == late_block)
    picked = jnp.take(fresh_blocks, jnp.clip(local_index, 0, blocks_dev - 1).reshape(-1), axis=1)
    picked = picked.reshape(2, groups, 2, block_len, local_width)
    picked = jnp.where(usable[None, :, :, None, None], picked, jnp.zeros((), jnp.bfloat16))
    arrived = lax.all_to_all(picked, "blk", split_axis=1, concat_axis=1, tiled=True)
    source_req = targets // group_size
    source_member = targets % group_size
    source_late = 2 * group_size - 1 - source_member
    wanted_in = 2 * ((my_index - new_home[source_req]) % groups)[:, None] + pair_index[None, :]
    in_half = wanted_in // half_blocks
    valid_in = (in_half == source_member[:, None]) | (in_half == source_late[:, None])
    target_slot = (
        new_table[source_req[:, None], jnp.clip(wanted_in, 0, new_count - 1)]
        - my_index * slot_count
    )
    target_slot = jnp.where(valid_in, target_slot, slot_count)
    updated_cache = kv_cache.at[:, target_slot.reshape(-1)].set(
        arrived.reshape(2, groups * 2, block_len, local_width), mode="drop"
    )
    lengths_blocks = jnp.sum((old_table >= 0).astype(jnp.int32), axis=1)
    first_dev = old_table[:, 0] // slot_count
    target_req = targets // group_size
    c_index = jnp.broadcast_to(jnp.arange(per_dev, dtype=jnp.int32)[None, :], (groups, per_dev))
    block_index = ((my_index - first_dev[target_req]) % groups)[:, None] + groups * c_index
    present = block_index < lengths_blocks[target_req][:, None]
    slot_index = (
        old_table[target_req[:, None], jnp.clip(block_index, 0, old_table.shape[1] - 1)]
        - my_index * slot_count
    )
    slot_index = jnp.clip(slot_index, 0, slot_count - 1)
    outgoing = jnp.take(kv_cache, slot_index.reshape(-1), axis=1).reshape(
        2, groups, per_dev, block_len, local_width
    )
    outgoing = jnp.where(present[None, :, :, None, None], outgoing, jnp.zeros((), jnp.bfloat16))
    received = lax.all_to_all(outgoing, "blk", split_axis=1, concat_axis=1, tiled=True)
    c_received = jnp.arange(per_dev, dtype=jnp.int32)
    source_first = (targets - first_dev[request]) % groups
    block_recv = source_first[:, None] + groups * c_received[None, :]
    key_pos = (
        block_recv[:, :, None] * block_len + jnp.arange(block_len, dtype=jnp.int32)[None, None, :]
    )
    cached_mask = jnp.broadcast_to(
        (key_pos < cached_len[request]).reshape(1, -1), (tok_rows, key_pos.size)
    )
    cached_keys = received[0].reshape(-1, local_width)
    cached_values = received[1].reshape(-1, local_width)
    collected = fresh_kv
    partner_new = swapped(collected, "blk", 0)
    lower_new = member // 2**0 % 2 == 0
    collected = jnp.where(
        lower_new,
        jnp.concatenate([collected, partner_new], axis=1),
        jnp.concatenate([partner_new, collected], axis=1),
    )
    member_ids = jnp.arange(group_size, dtype=jnp.int32)[:, None]
    group_ids = jnp.concatenate(
        [
            member_ids * half_rows + half_ids[None, :],
            (2 * group_size - 1 - member_ids) * half_rows + half_ids[None, :],
        ],
        axis=1,
    ).reshape(-1)
    group_mask = group_ids[None, :] <= token_offset[:, None]
    all_keys = jnp.concatenate([cached_keys, collected[0]], axis=0)
    all_values = jnp.concatenate([cached_values, collected[1]], axis=0)
    full_mask = jnp.concatenate([cached_mask, group_mask], axis=1)
    score_scale = HS ** (-0.5)

    def one_head(head_index):
        q_head = lax.dynamic_slice_in_dim(queries, head_index * HS, HS, 1)
        k_head = lax.dynamic_slice_in_dim(all_keys, head_index * HS, HS, 1)
        v_head = lax.dynamic_slice_in_dim(all_values, head_index * HS, HS, 1)
        scores = (
            jnp.einsum("qd,kd->qk", q_head, k_head, preferred_element_type=jnp.float32)
            * score_scale
        )
        scores = jnp.where(full_mask, scores, -jnp.inf)
        row_max = jnp.max(scores, axis=1, keepdims=True)
        weights = jnp.exp(scores - row_max)
        probabilities = (weights / jnp.sum(weights, axis=1, keepdims=True)).astype(jnp.bfloat16)
        return jnp.dot(probabilities, v_head, preferred_element_type=jnp.float32).astype(
            jnp.bfloat16
        )

    heads_out = lax.map(one_head, jnp.arange(local_heads, dtype=jnp.int32))
    attended = jnp.transpose(heads_out, (1, 0, 2)).reshape(tok_rows, local_width)
    return (attended, updated_cache)


def solution(mesh):
    return jax.shard_map(
        body,
        mesh=mesh,
        in_specs=(
            P("blk", "head"),
            P(None, None, "head"),
            P(None, "head"),
            P(None, "blk", None, "head"),
            P(),
            P(),
            P(),
        ),
        out_specs=(P("blk", "head"), P(None, "blk", None, "head")),
        check_vma=False,
    )
```

profile of v0, /device:TPU:10, one launch (start us, length us, event | category | flops | bytes accessed | tf_op | source)
XLA Modules:
  0.0 443.8 jit_solution(3828971185642472583)
XLA Ops:
  16.5 7.9 %gather_fusion.3 = bf16[64,2,64,512]{3,2,1,0:T(8,128)(2,1)} fusion(bf16[2,40,64,512]{3,2,1,0:T(8,128)(2,1)} %copy.76, s32[1024]{0:T(1024)S(1)} %pad_clamp_fusion.1), kind=kCustom, calls=%fused_computation.3 | custom fusion | bytes 16777472 | tf_op jit(solution)/shard_map/jit(_take)/gather | solution.py:129
  24.4 8.8 %copy.44 = bf16[2,64,64,512]{3,2,1,0:T(8,128)(2,1)} copy(bf16[2,64,64,512]{3,2,0,1:T(8,128)(2,1)} %bitcast.75) | data formatting | bytes 16777216 | tf_op jit(solution)/shard_map/jit(_take)/gather | solution.py:129
  33.3 8.2 %select_select_fusion = bf16[2,16,4,64,512]{4,3,2,1,0:T(8,128)(2,1)} fusion(bf16[2,16,4,64,512]{4,3,2,1,0:T(8,128)(2,1)} %bitcast.74, pred[16,4]{1,0:T(8,128)(4,1)S(1)} %compare_and_fusion.1, pred[16,4]{1,0:T(8,128)(4,1)S(1)} %add_compare_fusion.1), kind=kLoop, calls=%fused_computation.28 | loop fusion | flops 8388608 | bytes 16777344 | tf_op jit(solution)/shard_map/jit(_where)/select_n | solution.py:132
  41.5 7.9 %copy.45 = bf16[2,16,4,64,512]{4,3,2,0,1:T(8,128)(2,1)} copy(bf16[2,16,4,64,512]{4,3,2,1,0:T(8,128)(2,1)} %select_select_fusion) | data formatting | bytes 16777216 | tf_op jit(solution)/shard_map/jit(_where)/select_n | solution.py:132
  49.4 8.7 %all-to-all-start = ((bf16[2,16,4,64,512]{4,3,2,0,1:T(8,128)(2,1)}), bf16[2,16,4,64,512]{4,3,2,0,1:T(8,128)(2,1)}, u32[]{:S(2)}, u32[]{:S(2)}) async-start(bf16[2,16,4,64,512]{4,3,2,0,1:T(8,128)(2,1)} %copy.45), calls=%async_computation | async-start | bytes 16777216 | tf_op jit(solution)/shard_map/all_to_all | solution.py:133
  74.2 17.8 %fusion.20 = f32[1024,3,512]{0,2,1:T(8,128)S(1)} fusion(bf16[3,4096,512]{2,1,0:T(8,128)(2,1)} %param.10, bf16[1024,4096]{1,0:T(8,128)(2,1)} %all-gather.2.cloned.1.call-done), kind=kOutput, calls=%fused_computation.26 | convolution fusion | flops 12884901888 | bytes 27262976 | tf_op jit(solution)/shard_map/tc,jcw->tjw/dot_general | solution.py:53
  97.1 12.4 %all-reduce = (f32[1024]{0:T(1024)S(1)}, f32[1024]{0:T(1024)S(1)}) all-reduce(f32[1024]{0:T(1024)S(1)} %get-tuple-element.41, f32[1024]{0:T(1024)S(1)} %get-tuple-element.40), channel_id=1, replica_groups=mesh['head'=8,'blk'=16] {'head'}, use_global_device_ids=true, to_apply=%region_1.2 | all-reduce | flops 2048 | bytes 16384 | tf_op jit(solution)/shard_map/psum | solution.py:62
  122.3 40.8 %all-to-all-done = bf16[2,16,4,64,512]{4,3,2,0,1:T(8,128)(2,1)} async-done(((bf16[2,16,4,64,512]{4,3,2,0,1:T(8,128)(2,1)}), bf16[2,16,4,64,512]{4,3,2,0,1:T(8,128)(2,1)}, u32[]{:S(2)}, u32[]{:S(2)}) %all-to-all-start) | async-done | bytes 8388640 | tf_op jit(solution)/shard_map/all_to_all | solution.py:133
  184.6 52.7 %all-to-all-start.1 = ((bf16[2,16,2,64,512]{4,3,0,2,1:T(8,128)(2,1)}), bf16[2,16,2,64,512]{4,3,0,2,1:T(8,128)(2,1)}, u32[]{:S(2)}, u32[]{:S(2)}) async-start(bf16[2,16,2,64,512]{4,3,0,2,1:T(8,128)(2,1)} %select_select_fusion.1), calls=%async_computation.1 | async-start | bytes 8388608 | tf_op jit(solution)/shard_map/all_to_all | solution.py:103
  258.1 6.1 %pad_maximum_fusion.1 = bf16[6144,512]{1,0:T(8,128)(2,1)} fusion(bf16[2048,512]{1,0:T(8,128)(2,1)} %copy.49, bf16[4096,512]{1,0:T(8,128)(2,1)} %bitcast.77), kind=kLoop, calls=%fused_computation.30 | loop fusion | flops 12582912 | bytes 12582912 | tf_op jit(solution)/shard_map/concatenate | solution.py:163
  267.3 157.7 %while.10 = (s32[]{:T(128)}, bf16[4,1024,128]{2,1,0:T(8,128)(2,1)S(1)}, s32[4]{0:T(128)S(1)}, bf16[1024,512]{1,0:T(8,128)(2,1)}, bf16[6144,512]{1,0:T(8,128)(2,1...) while((s32[]{:T(128)}, ...), condition=%wide.region_8.9_spmd, body=%wide.region_5.8_spmd.sunk | while | flops 3296851968 | bytes 116937960 | solution.py:183
  268.8 13.2 %fusion.57 = (f32[1024]{0:T(1024)S(1)}, f32[1024,6144]{1,0:T(8,128)}) fusion(pred[1024,6144]{1,0:T(32,128)(4,1)} %get-tuple-element.162, bf16[6144,512]{1,0:T(8,128)(2,1)} %get-tuple-element.161, s32[]{:T(128)S(6)} %select_n.436, bf16[1024,512]{1,0:T(8,128)(2,1)} %get-tuple-element.160), kind=kOutput, calls=%fused_computation.12.clone.1 | convolution fusion | flops 1629486080 | bytes 33297408 | tf_op jit(solution)/shard_map/while/body/eval_jaxpr/qd,kd->qk/dot_general | solution.py:172
  282.0 12.3 %fusion.58 = f32[1024]{0:T(1024)S(1)} fusion(pred[1024,6144]{1,0:T(32,128)(4,1)S(1)} %bitcast.73, f32[1024,6144]{1,0:T(8,128)} %get-tuple-element.133, f32[1024]{0:T(1024)S(1)} %get-tuple-element.134), kind=kLoop, calls=%fused_computation.11.clone.1 | loop fusion | flops 25164800 | bytes 31465472 | tf_op jit(solution)/shard_map/while/body/eval_jaxpr/reduce_sum | solution.py:178
  294.3 12.5 %fusion.59 = bf16[4,1024,128]{2,1,0:T(8,128)(2,1)S(1)} fusion(bf16[4,1024,128]{2,1,0:T(8,128)(2,1)S(1)} %get-tuple-element.147, s32[]{:T(128)S(6)} %copy.64, bf16[6144,512]{1,0:T(8,128)(2,1)} %get-tuple-element.163, s32[]{:T(128)S(6)} %select_n.436, pred[1024,6144]{1,0:T(32,128)(4,1)S(1)} %bitcast.73, f32[1024,6144]{1,0:T(8,128)} %get-tuple-element.133, ...), kind=kOutput, calls=%fused_computation.19.clone.1 | convolution fusion | flops 1642201088 | bytes 33300488 | tf_op jit(solution)/shard_map/while/body/eval_jaxpr/dot_general | solution.py:179
  308.1 13.2 %fusion.57 = (f32[1024]{0:T(1024)S(1)}, f32[1024,6144]{1,0:T(8,128)}) fusion(pred[1024,6144]{1,0:T(32,128)(4,1)} %get-tuple-element.162, bf16[6144,512]{1,0:T(8,128)(2,1)} %get-tuple-element.161, s32[]{:T(128)S(6)} %select_n.436, bf16[1024,512]{1,0:T(8,128)(2,1)} %get-tuple-element.160), kind=kOutput, calls=%fused_computation.12.clone.1 | convolution fusion | flops 1629486080 | bytes 33297408 | tf_op jit(solution)/shard_map/while/body/eval_jaxpr/qd,kd->qk/dot_general | solution.py:172
  321.3 12.3 %fusion.58 = f32[1024]{0:T(1024)S(1)} fusion(pred[1024,6144]{1,0:T(32,128)(4,1)S(1)} %bitcast.73, f32[1024,6144]{1,0:T(8,128)} %get-tuple-element.133, f32[1024]{0:T(1024)S(1)} %get-tuple-element.134), kind=kLoop, calls=%fused_computation.11.clone.1 | loop fusion | flops 25164800 | bytes 31465472 | tf_op jit(solution)/shard_map/while/body/eval_jaxpr/reduce_sum | solution.py:178
  333.7 12.5 %fusion.59 = bf16[4,1024,128]{2,1,0:T(8,128)(2,1)S(1)} fusion(bf16[4,1024,128]{2,1,0:T(8,128)(2,1)S(1)} %get-tuple-element.147, s32[]{:T(128)S(6)} %copy.64, bf16[6144,512]{1,0:T(8,128)(2,1)} %get-tuple-element.163, s32[]{:T(128)S(6)} %select_n.436, pred[1024,6144]{1,0:T(32,128)(4,1)S(1)} %bitcast.73, f32[1024,6144]{1,0:T(8,128)} %get-tuple-element.133, ...), kind=kOutput, calls=%fused_computation.19.clone.1 | convolution fusion | flops 1642201088 | bytes 33300488 | tf_op jit(solution)/shard_map/while/body/eval_jaxpr/dot_general | solution.py:179
  347.5 13.2 %fusion.57 = (f32[1024]{0:T(1024)S(1)}, f32[1024,6144]{1,0:T(8,128)}) fusion(pred[1024,6144]{1,0:T(32,128)(4,1)} %get-tuple-element.162, bf16[6144,512]{1,0:T(8,128)(2,1)} %get-tuple-element.161, s32[]{:T(128)S(6)} %select_n.436, bf16[1024,512]{1,0:T(8,128)(2,1)} %get-tuple-element.160), kind=kOutput, calls=%fused_computation.12.clone.1 | convolution fusion | flops 1629486080 | bytes 33297408 | tf_op jit(solution)/shard_map/while/body/eval_jaxpr/qd,kd->qk/dot_general | solution.py:172
  360.7 12.3 %fusion.58 = f32[1024]{0:T(1024)S(1)} fusion(pred[1024,6144]{1,0:T(32,128)(4,1)S(1)} %bitcast.73, f32[1024,6144]{1,0:T(8,128)} %get-tuple-element.133, f32[1024]{0:T(1024)S(1)} %get-tuple-element.134), kind=kLoop, calls=%fused_computation.11.clone.1 | loop fusion | flops 25164800 | bytes 31465472 | tf_op jit(solution)/shard_map/while/body/eval_jaxpr/reduce_sum | solution.py:178
  373.1 12.5 %fusion.59 = bf16[4,1024,128]{2,1,0:T(8,128)(2,1)S(1)} fusion(bf16[4,1024,128]{2,1,0:T(8,128)(2,1)S(1)} %get-tuple-element.147, s32[]{:T(128)S(6)} %copy.64, bf16[6144,512]{1,0:T(8,128)(2,1)} %get-tuple-element.163, s32[]{:T(128)S(6)} %select_n.436, pred[1024,6144]{1,0:T(32,128)(4,1)S(1)} %bitcast.73, f32[1024,6144]{1,0:T(8,128)} %get-tuple-element.133, ...), kind=kOutput, calls=%fused_computation.19.clone.1 | convolution fusion | flops 1642201088 | bytes 33300488 | tf_op jit(solution)/shard_map/while/body/eval_jaxpr/dot_general | solution.py:179
  386.9 13.2 %fusion.57 = (f32[1024]{0:T(1024)S(1)}, f32[1024,6144]{1,0:T(8,128)}) fusion(pred[1024,6144]{1,0:T(32,128)(4,1)} %get-tuple-element.162, bf16[6144,512]{1,0:T(8,128)(2,1)} %get-tuple-element.161, s32[]{:T(128)S(6)} %select_n.436, bf16[1024,512]{1,0:T(8,128)(2,1)} %get-tuple-element.160), kind=kOutput, calls=%fused_computation.12.clone.1 | convolution fusion | flops 1629486080 | bytes 33297408 | tf_op jit(solution)/shard_map/while/body/eval_jaxpr/qd,kd->qk/dot_general | solution.py:172
  400.1 12.3 %fusion.58 = f32[1024]{0:T(1024)S(1)} fusion(pred[1024,6144]{1,0:T(32,128)(4,1)S(1)} %bitcast.73, f32[1024,6144]{1,0:T(8,128)} %get-tuple-element.133, f32[1024]{0:T(1024)S(1)} %get-tuple-element.134), kind=kLoop, calls=%fused_computation.11.clone.1 | loop fusion | flops 25164800 | bytes 31465472 | tf_op jit(solution)/shard_map/while/body/eval_jaxpr/reduce_sum | solution.py:178
  412.5 12.5 %fusion.59 = bf16[4,1024,128]{2,1,0:T(8,128)(2,1)S(1)} fusion(bf16[4,1024,128]{2,1,0:T(8,128)(2,1)S(1)} %get-tuple-element.147, s32[]{:T(128)S(6)} %copy.64, bf16[6144,512]{1,0:T(8,128)(2,1)} %get-tuple-element.163, s32[]{:T(128)S(6)} %select_n.436, pred[1024,6144]{1,0:T(32,128)(4,1)S(1)} %bitcast.73, f32[1024,6144]{1,0:T(8,128)} %get-tuple-element.133, ...), kind=kOutput, calls=%fused_computation.19.clone.1 | convolution fusion | flops 1642201088 | bytes 33300488 | tf_op jit(solution)/shard_map/while/body/eval_jaxpr/dot_general | solution.py:179
  426.1 10.6 %scatter_fusion = bf16[2,40,64,512]{3,2,1,0:T(8,128)(2,1)} fusion(bf16[2,40,64,512]{3,2,1,0:T(8,128)(2,1)} %copy.76, s32[32]{0:T(128)S(1)} %copy-done.13, bf16[32,2,64,512]{3,2,1,0:T(8,128)(2,1)} %bitcast.29), kind=kCustom, calls=%fused_computation.7 | custom fusion | bytes 12583040 | tf_op jit(solution)/shard_map/scatter | solution.py:115
  (151 shorter events, 91.8 us)
Async XLA Ops:
  7.2 6.6 %copy-start = (s32[8,64]{1,0:T(8,128)S(1)}, s32[8,64]{1,0:T(8,128)}, u32[]{:S(2)}) copy-start(s32[8,64]{1,0:T(8,128)} %param.14) | copy-start | bytes 6148
  7.2 5.6 %copy-start.1 = (s32[8,32]{1,0:T(8,128)S(1)}, s32[8,32]{1,0:T(8,128)}, u32[]{:S(2)}) copy-start(s32[8,32]{1,0:T(8,128)} %param.15) | copy-start | bytes 3076
  7.2 67.1 %all-gather.2.cloned.1.call-start = ((), (), s32[]{:S(2)}) async-start(), calls=%async_computation.2 | async-start | bytes 9437184 | tf_op jit(solution)/shard_map/all_gather | solution.py:55
  49.4 9.8 %copy-start.14 = (s32[8]{0:T(128)S(1)}, s32[8]{0:T(128)}, u32[]{:S(2)}) copy-start(s32[8]{0:T(128)} %param.13) | copy-start | bytes 100
  49.4 113.7 %all-to-all-start = ((bf16[2,16,4,64,512]{4,3,2,0,1:T(8,128)(2,1)}), bf16[2,16,4,64,512]{4,3,2,0,1:T(8,128)(2,1)}, u32[]{:S(2)}, u32[]{:S(2)}) async-start(bf16[2,16,4,64,512]{4,3,2,0,1:T(8,128)(2,1)} %copy.45), calls=%async_computation | async-start | bytes 16777216 | tf_op jit(solution)/shard_map/all_to_all | solution.py:133
  66.8 46.7 %copy-start.7 = (f32[1024,64]{1,0:T(8,128)}, f32[1024,64]{1,0:T(8,128)S(1)}, u32[]{:S(2)}) copy-start(f32[1024,64]{1,0:T(8,128)S(1)} %get-tuple-element.72) | copy-start | bytes 786436
  66.9 46.7 %copy-start.9 = (f32[1024,64]{1,0:T(8,128)}, f32[1024,64]{1,0:T(8,128)S(1)}, u32[]{:S(2)}) copy-start(f32[1024,64]{1,0:T(8,128)S(1)} %get-tuple-element.73) | copy-start | bytes 786436
  92.0 3.2 copy-start.6
  119.2 49.9 %copy-start.3 = (bf16[1,1024,512]{1,2,0:T(8,128)(2,1)}, bf16[1,1024,512]{1,2,0:T(8,128)(2,1)S(1)}, u32[]{:S(2)}) copy-start(bf16[1,1024,512]{1,2,0:T(8,128)(2,1)S(1)} %slice_bitcast_fusion.2) | copy-start | bytes 3145732
  120.9 126.9 %collective-permute-start = (bf16[2,1024,512]{1,2,0:T(8,128)(2,1)}, bf16[2,1024,512]{1,2,0:T(8,128)(2,1)}, u32[]{:S(2)}, u32[]{:S(2)}) collective-permute-start(bf16[2,1024,512]{1,2,0:T(8,128)(2,1)} %pad_maximum_fusion.2), channel_id=1, source_target_pairs={{0,1},{1,0},{2,3},{3,2},{4,5},{5,4},{6,7},{7,6},{8,9},{9,8},{10,11... | collective-permute-start | bytes 6291464 | tf_op jit(solution)/shard_map/ppermute | solution.py:21
  184.6 52.7 %copy-start.5 = (f32[1024,1,512]{0,2,1:T(8,128)S(1)}, f32[1024,1,512]{0,2,1:T(8,128)}, u32[]{:S(2)}) copy-start(f32[1024,1,512]{0,2,1:T(8,128)} %get-tuple-element.65) | copy-start | bytes 6291460
  184.6 241.5 %all-to-all-start.1 = ((bf16[2,16,2,64,512]{4,3,0,2,1:T(8,128)(2,1)}), bf16[2,16,2,64,512]{4,3,0,2,1:T(8,128)(2,1)}, u32[]{:S(2)}, u32[]{:S(2)}) async-start(bf16[2,16,2,64,512]{4,3,0,2,1:T(8,128)(2,1)} %select_select_fusion.1), calls=%async_computation.1 | async-start | bytes 8388608 | tf_op jit(solution)/shard_map/all_to_all | solution.py:103
  239.2 4.2 copy-start.8
  239.2 4.2 copy-start.10
  258.1 6.1 %copy-start.2 = (bf16[1,16,4,64,512]{4,3,2,0,1:T(8,128)(2,1)S(1)}, bf16[1,16,4,64,512]{4,3,2,0,1:T(8,128)(2,1)}, u32[]{:S(2)}) copy-start(bf16[1,16,4,64,512]{4,3,2,0,1:T(8,128)(2,1)} %get-tuple-element.63) | copy-start | bytes 12582916
  267.3 158.8 %copy-start.13 = (s32[32]{0:T(128)S(1)}, s32[32]{0:T(128)}, u32[]{:S(2)}) copy-start(s32[32]{0:T(128)} %fusion.46) | copy-start | bytes 388
  268.7 13.2 %slice-start = ((s8[6291456]{0:T(1024)(128)(4,1)}), s8[4194304]{0:T(1024)(128)(4,1)S(1)}, s32[]{:S(2)}) async-start(s8[6291456]{0:T(1024)(128)(4,1)} %bitcast.72), calls=%async_computation.3 | async-start | bytes 8388608 | tf_op jit(solution)/shard_map/while
  268.7 13.2 %slice-start.1 = ((s8[6291456]{0:T(1024)(128)(4,1)}), s8[2097152]{0:T(1024)(128)(4,1)S(1)}, s32[]{:S(2)}) async-start(s8[6291456]{0:T(1024)(128)(4,1)} %bitcast.72), calls=%async_computation.4 | async-start | bytes 4194304 | tf_op jit(solution)/shard_map/while
  308.1 13.2 %slice-start = ((s8[6291456]{0:T(1024)(128)(4,1)}), s8[4194304]{0:T(1024)(128)(4,1)S(1)}, s32[]{:S(2)}) async-start(s8[6291456]{0:T(1024)(128)(4,1)} %bitcast.72), calls=%async_computation.3 | async-start | bytes 8388608 | tf_op jit(solution)/shard_map/while
  308.1 13.2 %slice-start.1 = ((s8[6291456]{0:T(1024)(128)(4,1)}), s8[2097152]{0:T(1024)(128)(4,1)S(1)}, s32[]{:S(2)}) async-start(s8[6291456]{0:T(1024)(128)(4,1)} %bitcast.72), calls=%async_computation.4 | async-start | bytes 4194304 | tf_op jit(solution)/shard_map/while
  347.5 13.2 %slice-start = ((s8[6291456]{0:T(1024)(128)(4,1)}), s8[4194304]{0:T(1024)(128)(4,1)S(1)}, s32[]{:S(2)}) async-start(s8[6291456]{0:T(1024)(128)(4,1)} %bitcast.72), calls=%async_computation.3 | async-start | bytes 8388608 | tf_op jit(solution)/shard_map/while
  347.5 13.2 %slice-start.1 = ((s8[6291456]{0:T(1024)(128)(4,1)}), s8[2097152]{0:T(1024)(128)(4,1)S(1)}, s32[]{:S(2)}) async-start(s8[6291456]{0:T(1024)(128)(4,1)} %bitcast.72), calls=%async_computation.4 | async-start | bytes 4194304 | tf_op jit(solution)/shard_map/while
  386.9 13.2 %slice-start = ((s8[6291456]{0:T(1024)(128)(4,1)}), s8[4194304]{0:T(1024)(128)(4,1)S(1)}, s32[]{:S(2)}) async-start(s8[6291456]{0:T(1024)(128)(4,1)} %bitcast.72), calls=%async_computation.3 | async-start | bytes 8388608 | tf_op jit(solution)/shard_map/while
  386.9 13.2 %slice-start.1 = ((s8[6291456]{0:T(1024)(128)(4,1)}), s8[2097152]{0:T(1024)(128)(4,1)S(1)}, s32[]{:S(2)}) async-start(s8[6291456]{0:T(1024)(128)(4,1)} %bitcast.72), calls=%async_computation.4 | async-start | bytes 4194304 | tf_op jit(solution)/shard_map/while
  (3 other events, 8.3 us)
Sparse Core Ops, SparseCore 0:
  12.9 51.1 all-gather.1
where the time goes:
time: 449 us; the launch traced here: 444 us
  matrix products  121 us (27%)
  other arithmetic  109 us (24%)
  local copies, waits for them, and re-layouts  80.6 us (18%)
  starting transfers between devices  62.7 us (14%)
  waiting for transfers between devices  40.8 us (9%)
  between operations  14.7 us (3%)
  blocking collectives  12.4 us (3%)
    dot_general x4, matrix products, one_head(): jnp.einsum('qd,kd->qk', q_head, k_head, preferred_element_type=jnp.float32)  52.7 us
    all_to_all x1, starting transfers between devices, body(): lax.all_to_all(picked, 'blk', split_axis=1, concat_axis=1, tiled=True)  52.7 us
    dot_general x4, matrix products, one_head(): jnp.dot(probabilities, v_head, preferred_element_type=jnp.float32)  50.2 us
    reduce_sum x4, other arithmetic, one_head(): jnp.sum(weights, axis=1, keepdims=True)  49.4 us
    all_to_all x1, waiting for transfers between devices, body(): lax.all_to_all(outgoing, 'blk', split_axis=1, concat_axis=1, tiled=True)  40.8 us
    dot_general x1, matrix products, body(): jnp.einsum('tc,jcw->tjw', lax.all_gather(states, 'head', axis=1, tiled=Tr...  17.8 us
    gather x2, local copies, waits for them, and re-layouts, body(): jnp.take(kv_cache, slot_index.reshape(-1), axis=1)  16.7 us
    psum x1, blocking collectives, body(): lax.psum((jnp.sum(queries * queries, axis=1), jnp.sum(key_new * key_new,...  12.4 us
  transfers between devices with their start and end apart: 4, of which 1 were waited for; matrix products, arithmetic and copies ran while one was open for 66% of the time, Pallas kernels for 0%

commit v1 on v0

v1 whole, which is shorter than its diff:
```python
import functools

import jax
import jax.numpy as jnp
from jax import lax
from jax.experimental import pallas as pl
from jax.experimental.pallas import tpu as pltpu
from jax.sharding import PartitionSpec as P

D = 4096
HS = 128


rope_base = 500000.0
norm_eps = 1e-06
score_scale = HS ** (-0.5)


def swapped(block, axis, apart):
    count = lax.axis_size(axis)
    route = []
    for low in range(count):
        high = low | 1 << apart
        if high != low and high < count:
            route += [(low, high), (high, low)]
    return lax.ppermute(block, axis, route)


def rotate(values, positions, head_size):
    half_size = head_size // 2
    frequency = rope_base ** (-jnp.arange(half_size, dtype=jnp.float32) * 2.0 / head_size)
    angles = positions.astype(jnp.float32)[:, None] * frequency[None, :]
    cosine = jnp.cos(angles)[:, None, :]
    sine_part = jnp.sin(angles)[:, None, :]
    first_half = values[..., :half_size]
    second = values[..., half_size:]
    return jnp.concatenate(
        [first_half * cosine - second * sine_part, second * cosine + first_half * sine_part],
        axis=-1,
    )


def online_update(s, v, m_sc, l_sc, acc_sc):
    m_prev = m_sc[...]
    m_cur = jnp.max(s, axis=1, keepdims=True)
    m_next = jnp.maximum(m_prev, m_cur)
    alpha = jnp.exp(m_prev - m_next)
    p = jnp.exp(s - m_next[:, :1])
    l_sc[...] = alpha * l_sc[...] + jnp.sum(p, axis=1, keepdims=True)
    pv = jnp.dot(p.astype(jnp.bfloat16), v, preferred_element_type=jnp.float32)
    acc_sc[...] = acc_sc[...] * alpha + pv
    m_sc[...] = m_next


def scores_of(q, k):
    return (
        lax.dot_general(q, k, (((1,), (1,)), ((), ())), preferred_element_type=jnp.float32)
        * score_scale
    )


def new_kernel(meta_ref, q_ref, k_ref, v_ref, acc_out, m_out, l_out, m_sc, l_sc, acc_sc):
    qi = pl.program_id(1)
    kj = pl.program_id(2)
    member = meta_ref[0]
    q_chunk = jnp.where(qi == 0, member, 3 - member)
    k_chunk = jnp.where(kj == 0, 0, jnp.where(kj == 1, 3, kj - 1))

    @pl.when(kj == 0)
    def _():
        m_sc[...] = jnp.full(m_sc.shape, -jnp.inf, jnp.float32)
        l_sc[...] = jnp.zeros(l_sc.shape, jnp.float32)
        acc_sc[...] = jnp.zeros(acc_sc.shape, jnp.float32)

    @pl.when(k_chunk <= q_chunk)
    def _():
        s = scores_of(q_ref[...], k_ref[...])
        rows = lax.broadcasted_iota(jnp.int32, s.shape, 0)
        cols = lax.broadcasted_iota(jnp.int32, s.shape, 1)
        visible = (k_chunk < q_chunk) | (cols <= rows)
        s = jnp.where(visible, s, -jnp.inf)
        online_update(s, v_ref[...], m_sc, l_sc, acc_sc)

    @pl.when(kj == pl.num_programs(2) - 1)
    def _():
        acc_out[...] = acc_sc[...]
        m_out[...] = m_sc[...]
        l_out[...] = l_sc[...]


def cached_kernel(meta_ref, q_ref, k_ref, v_ref, acc_in, m_in, l_in, o_ref, m_sc, l_sc, acc_sc,
                  *, groups, per_half, block_len):
    c = pl.program_id(1)
    half = pl.program_id(2)
    length = meta_ref[1]
    first = meta_ref[2]
    tile = per_half * block_len

    @pl.when((c == 0) & (half == 0))
    def _():
        m_sc[...] = m_in[...]
        l_sc[...] = l_in[...]
        acc_sc[...] = acc_in[...]

    @pl.when(c * groups * block_len < length)
    def _():
        k = k_ref[...].reshape(tile, HS)
        v = v_ref[...].reshape(tile, HS)
        s = scores_of(q_ref[...], k)
        cols = lax.broadcasted_iota(jnp.int32, (1, tile), 1)
        src = half * per_half + cols // block_len
        block = (src - first + groups) % groups + groups * c
        visible = block * block_len + cols % block_len < length
        s = jnp.where(visible, s, -jnp.inf)
        online_update(s, v, m_sc, l_sc, acc_sc)

    @pl.when((c == pl.num_programs(1) - 1) & (half == pl.num_programs(2) - 1))
    def _():
        o_ref[...] = (acc_sc[...] / l_sc[...]).astype(o_ref.dtype)


def new_attention(meta, queries, keys, values):
    tok_rows, width = queries.shape
    heads = width // HS
    q_rows = tok_rows // 2
    key_rows = keys.shape[0]
    k_tiles = key_rows // q_rows
    state = jax.ShapeDtypeStruct((tok_rows, width), jnp.float32)
    state_spec = pl.BlockSpec((q_rows, HS), lambda h, i, j, meta: (i, h))
    flops = 2 * 2 * tok_rows * key_rows * width
    return pl.pallas_call(
        new_kernel,
        out_shape=(state, state, state),
        grid_spec=pltpu.PrefetchScalarGridSpec(
            num_scalar_prefetch=1,
            grid=(heads, 2, k_tiles),
            in_specs=[
                pl.BlockSpec((q_rows, HS), lambda h, i, j, meta: (i, h)),
                pl.BlockSpec((q_rows, HS), lambda h, i, j, meta: (j, h)),
                pl.BlockSpec((q_rows, HS), lambda h, i, j, meta: (j, h)),
            ],
            out_specs=[state_spec, state_spec, state_spec],
            scratch_shapes=[
                pltpu.VMEM((q_rows, HS), jnp.float32),
                pltpu.VMEM((q_rows, HS), jnp.float32),
                pltpu.VMEM((q_rows, HS), jnp.float32),
            ],
        ),
        compiler_params=pltpu.CompilerParams(
            dimension_semantics=("arbitrary", "arbitrary", "arbitrary")
        ),
        cost_estimate=pl.CostEstimate(
            flops=flops // 2,
            transcendentals=tok_rows * key_rows * heads // 2,
            bytes_accessed=2 * tok_rows * width * 2 + 2 * 2 * key_rows * width + 3 * 4 * tok_rows * width,
        ),
    )(meta, queries, keys, values)


def cached_attention(meta, queries, received, acc, m, l):
    tok_rows, width = queries.shape
    heads = width // HS
    groups, _, per_dev, block_len, _ = received.shape
    per_half = groups // 2

    def kv_map(index):
        def index_map(h, c, half, meta):
            last = (meta[1] + groups * block_len - 1) // (groups * block_len) - 1
            skip = c > last
            return (
                jnp.where(skip, 1, half),
                index,
                jnp.where(skip, last, c),
                0,
                h,
            )

        return index_map

    kv_block = (per_half, None, None, block_len, HS)
    state_spec = pl.BlockSpec((tok_rows, HS), lambda h, c, half, meta: (0, h))
    keys_total = groups * per_dev * block_len
    return pl.pallas_call(
        functools.partial(
            cached_kernel, groups=groups, per_half=per_half, block_len=block_len
        ),
        out_shape=jax.ShapeDtypeStruct((tok_rows, width), jnp.bfloat16),
        grid_spec=pltpu.PrefetchScalarGridSpec(
            num_scalar_prefetch=1,
            grid=(heads, per_dev, 2),
            in_specs=[
                pl.BlockSpec((tok_rows, HS), lambda h, c, half, meta: (0, h)),
                pl.BlockSpec(kv_block, kv_map(0)),
                pl.BlockSpec(kv_block, kv_map(1)),
                state_spec,
                state_spec,
                state_spec,
            ],
            out_specs=pl.BlockSpec((tok_rows, HS), lambda h, c, half, meta: (0, h)),
            scratch_shapes=[
                pltpu.VMEM((tok_rows, HS), jnp.float32),
                pltpu.VMEM((tok_rows, HS), jnp.float32),
                pltpu.VMEM((tok_rows, HS), jnp.float32),
            ],
        ),
        compiler_params=pltpu.CompilerParams(
            dimension_semantics=("arbitrary", "arbitrary", "arbitrary")
        ),
        cost_estimate=pl.CostEstimate(
            flops=2 * 2 * tok_rows * keys_total * width // 2,
            transcendentals=tok_rows * keys_total * heads // 2,
            bytes_accessed=2 * keys_total * width + 2 * tok_rows * width * 2 + 3 * 4 * tok_rows * width,
        ),
    )(meta, queries, received, received, acc, m, l)


def body(states, qkv_weight, norm_gains, kv_cache, cached_len, old_table, new_table):
    tok_rows = states.shape[0]
    half_rows = tok_rows // 2
    local_width = qkv_weight.shape[2]
    local_heads = local_width // HS
    groups = lax.axis_size("blk")
    slot_count = kv_cache.shape[1]
    block_len = kv_cache.shape[2]
    requests = cached_len.shape[0]
    group_size = groups // requests
    per_dev = old_table.shape[1] // groups
    my_index = lax.axis_index("blk")
    request = my_index // group_size
    member = my_index % group_size
    late_block = 2 * group_size - 1 - member
    targets = jnp.arange(groups, dtype=jnp.int32)
    kv_flat = kv_cache.reshape(2 * slot_count, block_len, local_width)

    lengths_blocks = jnp.sum((old_table >= 0).astype(jnp.int32), axis=1)
    first_dev = old_table[:, 0] // slot_count
    target_req = targets // group_size
    c_index = jnp.arange(per_dev, dtype=jnp.int32)
    block_index = ((my_index - first_dev[target_req]) % groups)[:, None] + groups * c_index[None, :]
    slot_index = (
        old_table[target_req[:, None], jnp.clip(block_index, 0, old_table.shape[1] - 1)]
        - my_index * slot_count
    )
    slot_index = jnp.clip(slot_index, 0, slot_count - 1)
    kv_ids = jnp.arange(2, dtype=jnp.int32)
    out_ids = kv_ids[None, :, None] * slot_count + slot_index[:, None, :]
    outgoing = jnp.take(kv_flat, out_ids.reshape(-1), axis=0).reshape(
        groups, 2, per_dev, block_len, local_width
    )
    received = lax.all_to_all(outgoing, "blk", split_axis=0, concat_axis=0, tiled=True)

    projected = jnp.einsum(
        "tc,jcw->tjw",
        lax.all_gather(states, "head", axis=1, tiled=True),
        qkv_weight,
        preferred_element_type=jnp.float32,
    )
    queries = projected[:, 0]
    key_new = projected[:, 1]
    value_new = projected[:, 2]
    query_sq, key_sq = lax.psum(
        (jnp.sum(queries * queries, axis=1), jnp.sum(key_new * key_new, axis=1)), "head"
    )
    gains = norm_gains.astype(jnp.float32)
    queries = queries * lax.rsqrt(query_sq / D + norm_eps)[:, None] * gains[0]
    key_new = key_new * lax.rsqrt(key_sq / D + norm_eps)[:, None] * gains[1]
    half_ids = jnp.arange(half_rows, dtype=jnp.int32)
    token_offset = jnp.concatenate(
        [member * half_rows + half_ids, late_block * half_rows + half_ids]
    )
    positions = cached_len[request] + token_offset
    queries = (
        rotate(queries.reshape(tok_rows, local_heads, HS), positions, HS)
        .reshape(tok_rows, local_width)
        .astype(jnp.bfloat16)
    )
    key_new = (
        rotate(key_new.reshape(tok_rows, local_heads, HS), positions, HS)
        .reshape(tok_rows, local_width)
        .astype(jnp.bfloat16)
    )
    value_new = value_new.astype(jnp.bfloat16)
    fresh_kv = jnp.stack([key_new, value_new])

    blocks_dev = tok_rows // block_len
    half_blocks = blocks_dev // 2
    new_count = new_table.shape[1]
    fresh_flat = fresh_kv.reshape(2 * blocks_dev, block_len, local_width)
    pair_index = jnp.arange(2, dtype=jnp.int32)
    new_home = new_table[:, 0] // slot_count
    wanted_out = 2 * ((targets - new_home[request]) % groups)[:, None] + pair_index[None, :]
    out_half = wanted_out // half_blocks
    local_index = jnp.where(
        out_half == member,
        wanted_out - member * half_blocks,
        wanted_out - late_block * half_blocks + half_blocks,
    )
    local_index = jnp.clip(local_index, 0, blocks_dev - 1)
    pick_ids = kv_ids[None, :, None] * blocks_dev + local_index[:, None, :]
    picked = jnp.take(fresh_flat, pick_ids.reshape(-1), axis=0).reshape(
        groups, 2, 2, block_len, local_width
    )
    arrived = lax.all_to_all(picked, "blk", split_axis=0, concat_axis=0, tiled=True)
    source_req = targets // group_size
    source_member = targets % group_size
    source_late = 2 * group_size - 1 - source_member
    wanted_in = 2 * ((my_index - new_home[source_req]) % groups)[:, None] + pair_index[None, :]
    in_half = wanted_in // half_blocks
    valid_in = (in_half == source_member[:, None]) | (in_half == source_late[:, None])
    target_slot = (
        new_table[source_req[:, None], jnp.clip(wanted_in, 0, new_count - 1)]
        - my_index * slot_count
    )
    target_ids = kv_ids[None, :, None] * slot_count + target_slot[:, None, :]
    target_ids = jnp.where(valid_in[:, None, :], target_ids, 2 * slot_count)
    updated_cache = (
        kv_flat.at[target_ids.reshape(-1)]
        .set(arrived.reshape(groups * 4, block_len, local_width), mode="drop")
        .reshape(kv_cache.shape)
    )

    collected = fresh_kv
    partner_new = swapped(collected, "blk", 0)
    lower_new = member // 2**0 % 2 == 0
    collected = jnp.where(
        lower_new,
        jnp.concatenate([collected, partner_new], axis=1),
        jnp.concatenate([partner_new, collected], axis=1),
    )
    meta = jnp.stack([member, cached_len[request], first_dev[request], 0]).astype(jnp.int32)
    acc, m, l = new_attention(meta, queries, collected[0], collected[1])
    attended = cached_attention(meta, queries, received, acc, m, l)
    return (attended, updated_cache)


def solution(mesh):
    return jax.shard_map(
        body,
        mesh=mesh,
        in_specs=(
            P("blk", "head"),
            P(None, None, "head"),
            P(None, "head"),
            P(None, "blk", None, "head"),
            P(),
            P(),
            P(),
        ),
        out_specs=(P("blk", "head"), P(None, "blk", None, "head")),
        check_vma=False,
    )
```

time: 449 us -> 336 us (0.75)
  matrix products: 121 us -> 17.8 us
  Pallas kernels: 0 us -> 101 us
  other arithmetic: 109 us -> 41.3 us
  local copies, waits for them, and re-layouts: 80.6 us -> 45.3 us
    dot_general x8 -> x0, matrix products: 103 us -> none  [the longest x4 52.7 us: one_head(): jnp.einsum('qd,kd->qk', q_head, k_head, preferred_element_type=jnp.float32)]
    pallas_call x0 -> x2, Pallas kernels: none -> 101 us  [the longest x1 69.8 us: cached_attention(): pl.pallas_call(functools.partial(cached_kernel, groups=groups, per_half=p...]
    reduce_sum x5 -> x0, other arithmetic: 49.5 us -> none  [the longest x4 49.4 us: one_head(): jnp.sum(weights, axis=1, keepdims=True)]
    all_to_all x2, waiting for transfers between devices: 40.8 us -> 19.3 us  [the longest x1 19.3 us: body(): lax.all_to_all(outgoing, 'blk', split_axis=0, concat_axis=0, tiled=True)]
    all_gather x1, waiting for transfers between devices: 0.01 us -> 17.5 us  [body(): lax.all_gather(states, 'head', axis=1, tiled=True)]
    concatenate x4 -> x0, other arithmetic: 15.7 us -> none  [the longest x1 6.13 us: body(): all_values = jnp.concatenate([cached_values, collected[1]], axis=0)]
    gather x4 -> x2, local copies, waits for them, and re-layouts: 20.1 us -> 11.8 us  [the longest x1 9.02 us: body(): jnp.take(kv_flat, out_ids.reshape(-1), axis=0)]
    select_n x1, local copies, waits for them, and re-layouts: 7.9 us -> 0.12 us  [body(): target_ids = jnp.where(valid_in[:, None, :], target_ids, 2 * slot_count)]
  transfers between devices with their start and end apart: 4 -> 4, of which waited for: 1 -> 2; matrix products, arithmetic and copies ran while one was open for 66% -> 26% of each run, Pallas kernels for 0% -> 30%
where the time goes in v1:
time: 336 us; the launch traced here: 331 us
  Pallas kernels  101 us (30%)
  starting transfers between devices  62 us (18%)
  local copies, waits for them, and re-layouts  45.3 us (13%)
  other arithmetic  41.3 us (12%)
  waiting for transfers between devices  36.8 us (11%)
  matrix products  17.8 us (5%)
  between operations  14.4 us (4%)
  blocking collectives  12.4 us (4%)
    pallas_call x1, Pallas kernels, cached_attention(): pl.pallas_call(functools.partial(cached_kernel, groups=groups, per_half=p...  69.8 us
    all_to_all x1, starting transfers between devices, body(): lax.all_to_all(picked, 'blk', split_axis=0, concat_axis=0, tiled=True)  52 us
    pallas_call x1, Pallas kernels, new_attention(): pl.pallas_call(new_kernel, out_shape=(state, state, state), grid_spec=plt...  30.9 us
    all_to_all x1, waiting for transfers between devices, body(): lax.all_to_all(outgoing, 'blk', split_axis=0, concat_axis=0, tiled=True)  19.3 us
    dot_general x1, matrix products, body(): jnp.einsum('tc,jcw->tjw', lax.all_gather(states, 'head', axis=1, tiled=Tr...  17.8 us
    all_gather x1, waiting for transfers between devices, body(): lax.all_gather(states, 'head', axis=1, tiled=True)  17.5 us
    psum x1, blocking collectives, body(): lax.psum((jnp.sum(queries * queries, axis=1), jnp.sum(key_new * key_new,...  12.4 us
    scatter x1, local copies, waits for them, and re-layouts, body(): updated_cache = kv_flat.at[target_ids.reshape(-1)].set(arrived.reshape(gr...  11.4 us
  transfers between devices with their start and end apart: 4, of which 2 were waited for; matrix products, arithmetic and copies ran while one was open for 26% of the time, Pallas kernels for 30%

profile of v1, /device:TPU:10, one launch (start us, length us, event | category | flops | bytes accessed | tf_op | source)
XLA Modules:
  0.0 330.7 jit_solution(13789638238988687954)
XLA Ops:
  7.2 5.5 %copy.31 = bf16[2,40,64,512]{3,2,1,0:T(8,128)(2,1)} copy(bf16[2,40,64,512]{3,2,1,0:T(8,128)(2,1)} %param.10) | data formatting | bytes 10485760
  15.9 9.0 %gather_fusion.2 = bf16[128,64,512]{2,1,0:T(8,128)(2,1)} fusion(bf16[80,64,512]{2,1,0:T(8,128)(2,1)} %bitcast.40, s32[1024]{0:T(1024)S(1)} %pad_clamp_fusion.1), kind=kCustom, calls=%fused_computation.2 | custom fusion | bytes 16777728 | tf_op jit(solution)/shard_map/jit(_take)/gather | solution.py:247
  25.0 8.3 %broadcast_select_fusion = bf16[16,2,4,64,512]{4,3,2,1,0:T(8,128)(2,1)} fusion(bf16[16,2,4,64,512]{4,3,2,1,0:T(8,128)(2,1)} %bitcast.43, pred[16,2,4]{2,1,0:T(4,128)(4,1)S(1)} %compare_and_fusion), kind=kLoop, calls=%fused_computation.9 | loop fusion | flops 4194304 | bytes 16777344 | tf_op jit(solution)/shard_map/jit(_take)/select_n | solution.py:247
  33.3 8.3 %all-to-all-start = ((bf16[16,2,4,64,512]{4,3,2,1,0:T(8,128)(2,1)}), bf16[16,2,4,64,512]{4,3,2,1,0:T(8,128)(2,1)}, u32[]{:S(2)}, u32[]{:S(2)}) async-start(bf16[16,2,4,64,512]{4,3,2,1,0:T(8,128)(2,1)} %broadcast_select_fusion), calls=%async_computation | async-start | bytes 16777216 | tf_op jit(solution)/shard_map/all_to_all | solution.py:250
  44.7 1.9 multiply_cosine_fusion
  46.6 17.5 %all-gather.2.cloned.1.call-done = bf16[1024,4096]{1,0:T(8,128)(2,1)} async-done(((bf16[1024,512]{1,0:T(8,128)(2,1)}), bf16[1024,4096]{1,0:T(8,128)(2,1)}) %all-gather.2.cloned.1.call-update) | async-done | bytes 8388624 | tf_op jit(solution)/shard_map/all_gather | solution.py:254
  64.0 17.8 %fusion = f32[1024,3,512]{0,2,1:T(8,128)S(1)} fusion(bf16[3,4096,512]{2,1,0:T(8,128)(2,1)} %param.8, bf16[1024,4096]{1,0:T(8,128)(2,1)} %all-gather.2.cloned.1.call-done), kind=kOutput, calls=%fused_computation.7 | convolution fusion | flops 12884901888 | bytes 27262976 | tf_op jit(solution)/shard_map/tc,jcw->tjw/dot_general | solution.py:252
  82.9 2.0 multiply_reduce_fusion
  84.9 2.9 copy.18
  89.7 12.4 %all-reduce = (f32[1024]{0:T(1024)S(1)}, f32[1024]{0:T(1024)S(1)}) all-reduce(f32[1024]{0:T(1024)S(1)} %get-tuple-element.9, f32[1024]{0:T(1024)S(1)} %get-tuple-element.8), channel_id=1, replica_groups=mesh['head'=8,'blk'=16] {'head'}, use_global_device_ids=true, to_apply=%region_1.2 | all-reduce | flops 2048 | bytes 16384 | tf_op jit(solution)/shard_map/psum | solution.py:261
  102.1 4.2 %multiply_multiply_fusion.1 = f32[1024,4,128]{2,1,0:T(4,128)S(1)} fusion(f32[1024,4,128]{2,1,0:T(4,128)} %copy.18, f32[4,128]{1,0:T(4,128)S(1)} %bitcast.54, f32[1024]{0:T(1024)S(1)} %get-tuple-element.29), kind=kLoop, calls=%fused_computation.21 | loop fusion | flops 1048576 | bytes 4200448 | tf_op jit(solution)/shard_map/mul | solution.py:265
  106.4 3.0 multiply_multiply_fusion
  109.3 4.2 %subtract_convert_fusion = (bf16[1024,4,64]{2,1,0:T(4,128)(2,1)S(1)}, bf16[1024,4,64]{2,1,0:T(4,128)(2,1)S(1)}, bf16[1024,4,64]{2,1,0:T(4,128)(2,1)}, bf16[1024,4,64]{2,1,0:T(4,128)(2,1)}) fusion(f32[1024,4,128]{2,1,0:T(4,128)S(1)} %multiply_multiply_fusion, f32[1024,64]{1,0:T(8,128)S(1)} %get-tuple-element.23, f32[1024,64]{1,0:T(8,128)S(1)} %get-tuple-element.22, ...), kind=kLoop, calls=%fused_computation.16 | loop fusion | flops 4194304 | bytes 6815744 | tf_op jit(solution)/shard_map/convert.1
  119.8 2.8 gather_fusion.5
  122.6 4.6 %broadcast_select_fusion.1 = bf16[16,2,2,64,512]{4,3,2,1,0:T(8,128)(2,1)} fusion(bf16[16,2,2,64,512]{4,3,2,1,0:T(8,128)(2,1)} %bitcast.45, pred[16,2,2]{2,1,0:T(4,128)(4,1)S(1)} %copy.22), kind=kLoop, calls=%fused_computation.11 | loop fusion | flops 2097152 | bytes 8388672 | tf_op jit(solution)/shard_map/jit(_take)/select_n | solution.py:300
  127.1 19.3 %all-to-all-done.k_ref.v_ref = bf16[16,2,4,64,512]{4,3,2,1,0:T(8,128)(2,1)} async-done(((bf16[16,2,4,64,512]{4,3,2,1,0:T(8,128)(2,1)}), bf16[16,2,4,64,512]{4,3,2,1,0:T(8,128)(2,1)}, u32[]{:S(2)}, u32[]{:S(2)}) %all-to-all-start) | async-done | bytes 8388640 | tf_op jit(solution)/shard_map/all_to_all | solution.py:250
  146.5 52.0 %all-to-all-start.1 = ((bf16[16,2,2,64,512]{4,3,2,1,0:T(8,128)(2,1)}), bf16[16,2,2,64,512]{4,3,2,1,0:T(8,128)(2,1)}, u32[]{:S(2)}, u32[]{:S(2)}) async-start(bf16[16,2,2,64,512]{4,3,2,1,0:T(8,128)(2,1)} %broadcast_select_fusion.1), calls=%async_computation.1 | async-start | bytes 8388608 | tf_op jit(solution)/shard_map/all_to_all | solution.py:303
  200.4 1.9 pad_add_fusion.meta_ref
  202.3 3.0 pad_maximum_fusion.1
  206.6 2.9 maximum_select_fusion
  209.4 2.3 slice_bitcast_fusion
  211.7 30.9 %shard_map.86 = (f32[1024,512]{1,0:T(8,128)}, f32[1024,512]{1,0:T(8,128)}, f32[1024,512]{1,0:T(8,128)}) custom-call(s32[4]{0:T(128)} %pad_add_fusion.meta_ref, bf16[1024,512]{1,0:T(8,128)(2,1)} %bitcast.50, bf16[2048,512]{1,0:T(8,128)(2,1)} %get-tuple-element.15.k_ref, bf16[2048,512]{1,0:T(8,128)(2,1)} %get-tuple-element.14.v_ref), custom_call_target="tpu_custom_call" | custom-call | flops 2147483648 | bytes 12582912 | tf_op jit(solution)/shard_map/pallas_call | solution.py:131
  242.7 69.8 %shard_map.87 = bf16[1024,512]{1,0:T(8,128)(2,1)} custom-call(s32[4]{0:T(128)} %pad_add_fusion.meta_ref, bf16[1024,512]{1,0:T(8,128)(2,1)} %bitcast.51, bf16[16,2,4,64,512]{4,3,2,1,0:T(8,128)(2,1)} %all-to-all-done.k_ref.v_ref, bf16[16,2,4,64,512]{4,3,2,1,0:T(8,128)(2,1)} %all-to-all-done.k_ref.v_ref, f32[1024,512]{1,0:T(8,128)} %get-tuple-element.5.acc_in, ...), custom_call_target="tpu_custom_call" | custom-call | flops 4294967296 | bytes 12582912 | tf_op jit(solution)/shard_map/pallas_call | solution.py:183
  312.5 11.4 %scatter_fusion = bf16[80,64,512]{2,1,0:T(8,128)(2,1)} fusion(bf16[80,64,512]{2,1,0:T(8,128)(2,1)} %bitcast.41, s32[64]{0:T(128)S(1)} %fusion.23, bf16[64,64,512]{2,1,0:T(8,128)(2,1)} %bitcast.19), kind=kCustom, calls=%fused_computation.6 | custom fusion | bytes 12583168 | tf_op jit(solution)/shard_map/scatter | solution.py:318
  (79 shorter events, 18.5 us)
Async XLA Ops:
  7.2 5.6 %copy-start = (s32[8,64]{1,0:T(8,128)S(1)}, s32[8,64]{1,0:T(8,128)}, u32[]{:S(2)}) copy-start(s32[8,64]{1,0:T(8,128)} %param.12) | copy-start | bytes 6148
  7.2 6.5 %copy-start.1 = (s32[8,32]{1,0:T(8,128)S(1)}, s32[8,32]{1,0:T(8,128)}, u32[]{:S(2)}) copy-start(s32[8,32]{1,0:T(8,128)} %param.13) | copy-start | bytes 3076
  7.2 56.9 %all-gather.2.cloned.1.call-start = ((), (), s32[]{:S(2)}) async-start(), calls=%async_computation.2 | async-start | bytes 9437184 | tf_op jit(solution)/shard_map/all_gather | solution.py:254
  33.3 8.9 %copy-start.6 = (s32[8]{0:T(128)S(1)}, s32[8]{0:T(128)}, u32[]{:S(2)}) copy-start(s32[8]{0:T(128)} %param.11) | copy-start | bytes 100
  33.3 11.3 %copy-start.5 = (bf16[2,512]{1,0:T(2,128)(2,1)S(1)}, bf16[2,512]{1,0:T(2,128)(2,1)}, u32[]{:S(2)}) copy-start(bf16[2,512]{1,0:T(2,128)(2,1)} %param.9) | copy-start | bytes 6148
  33.3 113.1 %all-to-all-start = ((bf16[16,2,4,64,512]{4,3,2,1,0:T(8,128)(2,1)}), bf16[16,2,4,64,512]{4,3,2,1,0:T(8,128)(2,1)}, u32[]{:S(2)}, u32[]{:S(2)}) async-start(bf16[16,2,4,64,512]{4,3,2,1,0:T(8,128)(2,1)} %broadcast_select_fusion), calls=%async_computation | async-start | bytes 16777216 | tf_op jit(solution)/shard_map/all_to_all | solution.py:250
  102.1 4.2 %copy-start.3 = (f32[1024,4,128]{2,1,0:T(4,128)S(1)}, f32[1024,4,128]{2,1,0:T(4,128)}, u32[]{:S(2)}) copy-start(f32[1024,4,128]{2,1,0:T(4,128)} %copy.19) | copy-start | bytes 6291460
  113.5 1.9 copy-start.4
  118.2 88.4 %collective-permute-start = (bf16[2,1024,512]{2,1,0:T(8,128)(2,1)S(1)}, bf16[2,1024,512]{2,1,0:T(8,128)(2,1)}, u32[]{:S(2)}, u32[]{:S(2)}) collective-permute-start(bf16[2,1024,512]{2,1,0:T(8,128)(2,1)S(1)} %pad_maximum_fusion), channel_id=1, source_target_pairs={{0,1},{1,0},{2,3},{3,2},{4,5},{5,4},{6,7},{7,6},{8,9},{9,8},{10,11... | collective-permute-start | bytes 6291464 | tf_op jit(solution)/shard_map/ppermute | solution.py:26
  146.5 166.0 %all-to-all-start.1 = ((bf16[16,2,2,64,512]{4,3,2,1,0:T(8,128)(2,1)}), bf16[16,2,2,64,512]{4,3,2,1,0:T(8,128)(2,1)}, u32[]{:S(2)}, u32[]{:S(2)}) async-start(bf16[16,2,2,64,512]{4,3,2,1,0:T(8,128)(2,1)} %broadcast_select_fusion.1), calls=%async_computation.1 | async-start | bytes 8388608 | tf_op jit(solution)/shard_map/all_to_all | solution.py:303
  202.3 4.2 %copy-start.2 = (bf16[1024,1,512]{2,0,1:T(8,128)(2,1)S(1)}, bf16[1024,1,512]{2,0,1:T(8,128)(2,1)}, u32[]{:S(2)}) copy-start(bf16[1024,1,512]{2,0,1:T(8,128)(2,1)} %copy.25) | copy-start | bytes 3145732
Sparse Core Ops, SparseCore 0:
  12.9 51.1 all-gather.1

commit v2 on v1

--- a/solution.py
+++ b/solution.py
@@ -6,6 +6,7 @@
 from jax.experimental import pallas as pl
 from jax.experimental.pallas import tpu as pltpu
 from jax.sharding import PartitionSpec as P
+
 
 D = 4096
 HS = 128
@@ -42,10 +43,10 @@
 
 def online_update(s, v, m_sc, l_sc, acc_sc):
     m_prev = m_sc[...]
-    m_cur = jnp.max(s, axis=1, keepdims=True)
+    m_cur = jnp.max(s, axis=1, keepdims=True) * score_scale
     m_next = jnp.maximum(m_prev, m_cur)
     alpha = jnp.exp(m_prev - m_next)
-    p = jnp.exp(s - m_next[:, :1])
+    p = jnp.exp(s * score_scale - m_next[:, :1])
     l_sc[...] = alpha * l_sc[...] + jnp.sum(p, axis=1, keepdims=True)
     pv = jnp.dot(p.astype(jnp.bfloat16), v, preferred_element_type=jnp.float32)
     acc_sc[...] = acc_sc[...] * alpha + pv
@@ -53,10 +54,7 @@
 
 
 def scores_of(q, k):
-    return (
-        lax.dot_general(q, k, (((1,), (1,)), ((), ())), preferred_element_type=jnp.float32)
-        * score_scale
-    )
+    return lax.dot_general(q, k, (((1,), (1,)), ((), ())), preferred_element_type=jnp.float32)
 
 
 def new_kernel(meta_ref, q_ref, k_ref, v_ref, acc_out, m_out, l_out, m_sc, l_sc, acc_sc):
@@ -72,13 +70,17 @@
         l_sc[...] = jnp.zeros(l_sc.shape, jnp.float32)
         acc_sc[...] = jnp.zeros(acc_sc.shape, jnp.float32)
 
-    @pl.when(k_chunk <= q_chunk)
+    @pl.when(k_chunk < q_chunk)
+    def _():
+        s = scores_of(q_ref[...], k_ref[...])
+        online_update(s, v_ref[...], m_sc, l_sc, acc_sc)
+
+    @pl.when(k_chunk == q_chunk)
     def _():
         s = scores_of(q_ref[...], k_ref[...])
         rows = lax.broadcasted_iota(jnp.int32, s.shape, 0)
         cols = lax.broadcasted_iota(jnp.int32, s.shape, 1)
-        visible = (k_chunk < q_chunk) | (cols <= rows)
-        s = jnp.where(visible, s, -jnp.inf)
+        s = jnp.where(cols <= rows, s, -jnp.inf)
         online_update(s, v_ref[...], m_sc, l_sc, acc_sc)
 
     @pl.when(kj == pl.num_programs(2) - 1)
@@ -102,7 +104,14 @@
         l_sc[...] = l_in[...]
         acc_sc[...] = acc_in[...]
 
-    @pl.when(c * groups * block_len < length)
+    @pl.when((c + 1) * groups * block_len <= length)
+    def _():
+        k = k_ref[...].reshape(tile, HS)
+        v = v_ref[...].reshape(tile, HS)
+        s = scores_of(q_ref[...], k)
+        online_update(s, v, m_sc, l_sc, acc_sc)
+
+    @pl.when((c * groups * block_len < length) & ((c + 1) * groups * block_len > length))
     def _():
         k = k_ref[...].reshape(tile, HS)
         v = v_ref[...].reshape(tile, HS)
@@ -244,7 +253,7 @@
     slot_index = jnp.clip(slot_index, 0, slot_count - 1)
     kv_ids = jnp.arange(2, dtype=jnp.int32)
     out_ids = kv_ids[None, :, None] * slot_count + slot_index[:, None, :]
-    outgoing = jnp.take(kv_flat, out_ids.reshape(-1), axis=0).reshape(
+    outgoing = jnp.take(kv_flat, out_ids.reshape(-1), axis=0, mode="clip").reshape(
         groups, 2, per_dev, block_len, local_width
     )
     received = lax.all_to_all(outgoing, "blk", split_axis=0, concat_axis=0, tiled=True)
@@ -297,7 +306,7 @@
     )
     local_index = jnp.clip(local_index, 0, blocks_dev - 1)
     pick_ids = kv_ids[None, :, None] * blocks_dev + local_index[:, None, :]
-    picked = jnp.take(fresh_flat, pick_ids.reshape(-1), axis=0).reshape(
+    picked = jnp.take(fresh_flat, pick_ids.reshape(-1), axis=0, mode="clip").reshape(
         groups, 2, 2, block_len, local_width
     )
     arrived = lax.all_to_all(picked, "blk", split_axis=0, concat_axis=0, tiled=True)

time: 336 us -> 325 us (0.967)
  the two profiles are of different devices: /device:TPU:10 before, /device:TPU:118 now
where the time goes in v2:
time: 325 us; the launch traced here: 324 us
  Pallas kernels  104 us (32%)
  starting transfers between devices  53.7 us (17%)
  local copies, waits for them, and re-layouts  46.9 us (14%)
  waiting for transfers between devices  44 us (14%)
  other arithmetic  31.7 us (10%)
  matrix products  17.8 us (5%)
  between operations  14.3 us (4%)
  blocking collectives  11.9 us (4%)
    pallas_call x1, Pallas kernels, cached_attention(): pl.pallas_call(functools.partial(cached_kernel, groups=groups, per_half=p...  69.8 us
    all_to_all x1, starting transfers between devices, body(): lax.all_to_all(picked, 'blk', split_axis=0, concat_axis=0, tiled=True)  45.8 us
    pallas_call x1, Pallas kernels, new_attention(): pl.pallas_call(new_kernel, out_shape=(state, state, state), grid_spec=plt...  33.8 us
    all_gather x1, waiting for transfers between devices, body(): lax.all_gather(states, 'head', axis=1, tiled=True)  24.6 us
    all_to_all x1, waiting for transfers between devices, body(): lax.all_to_all(outgoing, 'blk', split_axis=0, concat_axis=0, tiled=True)  19.5 us
    dot_general x1, matrix products, body(): jnp.einsum('tc,jcw->tjw', lax.all_gather(states, 'head', axis=1, tiled=Tr...  17.8 us
    psum x1, blocking collectives, body(): lax.psum((jnp.sum(queries * queries, axis=1), jnp.sum(key_new * key_new,...  11.9 us
    scatter x1, local copies, waits for them, and re-layouts, body(): updated_cache = kv_flat.at[target_ids.reshape(-1)].set(arrived.reshape(gr...  11.5 us
  transfers between devices with their start and end apart: 4, of which 2 were waited for; matrix products, arithmetic and copies ran while one was open for 24% of the time, Pallas kernels for 32%

profile of v2, /device:TPU:118, one launch (start us, length us, event | category | flops | bytes accessed | tf_op | source)
XLA Modules:
  0.0 324.0 jit_solution(3912965192125067812)
XLA Ops:
  7.2 5.5 %copy.24 = bf16[2,40,64,512]{3,2,1,0:T(8,128)(2,1)} copy(bf16[2,40,64,512]{3,2,1,0:T(8,128)(2,1)} %param.10) | data formatting | bytes 10485760
  15.9 9.2 %gather_fusion.2 = bf16[128,64,512]{2,1,0:T(8,128)(2,1)} fusion(bf16[80,64,512]{2,1,0:T(8,128)(2,1)} %bitcast.37, s32[1024]{0:T(1024)S(1)} %pad_clamp_fusion.1), kind=kCustom, calls=%fused_computation.2 | custom fusion | bytes 16777728 | tf_op jit(solution)/shard_map/jit(_take)/gather | solution.py:256
  25.1 7.0 %all-to-all-start = ((bf16[16,2,4,64,512]{4,3,2,1,0:T(8,128)(2,1)}), bf16[16,2,4,64,512]{4,3,2,1,0:T(8,128)(2,1)}, u32[]{:S(2)}, u32[]{:S(2)}) async-start(bf16[16,2,4,64,512]{4,3,2,1,0:T(8,128)(2,1)} %bitcast.40), calls=%async_computation | async-start | bytes 16777216 | tf_op jit(solution)/shard_map/all_to_all | solution.py:259
  34.9 3.0 multiply_cosine_fusion
  38.0 24.6 %all-gather.2.cloned.1.call-done = bf16[1024,4096]{1,0:T(8,128)(2,1)} async-done(((bf16[1024,512]{1,0:T(8,128)(2,1)}), bf16[1024,4096]{1,0:T(8,128)(2,1)}) %all-gather.2.cloned.1.call-update) | async-done | bytes 8388624 | tf_op jit(solution)/shard_map/all_gather | solution.py:263
  62.5 17.8 %fusion = f32[1024,3,512]{0,2,1:T(8,128)S(1)} fusion(bf16[3,4096,512]{2,1,0:T(8,128)(2,1)} %param.8, bf16[1024,4096]{1,0:T(8,128)(2,1)} %all-gather.2.cloned.1.call-done), kind=kOutput, calls=%fused_computation.7 | convolution fusion | flops 12884901888 | bytes 27262976 | tf_op jit(solution)/shard_map/tc,jcw->tjw/dot_general | solution.py:261
  80.3 2.6 copy-done.4
  83.7 4.2 %multiply_reduce_fusion = (f32[1024]{0:T(1024)S(1)}, f32[1024]{0:T(1024)S(1)}, f32[1024,1,512]{0,2,1:T(8,128)}, f32[1024,1,512]{0,2,1:T(8,128)S(1)}) fusion(f32[1024,3,512]{0,2,1:T(8,128)} %copy-done.4), kind=kLoop, calls=%fused_computation.16 | loop fusion | flops 2095104 | bytes 8396800 | tf_op jit(solution)/shard_map/reduce_sum | solution.py:271
  87.9 2.9 copy.15
  90.8 1.8 copy.14
  92.6 11.9 %all-reduce = (f32[1024]{0:T(1024)S(1)}, f32[1024]{0:T(1024)S(1)}) all-reduce(f32[1024]{0:T(1024)S(1)} %get-tuple-element.9, f32[1024]{0:T(1024)S(1)} %get-tuple-element.8), channel_id=1, replica_groups=mesh['head'=8,'blk'=16] {'head'}, use_global_device_ids=true, to_apply=%region_1.2 | all-reduce | flops 2048 | bytes 16384 | tf_op jit(solution)/shard_map/psum | solution.py:270
  104.5 4.2 %multiply_multiply_fusion = f32[1024,4,128]{2,1,0:T(4,128)S(1)} fusion(f32[1024,4,128]{2,1,0:T(4,128)} %copy.15, f32[4,128]{1,0:T(4,128)S(1)} %bitcast.51, f32[1024]{0:T(1024)S(1)} %get-tuple-element.28), kind=kLoop, calls=%fused_computation.15 | loop fusion | flops 1048576 | bytes 4200448 | tf_op jit(solution)/shard_map/mul | solution.py:275
  108.8 3.0 multiply_multiply_fusion.1
  111.8 4.2 %subtract_convert_fusion = (bf16[1024,4,64]{2,1,0:T(4,128)(2,1)S(1)}, bf16[1024,4,64]{2,1,0:T(4,128)(2,1)S(1)}, bf16[1024,4,64]{2,1,0:T(4,128)(2,1)}, bf16[1024,4,64]{2,1,0:T(4,128)(2,1)}) fusion(f32[1024,4,128]{2,1,0:T(4,128)S(1)} %multiply_multiply_fusion, f32[1024,64]{1,0:T(8,128)S(1)} %copy-done.6, f32[1024,64]{1,0:T(8,128)S(1)} %copy-done.5, ...), kind=kLoop, calls=%fused_computation.14 | loop fusion | flops 4194304 | bytes 6815744 | tf_op jit(solution)/shard_map/convert.1
  120.9 2.7 gather_fusion.5
  123.7 19.5 %all-to-all-done.k_ref.v_ref = bf16[16,2,4,64,512]{4,3,2,1,0:T(8,128)(2,1)} async-done(((bf16[16,2,4,64,512]{4,3,2,1,0:T(8,128)(2,1)}), bf16[16,2,4,64,512]{4,3,2,1,0:T(8,128)(2,1)}, u32[]{:S(2)}, u32[]{:S(2)}) %all-to-all-start) | async-done | bytes 8388640 | tf_op jit(solution)/shard_map/all_to_all | solution.py:259
  143.1 45.8 %all-to-all-start.1 = ((bf16[16,2,2,64,512]{4,3,2,1,0:T(8,128)(2,1)}), bf16[16,2,2,64,512]{4,3,2,1,0:T(8,128)(2,1)}, u32[]{:S(2)}, u32[]{:S(2)}) async-start(bf16[16,2,2,64,512]{4,3,2,1,0:T(8,128)(2,1)} %bitcast.42), calls=%async_computation.1 | async-start | bytes 8388608 | tf_op jit(solution)/shard_map/all_to_all | solution.py:312
  190.8 1.9 pad_add_fusion.meta_ref
  192.7 3.0 pad_maximum_fusion.1
  196.9 2.8 maximum_select_fusion
  199.8 2.3 slice_bitcast_fusion
  202.1 33.8 %shard_map.86 = (f32[1024,512]{1,0:T(8,128)}, f32[1024,512]{1,0:T(8,128)}, f32[1024,512]{1,0:T(8,128)}) custom-call(s32[4]{0:T(128)} %pad_add_fusion.meta_ref, bf16[1024,512]{1,0:T(8,128)(2,1)} %bitcast.47, bf16[2048,512]{1,0:T(8,128)(2,1)} %get-tuple-element.15.k_ref, bf16[2048,512]{1,0:T(8,128)(2,1)} %get-tuple-element.14.v_ref), custom_call_target="tpu_custom_call" | custom-call | flops 2147483648 | bytes 12582912 | tf_op jit(solution)/shard_map/pallas_call | solution.py:140
  235.8 69.8 %shard_map.87 = bf16[1024,512]{1,0:T(8,128)(2,1)} custom-call(s32[4]{0:T(128)} %pad_add_fusion.meta_ref, bf16[1024,512]{1,0:T(8,128)(2,1)} %bitcast.48, bf16[16,2,4,64,512]{4,3,2,1,0:T(8,128)(2,1)} %all-to-all-done.k_ref.v_ref, bf16[16,2,4,64,512]{4,3,2,1,0:T(8,128)(2,1)} %all-to-all-done.k_ref.v_ref, f32[1024,512]{1,0:T(8,128)} %get-tuple-element.5.acc_in, ...), custom_call_target="tpu_custom_call" | custom-call | flops 4294967296 | bytes 12582912 | tf_op jit(solution)/shard_map/pallas_call | solution.py:192
  305.6 11.5 %scatter_fusion = bf16[80,64,512]{2,1,0:T(8,128)(2,1)} fusion(bf16[80,64,512]{2,1,0:T(8,128)(2,1)} %bitcast.38, s32[64]{0:T(128)S(1)} %fusion.28, bf16[64,64,512]{2,1,0:T(8,128)(2,1)} %bitcast.17), kind=kCustom, calls=%fused_computation.6 | custom fusion | bytes 12583168 | tf_op jit(solution)/shard_map/scatter | solution.py:327
  (74 shorter events, 14.5 us)
Async XLA Ops:
  7.2 6.6 %copy-start = (s32[8,64]{1,0:T(8,128)S(1)}, s32[8,64]{1,0:T(8,128)}, u32[]{:S(2)}) copy-start(s32[8,64]{1,0:T(8,128)} %param.12) | copy-start | bytes 6148
  7.2 5.6 %copy-start.1 = (s32[8,32]{1,0:T(8,128)S(1)}, s32[8,32]{1,0:T(8,128)}, u32[]{:S(2)}) copy-start(s32[8,32]{1,0:T(8,128)} %param.13) | copy-start | bytes 3076
  7.2 55.3 %all-gather.2.cloned.1.call-start = ((), (), s32[]{:S(2)}) async-start(), calls=%async_computation.2 | async-start | bytes 9437184 | tf_op jit(solution)/shard_map/all_gather | solution.py:263
  25.1 7.6 %copy-start.8 = (s32[8]{0:T(128)S(1)}, s32[8]{0:T(128)}, u32[]{:S(2)}) copy-start(s32[8]{0:T(128)} %param.11) | copy-start | bytes 100
  25.1 9.8 %copy-start.7 = (bf16[2,512]{1,0:T(2,128)(2,1)S(1)}, bf16[2,512]{1,0:T(2,128)(2,1)}, u32[]{:S(2)}) copy-start(bf16[2,512]{1,0:T(2,128)(2,1)} %param.9) | copy-start | bytes 6148
  25.1 118.0 %all-to-all-start = ((bf16[16,2,4,64,512]{4,3,2,1,0:T(8,128)(2,1)}), bf16[16,2,4,64,512]{4,3,2,1,0:T(8,128)(2,1)}, u32[]{:S(2)}, u32[]{:S(2)}) async-start(bf16[16,2,4,64,512]{4,3,2,1,0:T(8,128)(2,1)} %bitcast.40), calls=%async_computation | async-start | bytes 16777216 | tf_op jit(solution)/shard_map/all_to_all | solution.py:259
  80.3 2.6 copy-start.4
  104.5 4.2 %copy-start.3 = (f32[1024,4,128]{2,1,0:T(4,128)S(1)}, f32[1024,4,128]{2,1,0:T(4,128)}, u32[]{:S(2)}) copy-start(f32[1024,4,128]{2,1,0:T(4,128)} %copy.14) | copy-start | bytes 6291460
  108.8 3.0 copy-start.5
  108.8 3.0 copy-start.6
  120.1 76.8 %collective-permute-start = (bf16[2,1024,512]{2,1,0:T(8,128)(2,1)S(1)}, bf16[2,1024,512]{2,1,0:T(8,128)(2,1)}, u32[]{:S(2)}, u32[]{:S(2)}) collective-permute-start(bf16[2,1024,512]{2,1,0:T(8,128)(2,1)S(1)} %pad_maximum_fusion), channel_id=1, source_target_pairs={{0,1},{1,0},{2,3},{3,2},{4,5},{5,4},{6,7},{7,6},{8,9},{9,8},{10,11... | collective-permute-start | bytes 6291464 | tf_op jit(solution)/shard_map/ppermute | solution.py:27
  143.1 162.5 %all-to-all-start.1 = ((bf16[16,2,2,64,512]{4,3,2,1,0:T(8,128)(2,1)}), bf16[16,2,2,64,512]{4,3,2,1,0:T(8,128)(2,1)}, u32[]{:S(2)}, u32[]{:S(2)}) async-start(bf16[16,2,2,64,512]{4,3,2,1,0:T(8,128)(2,1)} %bitcast.42), calls=%async_computation.1 | async-start | bytes 8388608 | tf_op jit(solution)/shard_map/all_to_all | solution.py:312
  192.7 4.2 %copy-start.2 = (bf16[1,1024,512]{2,1,0:T(8,128)(2,1)S(1)}, bf16[1,1024,512]{2,1,0:T(8,128)(2,1)}, u32[]{:S(2)}) copy-start(bf16[1,1024,512]{2,1,0:T(8,128)(2,1)} %convert_element_type.39) | copy-start | bytes 3145732
Sparse Core Ops, SparseCore 0:
  12.9 49.5 all-gather.1

commit v3 on v2

--- a/solution.py
+++ b/solution.py
@@ -15,16 +15,6 @@
 rope_base = 500000.0
 norm_eps = 1e-06
 score_scale = HS ** (-0.5)
-
-
-def swapped(block, axis, apart):
-    count = lax.axis_size(axis)
-    route = []
-    for low in range(count):
-        high = low | 1 << apart
-        if high != low and high < count:
-            route += [(low, high), (high, low)]
-    return lax.ppermute(block, axis, route)
 
 
 def rotate(values, positions, head_size):
@@ -57,18 +47,30 @@
     return lax.dot_general(q, k, (((1,), (1,)), ((), ())), preferred_element_type=jnp.float32)
 
 
-def new_kernel(meta_ref, q_ref, k_ref, v_ref, acc_out, m_out, l_out, m_sc, l_sc, acc_sc):
+def new_kernel(meta_ref, q_ref, k_ref, v_ref, *rest, partner):
+    if partner:
+        acc_in, m_in, l_in, acc_out, m_out, l_out, m_sc, l_sc, acc_sc = rest
+    else:
+        acc_out, m_out, l_out, m_sc, l_sc, acc_sc = rest
     qi = pl.program_id(1)
     kj = pl.program_id(2)
     member = meta_ref[0]
     q_chunk = jnp.where(qi == 0, member, 3 - member)
-    k_chunk = jnp.where(kj == 0, 0, jnp.where(kj == 1, 3, kj - 1))
+    if partner:
+        k_chunk = jnp.where(kj == 0, 1 - member, 2 + member)
+    else:
+        k_chunk = jnp.where(kj == 0, member, 3 - member)
 
     @pl.when(kj == 0)
     def _():
-        m_sc[...] = jnp.full(m_sc.shape, -jnp.inf, jnp.float32)
-        l_sc[...] = jnp.zeros(l_sc.shape, jnp.float32)
-        acc_sc[...] = jnp.zeros(acc_sc.shape, jnp.float32)
+        if partner:
+            m_sc[...] = m_in[...]
+            l_sc[...] = l_in[...]
+            acc_sc[...] = acc_in[...]
+        else:
+            m_sc[...] = jnp.full(m_sc.shape, -jnp.inf, jnp.float32)
+            l_sc[...] = jnp.zeros(l_sc.shape, jnp.float32)
+            acc_sc[...] = jnp.zeros(acc_sc.shape, jnp.float32)
 
     @pl.when(k_chunk < q_chunk)
     def _():
@@ -128,26 +130,31 @@
         o_ref[...] = (acc_sc[...] / l_sc[...]).astype(o_ref.dtype)
 
 
-def new_attention(meta, queries, keys, values):
+def new_attention(meta, queries, keys, values, state=None):
     tok_rows, width = queries.shape
     heads = width // HS
     q_rows = tok_rows // 2
     key_rows = keys.shape[0]
     k_tiles = key_rows // q_rows
-    state = jax.ShapeDtypeStruct((tok_rows, width), jnp.float32)
+    partner = state is not None
+    shape = jax.ShapeDtypeStruct((tok_rows, width), jnp.float32)
     state_spec = pl.BlockSpec((q_rows, HS), lambda h, i, j, meta: (i, h))
-    flops = 2 * 2 * tok_rows * key_rows * width
+    in_specs = [
+        pl.BlockSpec((q_rows, HS), lambda h, i, j, meta: (i, h)),
+        pl.BlockSpec((q_rows, HS), lambda h, i, j, meta: (j, h)),
+        pl.BlockSpec((q_rows, HS), lambda h, i, j, meta: (j, h)),
+    ]
+    operands = [meta, queries, keys, values]
+    if partner:
+        in_specs += [state_spec] * 3
+        operands += list(state)
     return pl.pallas_call(
-        new_kernel,
-        out_shape=(state, state, state),
+        functools.partial(new_kernel, partner=partner),
+        out_shape=(shape, shape, shape),
         grid_spec=pltpu.PrefetchScalarGridSpec(
             num_scalar_prefetch=1,
             grid=(heads, 2, k_tiles),
-            in_specs=[
-                pl.BlockSpec((q_rows, HS), lambda h, i, j, meta: (i, h)),
-                pl.BlockSpec((q_rows, HS), lambda h, i, j, meta: (j, h)),
-                pl.BlockSpec((q_rows, HS), lambda h, i, j, meta: (j, h)),
-            ],
+            in_specs=in_specs,
             out_specs=[state_spec, state_spec, state_spec],
             scratch_shapes=[
                 pltpu.VMEM((q_rows, HS), jnp.float32),
@@ -159,11 +166,11 @@
             dimension_semantics=("arbitrary", "arbitrary", "arbitrary")
         ),
         cost_estimate=pl.CostEstimate(
-            flops=flops // 2,
-            transcendentals=tok_rows * key_rows * heads // 2,
-            bytes_accessed=2 * tok_rows * width * 2 + 2 * 2 * key_rows * width + 3 * 4 * tok_rows * width,
-        ),
-    )(meta, queries, keys, values)
+            flops=2 * 2 * tok_rows * key_rows * width * 3 // 4,
+            transcendentals=tok_rows * key_rows * heads * 3 // 4,
+            bytes_accessed=2 * tok_rows * width + 2 * 2 * key_rows * width + 6 * 4 * tok_rows * width,
+        ),
+    )(*operands)
 
 
 def cached_attention(meta, queries, received, acc, m, l):
@@ -228,22 +235,21 @@
     half_rows = tok_rows // 2
     local_width = qkv_weight.shape[2]
     local_heads = local_width // HS
-    groups = lax.axis_size("blk")
+    pair = lax.axis_size("bp")
+    groups = lax.axis_size("bx") * pair
     slot_count = kv_cache.shape[1]
     block_len = kv_cache.shape[2]
-    requests = cached_len.shape[0]
-    group_size = groups // requests
     per_dev = old_table.shape[1] // groups
-    my_index = lax.axis_index("blk")
-    request = my_index // group_size
-    member = my_index % group_size
-    late_block = 2 * group_size - 1 - member
+    request = lax.axis_index("bx")
+    member = lax.axis_index("bp")
+    my_index = request * pair + member
+    late_block = 2 * pair - 1 - member
     targets = jnp.arange(groups, dtype=jnp.int32)
+    kv_ids = jnp.arange(2, dtype=jnp.int32)
     kv_flat = kv_cache.reshape(2 * slot_count, block_len, local_width)
 
-    lengths_blocks = jnp.sum((old_table >= 0).astype(jnp.int32), axis=1)
     first_dev = old_table[:, 0] // slot_count
-    target_req = targets // group_size
+    target_req = targets // pair
     c_index = jnp.arange(per_dev, dtype=jnp.int32)
     block_index = ((my_index - first_dev[target_req]) % groups)[:, None] + groups * c_index[None, :]
     slot_index = (
@@ -251,12 +257,13 @@
         - my_index * slot_count
     )
     slot_index = jnp.clip(slot_index, 0, slot_count - 1)
-    kv_ids = jnp.arange(2, dtype=jnp.int32)
     out_ids = kv_ids[None, :, None] * slot_count + slot_index[:, None, :]
     outgoing = jnp.take(kv_flat, out_ids.reshape(-1), axis=0, mode="clip").reshape(
         groups, 2, per_dev, block_len, local_width
     )
-    received = lax.all_to_all(outgoing, "blk", split_axis=0, concat_axis=0, tiled=True)
+    received = lax.all_to_all(
+        outgoing, ("bx", "bp"), split_axis=0, concat_axis=0, tiled=True
+    )
 
     projected = jnp.einsum(
         "tc,jcw->tjw",
@@ -290,71 +297,65 @@
     )
     value_new = value_new.astype(jnp.bfloat16)
     fresh_kv = jnp.stack([key_new, value_new])
+    meta = jnp.stack([member, cached_len[request], first_dev[request], 0]).astype(jnp.int32)
+
+    partner_new = lax.ppermute(fresh_kv, "bp", [(0, 1), (1, 0)])
+    state = new_attention(meta, queries, fresh_kv[0], fresh_kv[1])
 
     blocks_dev = tok_rows // block_len
-    half_blocks = blocks_dev // 2
-    new_count = new_table.shape[1]
-    fresh_flat = fresh_kv.reshape(2 * blocks_dev, block_len, local_width)
+    chunk_blocks = blocks_dev // 2
+    collected = jnp.where(
+        member == 0,
+        jnp.concatenate([fresh_kv, partner_new], axis=1),
+        jnp.concatenate([partner_new, fresh_kv], axis=1),
+    )
+    new_blocks = 2 * blocks_dev
+    collected_flat = collected.reshape(2 * new_blocks, block_len, local_width)
+    chunk_place = jnp.array([0, 2, 3, 1], dtype=jnp.int32)
+    new_home = new_table[:, 0] // slot_count
     pair_index = jnp.arange(2, dtype=jnp.int32)
-    new_home = new_table[:, 0] // slot_count
-    wanted_out = 2 * ((targets - new_home[request]) % groups)[:, None] + pair_index[None, :]
-    out_half = wanted_out // half_blocks
-    local_index = jnp.where(
-        out_half == member,
-        wanted_out - member * half_blocks,
-        wanted_out - late_block * half_blocks + half_blocks,
-    )
-    local_index = jnp.clip(local_index, 0, blocks_dev - 1)
-    pick_ids = kv_ids[None, :, None] * blocks_dev + local_index[:, None, :]
-    picked = jnp.take(fresh_flat, pick_ids.reshape(-1), axis=0, mode="clip").reshape(
-        groups, 2, 2, block_len, local_width
-    )
-    arrived = lax.all_to_all(picked, "blk", split_axis=0, concat_axis=0, tiled=True)
-    source_req = targets // group_size
-    source_member = targets % group_size
-    source_late = 2 * group_size - 1 - source_member
-    wanted_in = 2 * ((my_index - new_home[source_req]) % groups)[:, None] + pair_index[None, :]
-    in_half = wanted_in // half_blocks
-    valid_in = (in_half == source_member[:, None]) | (in_half == source_late[:, None])
+    reqs = jnp.arange(groups // pair, dtype=jnp.int32)
+    dest = reqs * pair + member
+    wanted_out = 2 * ((dest - new_home[request]) % groups)[:, None] + pair_index[None, :]
+    place = chunk_place[wanted_out // chunk_blocks] * chunk_blocks + wanted_out % chunk_blocks
+    pick_ids = kv_ids[None, :, None] * new_blocks + place[:, None, :]
+    picked = jnp.take(collected_flat, pick_ids.reshape(-1), axis=0, mode="clip").reshape(
+        groups // pair, 2, 2, block_len, local_width
+    )
+    arrived = lax.all_to_all(picked, "bx", split_axis=0, concat_axis=0, tiled=True)
+    wanted_in = 2 * ((my_index - new_home) % groups)[:, None] + pair_index[None, :]
     target_slot = (
-        new_table[source_req[:, None], jnp.clip(wanted_in, 0, new_count - 1)]
+        new_table[reqs[:, None], jnp.clip(wanted_in, 0, new_table.shape[1] - 1)]
         - my_index * slot_count
     )
     target_ids = kv_ids[None, :, None] * slot_count + target_slot[:, None, :]
-    target_ids = jnp.where(valid_in[:, None, :], target_ids, 2 * slot_count)
     updated_cache = (
         kv_flat.at[target_ids.reshape(-1)]
-        .set(arrived.reshape(groups * 4, block_len, local_width), mode="drop")
+        .set(arrived.reshape(-1, block_len, local_width), mode="drop")
         .reshape(kv_cache.shape)
     )
 
-    collected = fresh_kv
-    partner_new = swapped(collected, "blk", 0)
-    lower_new = member // 2**0 % 2 == 0
-    collected = jnp.where(
-        lower_new,
-        jnp.concatenate([collected, partner_new], axis=1),
-        jnp.concatenate([partner_new, collected], axis=1),
-    )
-    meta = jnp.stack([member, cached_len[request], first_dev[request], 0]).astype(jnp.int32)
-    acc, m, l = new_attention(meta, queries, collected[0], collected[1])
-    attended = cached_attention(meta, queries, received, acc, m, l)
+    state = new_attention(meta, queries, partner_new[0], partner_new[1], state)
+    attended = cached_attention(meta, queries, received, *state)
     return (attended, updated_cache)
 
 
 def solution(mesh):
+    heads, groups = mesh.devices.shape
+    split = jax.sharding.Mesh(mesh.devices.reshape(heads, groups // 2, 2), ("head", "bx", "bp"))
+    blk = ("bx", "bp")
     return jax.shard_map(
         body,
-        mesh=mesh,
+        mesh=split,
         in_specs=(
-            P("blk", "head"),
+            P(blk, "head"),
             P(None, None, "head"),
             P(None, "head"),
-            P(None, "blk", None, "head"),
+            P(None, blk, None, "head"),
             P(),
             P(),
             P(),
         ),
-        out_specs=(P("blk", "head"), P(None, "blk", None, "head")),
+        out_specs=(P(blk, "head"), P(None, blk, None, "head")),
         check_vma=False,
     )

time: 325 us -> 334 us (1.028)
  the two profiles are of different devices: /device:TPU:118 before, /device:TPU:110 now
where the time goes in v3:
time: 334 us; the launch traced here: 333 us
  Pallas kernels  110 us (33%)
  waiting for transfers between devices  81.9 us (25%)
  local copies, waits for them, and re-layouts  43.4 us (13%)
  other arithmetic  32.6 us (10%)
  starting transfers between devices  20.5 us (6%)
  matrix products  17.8 us (5%)
  between operations  14.4 us (4%)
  blocking collectives  12.4 us (4%)
    pallas_call x1, Pallas kernels, cached_attention(): pl.pallas_call(functools.partial(cached_kernel, groups=groups, per_half=p...  70.1 us
    ppermute x1, waiting for transfers between devices, body(): partner_new = lax.ppermute(fresh_kv, 'bp', [(0, 1), (1, 0)])  56 us
    pallas_call x2, Pallas kernels, new_attention(): pl.pallas_call(functools.partial(new_kernel, partner=partner), out_shape=...  40 us
    all_gather x1, waiting for transfers between devices, body(): lax.all_gather(states, 'head', axis=1, tiled=True)  25.9 us
    dot_general x1, matrix products, body(): jnp.einsum('tc,jcw->tjw', lax.all_gather(states, 'head', axis=1, tiled=Tr...  17.8 us
    all_to_all x1, starting transfers between devices, body(): lax.all_to_all(picked, 'bx', split_axis=0, concat_axis=0, tiled=True)  12.7 us
    psum x1, blocking collectives, body(): lax.psum((jnp.sum(queries * queries, axis=1), jnp.sum(key_new * key_new,...  12.4 us
    unnamed x26, local copies, waits for them, and re-layouts  11.1 us
  transfers between devices with their start and end apart: 4, of which 2 were waited for; matrix products, arithmetic and copies ran while one was open for 24% of the time, Pallas kernels for 33%

profile of v3, /device:TPU:110, one launch (start us, length us, event | category | flops | bytes accessed | tf_op | source)
XLA Modules:
  0.0 333.0 jit_solution(8706543364362463024)
XLA Ops:
  7.2 5.5 %copy.28 = bf16[2,40,64,512]{3,2,1,0:T(8,128)(2,1)} copy(bf16[2,40,64,512]{3,2,1,0:T(8,128)(2,1)} %param.11) | data formatting | bytes 10485760
  15.0 9.0 %gather_fusion.2 = bf16[128,64,512]{2,1,0:T(8,128)(2,1)} fusion(bf16[80,64,512]{2,1,0:T(8,128)(2,1)} %bitcast.46, s32[1024]{0:T(1024)S(1)} %pad_clamp_fusion.2), kind=kCustom, calls=%fused_computation.2 | custom fusion | bytes 16777728 | tf_op jit(solution)/shard_map/jit(_take)/gather | solution.py:261
  24.0 7.0 %all-to-all-start = ((bf16[16,2,4,64,512]{4,3,2,1,0:T(8,128)(2,1)}), bf16[16,2,4,64,512]{4,3,2,1,0:T(8,128)(2,1)}, u32[]{:S(2)}, u32[]{:S(2)}) async-start(bf16[16,2,4,64,512]{4,3,2,1,0:T(8,128)(2,1)} %bitcast.49), calls=%async_computation | async-start | bytes 16777216 | tf_op jit(solution)/shard_map/all_to_all | solution.py:264
  33.3 3.1 multiply_cosine_fusion
  37.0 25.9 %all-gather.2.cloned.1.call-done = bf16[1024,4096]{1,0:T(8,128)(2,1)} async-done(((bf16[1024,512]{1,0:T(8,128)(2,1)}), bf16[1024,4096]{1,0:T(8,128)(2,1)}) %all-gather.2.cloned.1.call-update) | async-done | bytes 8388624 | tf_op jit(solution)/shard_map/all_gather | solution.py:270
  62.9 17.8 %fusion = f32[1024,3,512]{0,2,1:T(8,128)S(1)} fusion(bf16[3,4096,512]{2,1,0:T(8,128)(2,1)} %param.9, bf16[1024,4096]{1,0:T(8,128)(2,1)} %all-gather.2.cloned.1.call-done), kind=kOutput, calls=%fused_computation.7 | convolution fusion | flops 12884901888 | bytes 27262976 | tf_op jit(solution)/shard_map/tc,jcw->tjw/dot_general | solution.py:268
  80.7 2.6 copy-done.8
  84.0 4.6 %multiply_reduce_fusion = (f32[1024]{0:T(1024)S(1)}, f32[1024]{0:T(1024)S(1)}, f32[1024,1,512]{0,2,1:T(8,128)S(1)}, f32[1024,1,512]{0,2,1:T(8,128)}) fusion(f32[1024,3,512]{0,2,1:T(8,128)} %copy-done.8), kind=kLoop, calls=%fused_computation.15 | loop fusion | flops 2095104 | bytes 8396800 | tf_op jit(solution)/shard_map/reduce_sum | solution.py:278
  88.6 1.9 copy.16
  90.5 12.4 %all-reduce = (f32[1024]{0:T(1024)S(1)}, f32[1024]{0:T(1024)S(1)}) all-reduce(f32[1024]{0:T(1024)S(1)} %get-tuple-element.15, f32[1024]{0:T(1024)S(1)} %get-tuple-element.14), channel_id=1, replica_groups=mesh['head'=8,'bx'=8,'bp'=2] {'head'}, use_global_device_ids=true, to_apply=%region_1.2 | all-reduce | flops 2048 | bytes 16384 | tf_op jit(solution)/shard_map/psum | solution.py:277
  102.9 4.2 %multiply_multiply_fusion = f32[1024,4,128]{2,1,0:T(4,128)S(1)} fusion(f32[1024,4,128]{2,1,0:T(4,128)} %copy.16, f32[4,128]{1,0:T(4,128)S(1)} %bitcast.65, f32[1024]{0:T(1024)S(1)} %get-tuple-element.34), kind=kLoop, calls=%fused_computation.14 | loop fusion | flops 1048576 | bytes 4200448 | tf_op jit(solution)/shard_map/mul | solution.py:282
  115.9 2.0 pad_add_fusion.meta_ref
  119.0 2.9 copy.15
  121.9 56.0 %collective-permute-done = bf16[2,1024,512]{2,1,0:T(8,128)(2,1)} collective-permute-done((bf16[2,1024,512]{2,1,0:T(8,128)(2,1)}, bf16[2,1024,512]{2,1,0:T(8,128)(2,1)}, u32[]{:S(2)}, u32[]{:S(2)}) %collective-permute-start) | collective-permute-done | bytes 2097184 | tf_op jit(solution)/shard_map/ppermute | solution.py:302
  178.0 4.3 %maximum_select_fusion = bf16[2,2048,512]{2,1,0:T(8,128)(2,1)} fusion(bf16[2,1024,512]{2,1,0:T(8,128)(2,1)} %collective-permute-done, bf16[1,1024,512]{2,1,0:T(8,128)(2,1)S(1)} %bitcast.56, bf16[1,1024,512]{2,1,0:T(8,128)(2,1)S(1)} %convert_element_type.32, pred[]{:T(512)S(6)} %eq.10), kind=kLoop, calls=%fused_computation.9 | loop fusion | flops 27262976 | bytes 8388609 | tf_op jit(solution)/shard_map/jit(_where)/select_n | solution.py:307
  182.3 4.2 %gather_fusion.5 = bf16[32,64,512]{2,1,0:T(8,128)(2,1)} fusion(bf16[64,64,512]{2,1,0:T(8,128)(2,1)} %bitcast.54, s32[1024]{0:T(1024)S(1)} %pad_clamp_fusion), kind=kCustom, calls=%fused_computation.5 | custom fusion | bytes 4194432 | tf_op jit(solution)/shard_map/jit(_take)/gather | solution.py:322
  186.5 12.7 %all-to-all-start.1 = ((bf16[8,2,2,64,512]{4,3,2,1,0:T(8,128)(2,1)}), bf16[8,2,2,64,512]{4,3,2,1,0:T(8,128)(2,1)S(1)}, u32[]{:S(2)}, u32[]{:S(2)}) async-start(bf16[8,2,2,64,512]{4,3,2,1,0:T(8,128)(2,1)} %bitcast.61), calls=%async_computation.1 | async-start | bytes 4194304 | tf_op jit(solution)/shard_map/all_to_all | solution.py:325
  199.1 4.2 %multiply_multiply_fusion.1 = f32[1024,4,128]{2,1,0:T(4,128)S(1)} fusion(f32[1024,4,128]{2,1,0:T(4,128)} %copy.15, f32[4,128]{1,0:T(4,128)S(1)} %bitcast.64, f32[1024]{0:T(1024)S(1)} %get-tuple-element.35), kind=kLoop, calls=%fused_computation.18 | loop fusion | flops 1048576 | bytes 4200448 | tf_op jit(solution)/shard_map/mul | solution.py:281
  203.3 1.7 subtract_convert_fusion
  207.7 18.4 %shard_map.95 = (f32[1024,512]{1,0:T(8,128)}, f32[1024,512]{1,0:T(8,128)}, f32[1024,512]{1,0:T(8,128)}) custom-call(s32[4]{0:T(128)} %pad_add_fusion.meta_ref, bf16[1024,512]{1,0:T(8,128)(2,1)} %bitcast.50, bf16[1024,512]{1,0:T(8,128)(2,1)} %bitcast.63, bf16[1024,512]{1,0:T(8,128)(2,1)} %bitcast.57), custom_call_target="tpu_custom_call" | custom-call | flops 1610612736 | bytes 15728640 | tf_op jit(solution)/shard_map/pallas_call | solution.py:151
  226.1 3.0 slice_bitcast_fusion
  229.1 21.6 %shard_map.96 = (f32[1024,512]{1,0:T(8,128)}, f32[1024,512]{1,0:T(8,128)}, f32[1024,512]{1,0:T(8,128)}) custom-call(s32[4]{0:T(128)} %pad_add_fusion.meta_ref, bf16[1024,512]{1,0:T(8,128)(2,1)} %bitcast.51, bf16[1024,512]{1,0:T(8,128)(2,1)} %get-tuple-element.29.k_ref, bf16[1024,512]{1,0:T(8,128)(2,1)} %get-tuple-element.28.v_ref, ...), custom_call_target="tpu_custom_call" | custom-call | flops 1610612736 | bytes 15728640 | tf_op jit(solution)/shard_map/pallas_call | solution.py:151
  250.7 70.1 %shard_map.97 = bf16[1024,512]{1,0:T(8,128)(2,1)} custom-call(s32[4]{0:T(128)} %pad_add_fusion.meta_ref, bf16[1024,512]{1,0:T(8,128)(2,1)} %bitcast.52, bf16[16,2,4,64,512]{4,3,2,1,0:T(8,128)(2,1)} %all-to-all-done.k_ref.v_ref, bf16[16,2,4,64,512]{4,3,2,1,0:T(8,128)(2,1)} %all-to-all-done.k_ref.v_ref, f32[1024,512]{1,0:T(8,128)} %get-tuple-element.11.acc_in, ...), custom_call_target="tpu_custom_call" | custom-call | flops 4294967296 | bytes 12582912 | tf_op jit(solution)/shard_map/pallas_call | solution.py:199
  320.8 5.3 %scatter_fusion = bf16[80,64,512]{2,1,0:T(8,128)(2,1)} fusion(bf16[80,64,512]{2,1,0:T(8,128)(2,1)} %bitcast.47, s32[32]{0:T(128)S(1)} %fusion.31, bf16[32,64,512]{2,1,0:T(8,128)(2,1)S(1)} %bitcast.59), kind=kCustom, calls=%fused_computation.6 | custom fusion | bytes 6291584 | tf_op jit(solution)/shard_map/scatter | solution.py:334
  (83 shorter events, 18.4 us)
Async XLA Ops:
  7.2 5.6 %copy-start.1 = (s32[8,64]{1,0:T(8,128)S(1)}, s32[8,64]{1,0:T(8,128)}, u32[]{:S(2)}) copy-start(s32[8,64]{1,0:T(8,128)} %param.13) | copy-start | bytes 6148
  7.2 55.7 %all-gather.2.cloned.1.call-start = ((), (), s32[]{:S(2)}) async-start(), calls=%async_computation.2 | async-start | bytes 9437184 | tf_op jit(solution)/shard_map/all_gather | solution.py:270
  24.0 7.0 %copy-start.10 = (s32[8]{0:T(128)S(1)}, s32[8]{0:T(128)}, u32[]{:S(2)}) copy-start(s32[8]{0:T(128)} %param.12) | copy-start | bytes 100
  24.0 7.7 %copy-start.2 = (s32[8,32]{1,0:T(8,128)S(1)}, s32[8,32]{1,0:T(8,128)}, u32[]{:S(2)}) copy-start(s32[8,32]{1,0:T(8,128)} %param.14) | copy-start | bytes 3076
  24.0 9.3 %copy-start.9 = (bf16[2,512]{1,0:T(2,128)(2,1)S(1)}, bf16[2,512]{1,0:T(2,128)(2,1)}, u32[]{:S(2)}) copy-start(bf16[2,512]{1,0:T(2,128)(2,1)} %param.10) | copy-start | bytes 6148
  24.0 162.5 %all-to-all-start = ((bf16[16,2,4,64,512]{4,3,2,1,0:T(8,128)(2,1)}), bf16[16,2,4,64,512]{4,3,2,1,0:T(8,128)(2,1)}, u32[]{:S(2)}, u32[]{:S(2)}) async-start(bf16[16,2,4,64,512]{4,3,2,1,0:T(8,128)(2,1)} %bitcast.49), calls=%async_computation | async-start | bytes 16777216 | tf_op jit(solution)/shard_map/all_to_all | solution.py:264
  80.6 2.7 copy-start.8
  84.0 93.9 %copy-start.3 = (bf16[1024,1,512]{2,0,1:T(8,128)(2,1)}, bf16[1024,1,512]{2,0,1:T(8,128)(2,1)S(1)}, u32[]{:S(2)}) copy-start(bf16[1024,1,512]{2,0,1:T(8,128)(2,1)S(1)} %copy.19) | copy-start | bytes 3145732
  102.9 4.2 %copy-start.4 = (f32[1024,64]{1,0:T(8,128)S(1)}, f32[1024,64]{1,0:T(8,128)}, u32[]{:S(2)}) copy-start(f32[1024,64]{1,0:T(8,128)} %get-tuple-element.30) | copy-start | bytes 786436
  102.9 4.2 %copy-start.6 = (f32[1024,64]{1,0:T(8,128)S(1)}, f32[1024,64]{1,0:T(8,128)}, u32[]{:S(2)}) copy-start(f32[1024,64]{1,0:T(8,128)} %get-tuple-element.31) | copy-start | bytes 786436
  110.7 3.1 copy-start
  112.3 65.7 %collective-permute-start = (bf16[2,1024,512]{2,1,0:T(8,128)(2,1)}, bf16[2,1024,512]{2,1,0:T(8,128)(2,1)}, u32[]{:S(2)}, u32[]{:S(2)}) collective-permute-start(bf16[2,1024,512]{2,1,0:T(8,128)(2,1)} %pad_maximum_fusion), channel_id=1, source_target_pairs={{0,1},{1,0},{2,3},{3,2},{4,5},{5,4},{6,7},{7,6},{8,9},{9,8},{10,11... | collective-permute-start | bytes 6291464 | tf_op jit(solution)/shard_map/ppermute | solution.py:302
  186.5 134.3 %all-to-all-start.1 = ((bf16[8,2,2,64,512]{4,3,2,1,0:T(8,128)(2,1)}), bf16[8,2,2,64,512]{4,3,2,1,0:T(8,128)(2,1)S(1)}, u32[]{:S(2)}, u32[]{:S(2)}) async-start(bf16[8,2,2,64,512]{4,3,2,1,0:T(8,128)(2,1)} %bitcast.61), calls=%async_computation.1 | async-start | bytes 4194304 | tf_op jit(solution)/shard_map/all_to_all | solution.py:325
  199.1 4.2 %copy-start.5 = (f32[1024,64]{1,0:T(8,128)S(1)}, f32[1024,64]{1,0:T(8,128)}, u32[]{:S(2)}) copy-start(f32[1024,64]{1,0:T(8,128)} %get-tuple-element.30) | copy-start | bytes 786436
  199.1 4.2 %copy-start.7 = (f32[1024,64]{1,0:T(8,128)S(1)}, f32[1024,64]{1,0:T(8,128)}, u32[]{:S(2)}) copy-start(f32[1024,64]{1,0:T(8,128)} %get-tuple-element.31) | copy-start | bytes 786436
Sparse Core Ops, SparseCore 0:
  12.9 49.9 all-gather.1

commit v4 on v3

--- a/solution.py
+++ b/solution.py
@@ -92,15 +92,19 @@
         l_out[...] = l_sc[...]
 
 
-def cached_kernel(meta_ref, q_ref, k_ref, v_ref, acc_in, m_in, l_in, o_ref, m_sc, l_sc, acc_sc,
-                  *, groups, per_half, block_len):
-    c = pl.program_id(1)
+def cached_kernel(meta_ref, q_ref, k_ref, v_ref, acc_in, m_in, l_in, *rest,
+                  groups, per_half, block_len, level0, final):
+    if final:
+        o_ref, m_sc, l_sc, acc_sc = rest
+    else:
+        acc_out, m_out, l_out, m_sc, l_sc, acc_sc = rest
+    c = pl.program_id(1) + level0
     half = pl.program_id(2)
     length = meta_ref[1]
     first = meta_ref[2]
     tile = per_half * block_len
 
-    @pl.when((c == 0) & (half == 0))
+    @pl.when((pl.program_id(1) == 0) & (half == 0))
     def _():
         m_sc[...] = m_in[...]
         l_sc[...] = l_in[...]
@@ -125,9 +129,14 @@
         s = jnp.where(visible, s, -jnp.inf)
         online_update(s, v, m_sc, l_sc, acc_sc)
 
-    @pl.when((c == pl.num_programs(1) - 1) & (half == pl.num_programs(2) - 1))
-    def _():
-        o_ref[...] = (acc_sc[...] / l_sc[...]).astype(o_ref.dtype)
+    @pl.when((pl.program_id(1) == pl.num_programs(1) - 1) & (half == pl.num_programs(2) - 1))
+    def _():
+        if final:
+            o_ref[...] = (acc_sc[...] / l_sc[...]).astype(o_ref.dtype)
+        else:
+            acc_out[...] = acc_sc[...]
+            m_out[...] = m_sc[...]
+            l_out[...] = l_sc[...]
 
 
 def new_attention(meta, queries, keys, values, state=None):
@@ -173,20 +182,20 @@
     )(*operands)
 
 
-def cached_attention(meta, queries, received, acc, m, l):
+def cached_attention(meta, queries, received, acc, m, l, level0, final):
     tok_rows, width = queries.shape
     heads = width // HS
-    groups, _, per_dev, block_len, _ = received.shape
+    groups, _, levels, block_len, _ = received.shape
     per_half = groups // 2
 
     def kv_map(index):
         def index_map(h, c, half, meta):
-            last = (meta[1] + groups * block_len - 1) // (groups * block_len) - 1
+            last = (meta[1] + groups * block_len - 1) // (groups * block_len) - 1 - level0
             skip = c > last
             return (
                 jnp.where(skip, 1, half),
                 index,
-                jnp.where(skip, last, c),
+                jnp.where(skip, jnp.clip(last, 0, levels - 1), c),
                 0,
                 h,
             )
@@ -195,15 +204,23 @@
 
     kv_block = (per_half, None, None, block_len, HS)
     state_spec = pl.BlockSpec((tok_rows, HS), lambda h, c, half, meta: (0, h))
-    keys_total = groups * per_dev * block_len
+    keys_total = groups * levels * block_len
+    if final:
+        out_shape = jax.ShapeDtypeStruct((tok_rows, width), jnp.bfloat16)
+        out_specs = state_spec
+    else:
+        state = jax.ShapeDtypeStruct((tok_rows, width), jnp.float32)
+        out_shape = (state, state, state)
+        out_specs = [state_spec, state_spec, state_spec]
     return pl.pallas_call(
         functools.partial(
-            cached_kernel, groups=groups, per_half=per_half, block_len=block_len
-        ),
-        out_shape=jax.ShapeDtypeStruct((tok_rows, width), jnp.bfloat16),
+            cached_kernel, groups=groups, per_half=per_half, block_len=block_len,
+            level0=level0, final=final,
+        ),
+        out_shape=out_shape,
         grid_spec=pltpu.PrefetchScalarGridSpec(
             num_scalar_prefetch=1,
-            grid=(heads, per_dev, 2),
+            grid=(heads, levels, 2),
             in_specs=[
                 pl.BlockSpec((tok_rows, HS), lambda h, c, half, meta: (0, h)),
                 pl.BlockSpec(kv_block, kv_map(0)),
@@ -212,7 +229,7 @@
                 state_spec,
                 state_spec,
             ],
-            out_specs=pl.BlockSpec((tok_rows, HS), lambda h, c, half, meta: (0, h)),
+            out_specs=out_specs,
             scratch_shapes=[
                 pltpu.VMEM((tok_rows, HS), jnp.float32),
                 pltpu.VMEM((tok_rows, HS), jnp.float32),
@@ -225,7 +242,7 @@
         cost_estimate=pl.CostEstimate(
             flops=2 * 2 * tok_rows * keys_total * width // 2,
             transcendentals=tok_rows * keys_total * heads // 2,
-            bytes_accessed=2 * keys_total * width + 2 * tok_rows * width * 2 + 3 * 4 * tok_rows * width,
+            bytes_accessed=2 * keys_total * width + 2 * tok_rows * width * 2 + 6 * 4 * tok_rows * width,
         ),
     )(meta, queries, received, received, acc, m, l)
 
@@ -258,19 +275,19 @@
     )
     slot_index = jnp.clip(slot_index, 0, slot_count - 1)
     out_ids = kv_ids[None, :, None] * slot_count + slot_index[:, None, :]
-    outgoing = jnp.take(kv_flat, out_ids.reshape(-1), axis=0, mode="clip").reshape(
-        groups, 2, per_dev, block_len, local_width
-    )
-    received = lax.all_to_all(
-        outgoing, ("bx", "bp"), split_axis=0, concat_axis=0, tiled=True
-    )
-
-    projected = jnp.einsum(
-        "tc,jcw->tjw",
-        lax.all_gather(states, "head", axis=1, tiled=True),
-        qkv_weight,
-        preferred_element_type=jnp.float32,
-    )
+    low_levels = per_dev // 2
+
+    def cached_part(ids):
+        outgoing = jnp.take(kv_flat, ids.reshape(-1), axis=0, mode="clip").reshape(
+            groups, 2, ids.shape[2], block_len, local_width
+        )
+        return lax.all_to_all(outgoing, ("bx", "bp"), split_axis=0, concat_axis=0, tiled=True)
+
+    received_lo = cached_part(out_ids[:, :, :low_levels])
+    received_hi = cached_part(out_ids[:, :, low_levels:])
+
+    gathered = lax.all_gather(states, "head", axis=1, tiled=True)
+    projected = jnp.einsum("tc,jcw->tjw", gathered, qkv_weight, preferred_element_type=jnp.float32)
     queries = projected[:, 0]
     key_new = projected[:, 1]
     value_new = projected[:, 2]
@@ -336,7 +353,8 @@
     )
 
     state = new_attention(meta, queries, partner_new[0], partner_new[1], state)
-    attended = cached_attention(meta, queries, received, *state)
+    state = cached_attention(meta, queries, received_lo, *state, 0, False)
+    attended = cached_attention(meta, queries, received_hi, *state, low_levels, True)
     return (attended, updated_cache)
 
 

time: 334 us -> 356 us (1.066)
  the two profiles are of different devices: /device:TPU:110 before, /device:TPU:126 now
where the time goes in v4:
time: 356 us; the launch traced here: 354 us
  Pallas kernels  115 us (32%)
  waiting for transfers between devices  91.6 us (26%)
  local copies, waits for them, and re-layouts  46.3 us (13%)
  other arithmetic  29.6 us (8%)
  starting transfers between devices  28.1 us (8%)
  matrix products  17.8 us (5%)
  between operations  14.4 us (4%)
  blocking collectives  11.6 us (3%)
    pallas_call x2, Pallas kernels, cached_attention(): pl.pallas_call(functools.partial(cached_kernel, groups=groups, per_half=p...  74.6 us
    ppermute x1, waiting for transfers between devices, body(): partner_new = lax.ppermute(fresh_kv, 'bp', [(0, 1), (1, 0)])  67.4 us
    pallas_call x2, Pallas kernels, new_attention(): pl.pallas_call(functools.partial(new_kernel, partner=partner), out_shape=...  40 us
    all_gather x1, waiting for transfers between devices, body(): gathered = lax.all_gather(states, 'head', axis=1, tiled=True)  24.2 us
    dot_general x1, matrix products, body(): jnp.einsum('tc,jcw->tjw', gathered, qkv_weight, preferred_element_type=jn...  17.8 us
    all_to_all x2, starting transfers between devices, cached_part(): lax.all_to_all(outgoing, ('bx', 'bp'), split_axis=0, concat_axis=0, tiled...  14.6 us
    all_to_all x1, starting transfers between devices, body(): lax.all_to_all(picked, 'bx', split_axis=0, concat_axis=0, tiled=True)  12.6 us
    psum x1, blocking collectives, body(): lax.psum((jnp.sum(queries * queries, axis=1), jnp.sum(key_new * key_new,...  11.6 us
  transfers between devices with their start and end apart: 5, of which 2 were waited for; matrix products, arithmetic and copies ran while one was open for 23% of the time, Pallas kernels for 32%

profile of v4, /device:TPU:126, one launch (start us, length us, event | category | flops | bytes accessed | tf_op | source)
XLA Modules:
  0.0 353.9 jit_solution(18401342563801720286)
XLA Ops:
  7.2 5.5 %copy.28 = bf16[2,40,64,512]{3,2,1,0:T(8,128)(2,1)} copy(bf16[2,40,64,512]{3,2,1,0:T(8,128)(2,1)} %param.11) | data formatting | bytes 10485760
  15.0 5.2 %gather_fusion.3 = bf16[64,64,512]{2,1,0:T(8,128)(2,1)} fusion(bf16[80,64,512]{2,1,0:T(8,128)(2,1)} %bitcast.47, s32[1024]{0:T(1024)S(1)} %pad_clamp_fusion.2), kind=kCustom, calls=%fused_computation.3 | custom fusion | bytes 8388864 | tf_op jit(solution)/shard_map/jit(_take)/gather | solution.py:281
  20.3 7.0 %all-to-all-start.1 = ((bf16[16,2,2,64,512]{4,3,2,1,0:T(8,128)(2,1)}), bf16[16,2,2,64,512]{4,3,2,1,0:T(8,128)(2,1)}, u32[]{:S(2)}, u32[]{:S(2)}) async-start(bf16[16,2,2,64,512]{4,3,2,1,0:T(8,128)(2,1)} %bitcast.56), calls=%async_computation.1 | async-start | bytes 8388608 | tf_op jit(solution)/shard_map/all_to_all | solution.py:284
  30.3 5.3 %gather_fusion.2 = bf16[64,64,512]{2,1,0:T(8,128)(2,1)} fusion(bf16[80,64,512]{2,1,0:T(8,128)(2,1)} %bitcast.48, s32[1024]{0:T(1024)S(1)} %pad_clamp_fusion.3), kind=kCustom, calls=%fused_computation.2 | custom fusion | bytes 8388864 | tf_op jit(solution)/shard_map/jit(_take)/gather | solution.py:281
  35.6 1.9 multiply_cosine_fusion
  37.5 24.2 %all-gather.2.cloned.1.call-done = bf16[1024,4096]{1,0:T(8,128)(2,1)} async-done(((bf16[1024,512]{1,0:T(8,128)(2,1)}), bf16[1024,4096]{1,0:T(8,128)(2,1)}) %all-gather.2.cloned.1.call-update) | async-done | bytes 8388624 | tf_op jit(solution)/shard_map/all_gather | solution.py:289
  61.7 17.8 %fusion = f32[1024,3,512]{0,2,1:T(8,128)S(1)} fusion(bf16[3,4096,512]{2,1,0:T(8,128)(2,1)} %param.9, bf16[1024,4096]{1,0:T(8,128)(2,1)} %all-gather.2.cloned.1.call-done), kind=kOutput, calls=%fused_computation.8 | convolution fusion | flops 12884901888 | bytes 27262976 | tf_op jit(solution)/shard_map/tc,jcw->tjw/dot_general | solution.py:290
  79.5 3.1 multiply_reduce_fusion
  83.5 11.6 %all-reduce = (f32[1024]{0:T(1024)S(1)}, f32[1024]{0:T(1024)S(1)}) all-reduce(f32[1024]{0:T(1024)S(1)} %get-tuple-element.21, f32[1024]{0:T(1024)S(1)} %get-tuple-element.20), channel_id=1, replica_groups=mesh['head'=8,'bx'=8,'bp'=2] {'head'}, use_global_device_ids=true, to_apply=%region_1.2 | all-reduce | flops 2048 | bytes 16384 | tf_op jit(solution)/shard_map/psum | solution.py:294
  95.1 7.5 %all-to-all-start = ((bf16[16,2,2,64,512]{4,3,2,1,0:T(8,128)(2,1)}), bf16[16,2,2,64,512]{4,3,2,1,0:T(8,128)(2,1)}, u32[]{:S(2)}, u32[]{:S(2)}) async-start(bf16[16,2,2,64,512]{4,3,2,1,0:T(8,128)(2,1)} %bitcast.55), calls=%async_computation | async-start | bytes 8388608 | tf_op jit(solution)/shard_map/all_to_all | solution.py:284
  105.0 3.3 copy.16
  108.2 4.1 %multiply_multiply_fusion = f32[1024,4,128]{2,1,0:T(4,128)S(1)} fusion(f32[1024,4,128]{2,1,0:T(4,128)} %copy.16, f32[4,128]{1,0:T(4,128)S(1)} %bitcast.69, f32[1024]{0:T(1024)S(1)} %get-tuple-element.42), kind=kLoop, calls=%fused_computation.15 | loop fusion | flops 1048576 | bytes 4200448 | tf_op jit(solution)/shard_map/mul | solution.py:299
  124.3 2.9 copy.15
  127.2 67.4 %collective-permute-done = bf16[2,1024,512]{2,1,0:T(8,128)(2,1)} collective-permute-done((bf16[2,1024,512]{2,1,0:T(8,128)(2,1)}, bf16[2,1024,512]{2,1,0:T(8,128)(2,1)}, u32[]{:S(2)}, u32[]{:S(2)}) %collective-permute-start) | collective-permute-done | bytes 2097184 | tf_op jit(solution)/shard_map/ppermute | solution.py:319
  194.6 4.2 %maximum_select_fusion = bf16[2,2048,512]{2,1,0:T(8,128)(2,1)} fusion(bf16[2,1024,512]{2,1,0:T(8,128)(2,1)} %collective-permute-done, bf16[1,1024,512]{2,1,0:T(8,128)(2,1)S(1)} %bitcast.60, bf16[1,1024,512]{2,1,0:T(8,128)(2,1)S(1)} %convert_element_type.32, pred[]{:T(512)S(6)} %eq.10), kind=kLoop, calls=%fused_computation.10 | loop fusion | flops 27262976 | bytes 8388609 | tf_op jit(solution)/shard_map/jit(_where)/select_n | solution.py:324
  198.8 4.2 %gather_fusion.6 = bf16[32,64,512]{2,1,0:T(8,128)(2,1)} fusion(bf16[64,64,512]{2,1,0:T(8,128)(2,1)} %bitcast.58, s32[1024]{0:T(1024)S(1)} %pad_clamp_fusion), kind=kCustom, calls=%fused_computation.6 | custom fusion | bytes 4194432 | tf_op jit(solution)/shard_map/jit(_take)/gather | solution.py:339
  203.0 12.6 %all-to-all-start.2 = ((bf16[8,2,2,64,512]{4,3,2,1,0:T(8,128)(2,1)}), bf16[8,2,2,64,512]{4,3,2,1,0:T(8,128)(2,1)S(1)}, u32[]{:S(2)}, u32[]{:S(2)}) async-start(bf16[8,2,2,64,512]{4,3,2,1,0:T(8,128)(2,1)} %bitcast.65), calls=%async_computation.2 | async-start | bytes 4194304 | tf_op jit(solution)/shard_map/all_to_all | solution.py:342
  215.6 4.2 %multiply_multiply_fusion.1 = f32[1024,4,128]{2,1,0:T(4,128)S(1)} fusion(f32[1024,4,128]{2,1,0:T(4,128)} %copy.15, f32[4,128]{1,0:T(4,128)S(1)} %bitcast.68, f32[1024]{0:T(1024)S(1)} %get-tuple-element.43), kind=kLoop, calls=%fused_computation.19 | loop fusion | flops 1048576 | bytes 4200448 | tf_op jit(solution)/shard_map/mul | solution.py:298
  224.1 18.4 %shard_map.95 = (f32[1024,512]{1,0:T(8,128)}, f32[1024,512]{1,0:T(8,128)}, f32[1024,512]{1,0:T(8,128)}) custom-call(s32[4]{0:T(128)} %pad_add_fusion.meta_ref, bf16[1024,512]{1,0:T(8,128)(2,1)} %bitcast.51, bf16[1024,512]{1,0:T(8,128)(2,1)} %bitcast.67, bf16[1024,512]{1,0:T(8,128)(2,1)} %bitcast.61), custom_call_target="tpu_custom_call" | custom-call | flops 1610612736 | bytes 15728640 | tf_op jit(solution)/shard_map/pallas_call | solution.py:160
  242.5 3.0 slice_bitcast_fusion
  245.6 21.6 %shard_map.96 = (f32[1024,512]{1,0:T(8,128)}, f32[1024,512]{1,0:T(8,128)}, f32[1024,512]{1,0:T(8,128)}) custom-call(s32[4]{0:T(128)} %pad_add_fusion.meta_ref, bf16[1024,512]{1,0:T(8,128)(2,1)} %bitcast.52, bf16[1024,512]{1,0:T(8,128)(2,1)} %get-tuple-element.35.k_ref, bf16[1024,512]{1,0:T(8,128)(2,1)} %get-tuple-element.34.v_ref, ...), custom_call_target="tpu_custom_call" | custom-call | flops 1610612736 | bytes 15728640 | tf_op jit(solution)/shard_map/pallas_call | solution.py:160
  267.1 37.6 %shard_map.97 = (f32[1024,512]{1,0:T(8,128)}, f32[1024,512]{1,0:T(8,128)}, f32[1024,512]{1,0:T(8,128)}) custom-call(s32[4]{0:T(128)} %pad_add_fusion.meta_ref, bf16[1024,512]{1,0:T(8,128)(2,1)} %bitcast.53, bf16[16,2,2,64,512]{4,3,2,1,0:T(8,128)(2,1)} %all-to-all-done.1.k_ref.v_ref, bf16[16,2,2,64,512]{4,3,2,1,0:T(8,128)(2,1)} %all-to-all-done.1.k_ref.v_ref, ...), custom_call_target="tpu_custom_call" | custom-call | flops 2147483648 | bytes 16777216 | tf_op jit(solution)/shard_map/pallas_call | solution.py:215
  304.7 37.1 %shard_map.98 = bf16[1024,512]{1,0:T(8,128)(2,1)} custom-call(s32[4]{0:T(128)} %pad_add_fusion.meta_ref, bf16[1024,512]{1,0:T(8,128)(2,1)} %bitcast.54, bf16[16,2,2,64,512]{4,3,2,1,0:T(8,128)(2,1)} %all-to-all-done.k_ref.v_ref, bf16[16,2,2,64,512]{4,3,2,1,0:T(8,128)(2,1)} %all-to-all-done.k_ref.v_ref, f32[1024,512]{1,0:T(8,128)} %get-tuple-element.17.acc_in, ...), custom_call_target="tpu_custom_call" | custom-call | flops 2147483648 | bytes 16777216 | tf_op jit(solution)/shard_map/pallas_call | solution.py:215
  341.8 5.3 %scatter_fusion = bf16[80,64,512]{2,1,0:T(8,128)(2,1)} fusion(bf16[80,64,512]{2,1,0:T(8,128)(2,1)} %bitcast.49, s32[32]{0:T(128)S(1)} %fusion.31, bf16[32,64,512]{2,1,0:T(8,128)(2,1)S(1)} %bitcast.63), kind=kCustom, calls=%fused_computation.7 | custom fusion | bytes 6291584 | tf_op jit(solution)/shard_map/scatter | solution.py:351
  (90 shorter events, 24.6 us)
Async XLA Ops:
  7.2 5.6 %copy-start.1 = (s32[8,64]{1,0:T(8,128)S(1)}, s32[8,64]{1,0:T(8,128)}, u32[]{:S(2)}) copy-start(s32[8,64]{1,0:T(8,128)} %param.13) | copy-start | bytes 6148
  7.2 54.5 %all-gather.2.cloned.1.call-start = ((), (), s32[]{:S(2)}) async-start(), calls=%async_computation.3 | async-start | bytes 9437184 | tf_op jit(solution)/shard_map/all_gather | solution.py:289
  20.3 7.0 %copy-start.10 = (s32[8]{0:T(128)S(1)}, s32[8]{0:T(128)}, u32[]{:S(2)}) copy-start(s32[8]{0:T(128)} %param.12) | copy-start | bytes 100
  20.3 7.7 %copy-start.2 = (s32[8,32]{1,0:T(8,128)S(1)}, s32[8,32]{1,0:T(8,128)}, u32[]{:S(2)}) copy-start(s32[8,32]{1,0:T(8,128)} %param.14) | copy-start | bytes 3076
  20.3 9.3 %copy-start.9 = (bf16[2,512]{1,0:T(2,128)(2,1)S(1)}, bf16[2,512]{1,0:T(2,128)(2,1)}, u32[]{:S(2)}) copy-start(bf16[2,512]{1,0:T(2,128)(2,1)} %param.10) | copy-start | bytes 6148
  20.3 74.8 %all-to-all-start.1 = ((bf16[16,2,2,64,512]{4,3,2,1,0:T(8,128)(2,1)}), bf16[16,2,2,64,512]{4,3,2,1,0:T(8,128)(2,1)}, u32[]{:S(2)}, u32[]{:S(2)}) async-start(bf16[16,2,2,64,512]{4,3,2,1,0:T(8,128)(2,1)} %bitcast.56), calls=%async_computation.1 | async-start | bytes 8388608 | tf_op jit(solution)/shard_map/all_to_all | solution.py:284
  37.5 74.8 %copy-start.4 = (f32[1024,64]{1,0:T(8,128)}, f32[1024,64]{1,0:T(8,128)S(1)}, u32[]{:S(2)}) copy-start(f32[1024,64]{1,0:T(8,128)S(1)} %get-tuple-element.38) | copy-start | bytes 786436
  37.5 74.8 %copy-start.6 = (f32[1024,64]{1,0:T(8,128)}, f32[1024,64]{1,0:T(8,128)S(1)}, u32[]{:S(2)}) copy-start(f32[1024,64]{1,0:T(8,128)S(1)} %get-tuple-element.39) | copy-start | bytes 786436
  79.5 4.0 %copy-start.8 = (f32[1024,3,512]{0,2,1:T(8,128)}, f32[1024,3,512]{0,2,1:T(8,128)S(1)}, u32[]{:S(2)}) copy-start(f32[1024,3,512]{0,2,1:T(8,128)S(1)} %fusion) | copy-start | bytes 18874372
  95.1 107.9 %all-to-all-start = ((bf16[16,2,2,64,512]{4,3,2,1,0:T(8,128)(2,1)}), bf16[16,2,2,64,512]{4,3,2,1,0:T(8,128)(2,1)}, u32[]{:S(2)}, u32[]{:S(2)}) async-start(bf16[16,2,2,64,512]{4,3,2,1,0:T(8,128)(2,1)} %bitcast.55), calls=%async_computation | async-start | bytes 8388608 | tf_op jit(solution)/shard_map/all_to_all | solution.py:284
  105.0 89.7 %copy-start.3 = (bf16[1024,1,512]{2,0,1:T(8,128)(2,1)}, bf16[1024,1,512]{2,0,1:T(8,128)(2,1)S(1)}, u32[]{:S(2)}) copy-start(bf16[1024,1,512]{2,0,1:T(8,128)(2,1)S(1)} %copy.19) | copy-start | bytes 3145732
  116.0 3.1 copy-start
  117.6 77.1 %collective-permute-start = (bf16[2,1024,512]{2,1,0:T(8,128)(2,1)}, bf16[2,1024,512]{2,1,0:T(8,128)(2,1)}, u32[]{:S(2)}, u32[]{:S(2)}) collective-permute-start(bf16[2,1024,512]{2,1,0:T(8,128)(2,1)} %pad_maximum_fusion), channel_id=1, source_target_pairs={{0,1},{1,0},{2,3},{3,2},{4,5},{5,4},{6,7},{7,6},{8,9},{9,8},{10,11... | collective-permute-start | bytes 6291464 | tf_op jit(solution)/shard_map/ppermute | solution.py:319
  203.0 138.8 %all-to-all-start.2 = ((bf16[8,2,2,64,512]{4,3,2,1,0:T(8,128)(2,1)}), bf16[8,2,2,64,512]{4,3,2,1,0:T(8,128)(2,1)S(1)}, u32[]{:S(2)}, u32[]{:S(2)}) async-start(bf16[8,2,2,64,512]{4,3,2,1,0:T(8,128)(2,1)} %bitcast.65), calls=%async_computation.2 | async-start | bytes 4194304 | tf_op jit(solution)/shard_map/all_to_all | solution.py:342
  215.6 4.2 %copy-start.5 = (f32[1024,64]{1,0:T(8,128)S(1)}, f32[1024,64]{1,0:T(8,128)}, u32[]{:S(2)}) copy-start(f32[1024,64]{1,0:T(8,128)} %copy-done.4) | copy-start | bytes 786436
  215.6 4.2 %copy-start.7 = (f32[1024,64]{1,0:T(8,128)S(1)}, f32[1024,64]{1,0:T(8,128)}, u32[]{:S(2)}) copy-start(f32[1024,64]{1,0:T(8,128)} %copy-done.6) | copy-start | bytes 786436
Sparse Core Ops, SparseCore 0:
  12.9 48.8 all-gather.1

commit v5 on v3

--- a/solution.py
+++ b/solution.py
@@ -299,16 +299,12 @@
     fresh_kv = jnp.stack([key_new, value_new])
     meta = jnp.stack([member, cached_len[request], first_dev[request], 0]).astype(jnp.int32)
 
-    partner_new = lax.ppermute(fresh_kv, "bp", [(0, 1), (1, 0)])
+    collected = lax.all_gather(fresh_kv, "bp", axis=1, tiled=True)
     state = new_attention(meta, queries, fresh_kv[0], fresh_kv[1])
+    partner_new = lax.dynamic_slice_in_dim(collected, (1 - member) * tok_rows, tok_rows, axis=1)
 
     blocks_dev = tok_rows // block_len
     chunk_blocks = blocks_dev // 2
-    collected = jnp.where(
-        member == 0,
-        jnp.concatenate([fresh_kv, partner_new], axis=1),
-        jnp.concatenate([partner_new, fresh_kv], axis=1),
-    )
     new_blocks = 2 * blocks_dev
     collected_flat = collected.reshape(2 * new_blocks, block_len, local_width)
     chunk_place = jnp.array([0, 2, 3, 1], dtype=jnp.int32)

time: 334 us -> 349 us (1.045)
  the two profiles are of different devices: /device:TPU:110 before, /device:TPU:102 now
where the time goes in v5:
time: 349 us; the launch traced here: 347 us
  Pallas kernels  110 us (32%)
  waiting for transfers between devices  84.4 us (24%)
  local copies, waits for them, and re-layouts  45.9 us (13%)
  starting transfers between devices  32.9 us (9%)
  other arithmetic  27.7 us (8%)
  matrix products  17.8 us (5%)
  blocking collectives  14.4 us (4%)
  between operations  14.4 us (4%)
    pallas_call x1, Pallas kernels, cached_attention(): pl.pallas_call(functools.partial(cached_kernel, groups=groups, per_half=p...  69.8 us
    all_gather x1, waiting for transfers between devices, body(): collected = lax.all_gather(fresh_kv, 'bp', axis=1, tiled=True)  54.7 us
    pallas_call x2, Pallas kernels, new_attention(): pl.pallas_call(functools.partial(new_kernel, partner=partner), out_shape=...  40 us
    all_gather x1, waiting for transfers between devices, body(): lax.all_gather(states, 'head', axis=1, tiled=True)  29.6 us
    all_to_all x1, starting transfers between devices, body(): lax.all_to_all(picked, 'bx', split_axis=0, concat_axis=0, tiled=True)  25.8 us
    dot_general x1, matrix products, body(): jnp.einsum('tc,jcw->tjw', lax.all_gather(states, 'head', axis=1, tiled=Tr...  17.8 us
    psum x1, blocking collectives, body(): lax.psum((jnp.sum(queries * queries, axis=1), jnp.sum(key_new * key_new,...  14.4 us
    unnamed x24, local copies, waits for them, and re-layouts  12 us
  transfers between devices with their start and end apart: 4, of which 2 were waited for; matrix products, arithmetic and copies ran while one was open for 22% of the time, Pallas kernels for 32%

profile of v5, /device:TPU:102, one launch (start us, length us, event | category | flops | bytes accessed | tf_op | source)
XLA Modules:
  0.0 347.3 jit_solution(1161876394603291985)
XLA Ops:
  7.2 5.5 %copy.28 = bf16[2,40,64,512]{3,2,1,0:T(8,128)(2,1)} copy(bf16[2,40,64,512]{3,2,1,0:T(8,128)(2,1)} %param.11) | data formatting | bytes 10485760
  15.0 9.0 %gather_fusion.2 = bf16[128,64,512]{2,1,0:T(8,128)(2,1)} fusion(bf16[80,64,512]{2,1,0:T(8,128)(2,1)} %bitcast.46, s32[1024]{0:T(1024)S(1)} %pad_clamp_fusion.2), kind=kCustom, calls=%fused_computation.2 | custom fusion | bytes 16777728 | tf_op jit(solution)/shard_map/jit(_take)/gather | solution.py:261
  24.0 7.0 %all-to-all-start = ((bf16[16,2,4,64,512]{4,3,2,1,0:T(8,128)(2,1)}), bf16[16,2,4,64,512]{4,3,2,1,0:T(8,128)(2,1)}, u32[]{:S(2)}, u32[]{:S(2)}) async-start(bf16[16,2,4,64,512]{4,3,2,1,0:T(8,128)(2,1)} %bitcast.49), calls=%async_computation | async-start | bytes 16777216 | tf_op jit(solution)/shard_map/all_to_all | solution.py:264
  32.2 1.9 multiply_cosine_fusion
  34.2 29.6 %all-gather.3.cloned.1.call-done = bf16[1024,4096]{1,0:T(8,128)(2,1)} async-done(((bf16[1024,512]{1,0:T(8,128)(2,1)}), bf16[1024,4096]{1,0:T(8,128)(2,1)}) %all-gather.3.cloned.1.call-update) | async-done | bytes 8388624 | tf_op jit(solution)/shard_map/all_gather | solution.py:270
  63.8 17.8 %fusion = f32[1024,3,512]{0,2,1:T(8,128)S(1)} fusion(bf16[3,4096,512]{2,1,0:T(8,128)(2,1)} %param.9, bf16[1024,4096]{1,0:T(8,128)(2,1)} %all-gather.3.cloned.1.call-done), kind=kOutput, calls=%fused_computation.7 | convolution fusion | flops 12884901888 | bytes 27262976 | tf_op jit(solution)/shard_map/tc,jcw->tjw/dot_general | solution.py:268
  81.6 2.7 copy-done.7
  85.7 4.2 %multiply_reduce_fusion = (f32[1024]{0:T(1024)S(1)}, f32[1024]{0:T(1024)S(1)}, f32[1024,1,512]{0,2,1:T(8,128)}, f32[1024,1,512]{0,2,1:T(8,128)S(1)}) fusion(f32[1024,3,512]{0,2,1:T(8,128)} %copy-done.7), kind=kLoop, calls=%fused_computation.14 | loop fusion | flops 2095104 | bytes 8396800 | tf_op jit(solution)/shard_map/reduce_sum | solution.py:278
  89.9 2.9 copy.16
  92.9 14.4 %all-reduce = (f32[1024]{0:T(1024)S(1)}, f32[1024]{0:T(1024)S(1)}) all-reduce(f32[1024]{0:T(1024)S(1)} %get-tuple-element.15, f32[1024]{0:T(1024)S(1)} %get-tuple-element.14), channel_id=1, replica_groups=mesh['head'=8,'bx'=8,'bp'=2] {'head'}, use_global_device_ids=true, to_apply=%region_1.2 | all-reduce | flops 2048 | bytes 16384 | tf_op jit(solution)/shard_map/psum | solution.py:277
  107.3 4.1 %multiply_multiply_fusion = f32[1024,4,128]{2,1,0:T(4,128)S(1)} fusion(f32[1024,4,128]{2,1,0:T(4,128)} %copy.16, f32[4,128]{1,0:T(4,128)S(1)} %bitcast.63, f32[1024]{0:T(1024)S(1)} %get-tuple-element.36), kind=kLoop, calls=%fused_computation.13 | loop fusion | flops 1048576 | bytes 4200448 | tf_op jit(solution)/shard_map/mul | solution.py:282
  115.7 3.1 pad_maximum_fusion
  123.3 54.7 %all-gather.5.cloned.1.call-done = bf16[2,2048,512]{2,1,0:T(8,128)(2,1)} async-done(((bf16[2,1024,512]{2,1,0:T(8,128)(2,1)}), bf16[2,2048,512]{2,1,0:T(8,128)(2,1)}) %all-gather.5.cloned.1.call-update) | async-done | bytes 4194320 | tf_op jit(solution)/shard_map/all_gather | solution.py:302
  178.1 4.2 %gather_fusion.5 = bf16[32,64,512]{2,1,0:T(8,128)(2,1)} fusion(bf16[64,64,512]{2,1,0:T(8,128)(2,1)} %bitcast.58, s32[1024]{0:T(1024)S(1)} %pad_clamp_fusion), kind=kCustom, calls=%fused_computation.5 | custom fusion | bytes 4194432 | tf_op jit(solution)/shard_map/jit(_take)/gather | solution.py:318
  182.3 25.8 %all-to-all-start.1 = ((bf16[8,2,2,64,512]{4,3,2,1,0:T(8,128)(2,1)}), bf16[8,2,2,64,512]{4,3,2,1,0:T(8,128)(2,1)}, u32[]{:S(2)}, u32[]{:S(2)}) async-start(bf16[8,2,2,64,512]{4,3,2,1,0:T(8,128)(2,1)} %bitcast.56), calls=%async_computation.1 | async-start | bytes 4194304 | tf_op jit(solution)/shard_map/all_to_all | solution.py:321
  208.1 1.7 pad_add_fusion.meta_ref
  211.0 1.8 copy.15
  212.8 4.2 %multiply_multiply_fusion.1 = f32[1024,4,128]{2,1,0:T(4,128)S(1)} fusion(f32[1024,4,128]{2,1,0:T(4,128)} %copy.15, f32[4,128]{1,0:T(4,128)S(1)} %bitcast.62, f32[1024]{0:T(1024)S(1)} %get-tuple-element.37), kind=kLoop, calls=%fused_computation.17 | loop fusion | flops 1048576 | bytes 4200448 | tf_op jit(solution)/shard_map/mul | solution.py:281
  217.0 1.7 subtract_convert_fusion
  221.4 18.5 %shard_map.95 = (f32[1024,512]{1,0:T(8,128)}, f32[1024,512]{1,0:T(8,128)}, f32[1024,512]{1,0:T(8,128)}) custom-call(s32[4]{0:T(128)} %pad_add_fusion.meta_ref, bf16[1024,512]{1,0:T(8,128)(2,1)} %bitcast.50, bf16[1024,512]{1,0:T(8,128)(2,1)} %bitcast.61, bf16[1024,512]{1,0:T(8,128)(2,1)} %bitcast.60), custom_call_target="tpu_custom_call" | custom-call | flops 1610612736 | bytes 15728640 | tf_op jit(solution)/shard_map/pallas_call | solution.py:151
  239.8 3.0 dynamic-slice_bitcast_fusion
  242.8 21.6 %shard_map.96 = (f32[1024,512]{1,0:T(8,128)}, f32[1024,512]{1,0:T(8,128)}, f32[1024,512]{1,0:T(8,128)}) custom-call(s32[4]{0:T(128)} %pad_add_fusion.meta_ref, bf16[1024,512]{1,0:T(8,128)(2,1)} %bitcast.51, bf16[1024,512]{1,0:T(8,128)(2,1)} %get-tuple-element.25.k_ref, bf16[1024,512]{1,0:T(8,128)(2,1)} %get-tuple-element.24.v_ref, ...), custom_call_target="tpu_custom_call" | custom-call | flops 1610612736 | bytes 15728640 | tf_op jit(solution)/shard_map/pallas_call | solution.py:151
  264.4 69.8 %shard_map.97 = bf16[1024,512]{1,0:T(8,128)(2,1)} custom-call(s32[4]{0:T(128)} %pad_add_fusion.meta_ref, bf16[1024,512]{1,0:T(8,128)(2,1)} %bitcast.52, bf16[16,2,4,64,512]{4,3,2,1,0:T(8,128)(2,1)} %all-to-all-done.k_ref.v_ref, bf16[16,2,4,64,512]{4,3,2,1,0:T(8,128)(2,1)} %all-to-all-done.k_ref.v_ref, f32[1024,512]{1,0:T(8,128)} %get-tuple-element.11.acc_in, ...), custom_call_target="tpu_custom_call" | custom-call | flops 4294967296 | bytes 12582912 | tf_op jit(solution)/shard_map/pallas_call | solution.py:199
  334.2 6.2 %scatter_fusion = bf16[80,64,512]{2,1,0:T(8,128)(2,1)} fusion(bf16[80,64,512]{2,1,0:T(8,128)(2,1)} %bitcast.47, s32[32]{0:T(128)S(1)} %fusion.31, bf16[32,64,512]{2,1,0:T(8,128)(2,1)} %bitcast.18), kind=kCustom, calls=%fused_computation.6 | custom fusion | bytes 6291584 | tf_op jit(solution)/shard_map/scatter | solution.py:330
  (81 shorter events, 17.6 us)
Async XLA Ops:
  7.2 5.6 %copy-start.1 = (s32[8,64]{1,0:T(8,128)S(1)}, s32[8,64]{1,0:T(8,128)}, u32[]{:S(2)}) copy-start(s32[8,64]{1,0:T(8,128)} %param.13) | copy-start | bytes 6148
  7.2 56.6 %all-gather.3.cloned.1.call-start = ((), (), s32[]{:S(2)}) async-start(), calls=%async_computation.2 | async-start | bytes 9437184 | tf_op jit(solution)/shard_map/all_gather | solution.py:270
  24.0 7.1 %copy-start.9 = (s32[8]{0:T(128)S(1)}, s32[8]{0:T(128)}, u32[]{:S(2)}) copy-start(s32[8]{0:T(128)} %param.12) | copy-start | bytes 100
  24.0 8.3 %copy-start.8 = (bf16[2,512]{1,0:T(2,128)(2,1)S(1)}, bf16[2,512]{1,0:T(2,128)(2,1)}, u32[]{:S(2)}) copy-start(bf16[2,512]{1,0:T(2,128)(2,1)} %param.10) | copy-start | bytes 6148
  24.0 158.3 %all-to-all-start = ((bf16[16,2,4,64,512]{4,3,2,1,0:T(8,128)(2,1)}), bf16[16,2,4,64,512]{4,3,2,1,0:T(8,128)(2,1)}, u32[]{:S(2)}, u32[]{:S(2)}) async-start(bf16[16,2,4,64,512]{4,3,2,1,0:T(8,128)(2,1)} %bitcast.49), calls=%async_computation | async-start | bytes 16777216 | tf_op jit(solution)/shard_map/all_to_all | solution.py:264
  31.0 147.1 %all-gather.5.cloned.1.call-start = ((), (), s32[]{:S(2)}) async-start(), calls=%async_computation.3 | async-start | bytes 6291456 | tf_op jit(solution)/shard_map/all_gather | solution.py:302
  34.1 77.2 %copy-start.3 = (f32[1024,64]{1,0:T(8,128)}, f32[1024,64]{1,0:T(8,128)S(1)}, u32[]{:S(2)}) copy-start(f32[1024,64]{1,0:T(8,128)S(1)} %get-tuple-element.30) | copy-start | bytes 786436
  34.1 77.2 %copy-start.5 = (f32[1024,64]{1,0:T(8,128)}, f32[1024,64]{1,0:T(8,128)S(1)}, u32[]{:S(2)}) copy-start(f32[1024,64]{1,0:T(8,128)S(1)} %get-tuple-element.31) | copy-start | bytes 786436
  81.6 2.7 copy-start.7
  118.8 0.7 copy-start.2
  118.8 2.4 copy-start
  182.3 151.9 %all-to-all-start.1 = ((bf16[8,2,2,64,512]{4,3,2,1,0:T(8,128)(2,1)}), bf16[8,2,2,64,512]{4,3,2,1,0:T(8,128)(2,1)}, u32[]{:S(2)}, u32[]{:S(2)}) async-start(bf16[8,2,2,64,512]{4,3,2,1,0:T(8,128)(2,1)} %bitcast.56), calls=%async_computation.1 | async-start | bytes 4194304 | tf_op jit(solution)/shard_map/all_to_all | solution.py:321
  212.8 4.2 %copy-start.4 = (f32[1024,64]{1,0:T(8,128)S(1)}, f32[1024,64]{1,0:T(8,128)}, u32[]{:S(2)}) copy-start(f32[1024,64]{1,0:T(8,128)} %copy-done.3) | copy-start | bytes 786436
  212.8 4.2 %copy-start.6 = (f32[1024,64]{1,0:T(8,128)S(1)}, f32[1024,64]{1,0:T(8,128)}, u32[]{:S(2)}) copy-start(f32[1024,64]{1,0:T(8,128)} %copy-done.5) | copy-start | bytes 786436
Sparse Core Ops, SparseCore 0:
  12.9 50.8 all-gather.2
  118.9 59.1 all-gather.4

commit v6 on v3

--- a/solution.py
+++ b/solution.py
@@ -15,6 +15,7 @@
 rope_base = 500000.0
 norm_eps = 1e-06
 score_scale = HS ** (-0.5)
+scale2 = score_scale * 1.4426950408889634
 
 
 def rotate(values, positions, head_size):
@@ -33,10 +34,10 @@
 
 def online_update(s, v, m_sc, l_sc, acc_sc):
     m_prev = m_sc[...]
-    m_cur = jnp.max(s, axis=1, keepdims=True) * score_scale
+    m_cur = jnp.max(s, axis=1, keepdims=True) * scale2
     m_next = jnp.maximum(m_prev, m_cur)
-    alpha = jnp.exp(m_prev - m_next)
-    p = jnp.exp(s * score_scale - m_next[:, :1])
+    alpha = jnp.exp2(m_prev - m_next)
+    p = jnp.exp2(s * scale2 - m_next[:, :1])
     l_sc[...] = alpha * l_sc[...] + jnp.sum(p, axis=1, keepdims=True)
     pv = jnp.dot(p.astype(jnp.bfloat16), v, preferred_element_type=jnp.float32)
     acc_sc[...] = acc_sc[...] * alpha + pv
@@ -93,14 +94,13 @@
 
 
 def cached_kernel(meta_ref, q_ref, k_ref, v_ref, acc_in, m_in, l_in, o_ref, m_sc, l_sc, acc_sc,
-                  *, groups, per_half, block_len):
+                  *, groups, block_len):
     c = pl.program_id(1)
-    half = pl.program_id(2)
     length = meta_ref[1]
     first = meta_ref[2]
-    tile = per_half * block_len
-
-    @pl.when((c == 0) & (half == 0))
+    tile = groups * block_len
+
+    @pl.when(c == 0)
     def _():
         m_sc[...] = m_in[...]
         l_sc[...] = l_in[...]
@@ -119,13 +119,13 @@
         v = v_ref[...].reshape(tile, HS)
         s = scores_of(q_ref[...], k)
         cols = lax.broadcasted_iota(jnp.int32, (1, tile), 1)
-        src = half * per_half + cols // block_len
+        src = cols // block_len
         block = (src - first + groups) % groups + groups * c
         visible = block * block_len + cols % block_len < length
         s = jnp.where(visible, s, -jnp.inf)
         online_update(s, v, m_sc, l_sc, acc_sc)
 
-    @pl.when((c == pl.num_programs(1) - 1) & (half == pl.num_programs(2) - 1))
+    @pl.when(c == pl.num_programs(1) - 1)
     def _():
         o_ref[...] = (acc_sc[...] / l_sc[...]).astype(o_ref.dtype)
 
@@ -177,51 +177,41 @@
     tok_rows, width = queries.shape
     heads = width // HS
     groups, _, per_dev, block_len, _ = received.shape
-    per_half = groups // 2
 
     def kv_map(index):
-        def index_map(h, c, half, meta):
+        def index_map(h, c, meta):
             last = (meta[1] + groups * block_len - 1) // (groups * block_len) - 1
-            skip = c > last
-            return (
-                jnp.where(skip, 1, half),
-                index,
-                jnp.where(skip, last, c),
-                0,
-                h,
-            )
+            return (0, index, jnp.minimum(c, last), 0, h)
 
         return index_map
 
-    kv_block = (per_half, None, None, block_len, HS)
-    state_spec = pl.BlockSpec((tok_rows, HS), lambda h, c, half, meta: (0, h))
+    kv_block = (groups, None, None, block_len, HS)
+    state_spec = pl.BlockSpec((tok_rows, HS), lambda h, c, meta: (0, h))
     keys_total = groups * per_dev * block_len
     return pl.pallas_call(
         functools.partial(
-            cached_kernel, groups=groups, per_half=per_half, block_len=block_len
+            cached_kernel, groups=groups, block_len=block_len
         ),
         out_shape=jax.ShapeDtypeStruct((tok_rows, width), jnp.bfloat16),
         grid_spec=pltpu.PrefetchScalarGridSpec(
             num_scalar_prefetch=1,
-            grid=(heads, per_dev, 2),
+            grid=(heads, per_dev),
             in_specs=[
-                pl.BlockSpec((tok_rows, HS), lambda h, c, half, meta: (0, h)),
+                pl.BlockSpec((tok_rows, HS), lambda h, c, meta: (0, h)),
                 pl.BlockSpec(kv_block, kv_map(0)),
                 pl.BlockSpec(kv_block, kv_map(1)),
                 state_spec,
                 state_spec,
                 state_spec,
             ],
-            out_specs=pl.BlockSpec((tok_rows, HS), lambda h, c, half, meta: (0, h)),
+            out_specs=pl.BlockSpec((tok_rows, HS), lambda h, c, meta: (0, h)),
             scratch_shapes=[
                 pltpu.VMEM((tok_rows, HS), jnp.float32),
                 pltpu.VMEM((tok_rows, HS), jnp.float32),
                 pltpu.VMEM((tok_rows, HS), jnp.float32),
             ],
         ),
-        compiler_params=pltpu.CompilerParams(
-            dimension_semantics=("arbitrary", "arbitrary", "arbitrary")
-        ),
+        compiler_params=pltpu.CompilerParams(dimension_semantics=("arbitrary", "arbitrary")),
         cost_estimate=pl.CostEstimate(
             flops=2 * 2 * tok_rows * keys_total * width // 2,
             transcendentals=tok_rows * keys_total * heads // 2,

time: 334 us -> 304 us (0.910)
  Pallas kernels: 110 us -> 79.5 us
    pallas_call x1, Pallas kernels: 70.1 us -> 39.6 us  [cached_attention(): pl.pallas_call(functools.partial(cached_kernel, groups=groups, block_len=...]
  transfers between devices with their start and end apart: 4 -> 4, of which waited for: 2 -> 2; matrix products, arithmetic and copies ran while one was open for 24% -> 27% of each run, Pallas kernels for 33% -> 26%
where the time goes in v6:
time: 304 us; the launch traced here: 302 us
  waiting for transfers between devices  81.9 us (27%)
  Pallas kernels  79.5 us (26%)
  local copies, waits for them, and re-layouts  43.4 us (14%)
  other arithmetic  32.6 us (11%)
  starting transfers between devices  20.5 us (7%)
  matrix products  17.8 us (6%)
  between operations  14.4 us (5%)
  blocking collectives  12.4 us (4%)
    ppermute x1, waiting for transfers between devices, body(): partner_new = lax.ppermute(fresh_kv, 'bp', [(0, 1), (1, 0)])  56 us
    pallas_call x2, Pallas kernels, new_attention(): pl.pallas_call(functools.partial(new_kernel, partner=partner), out_shape=...  39.9 us
    pallas_call x1, Pallas kernels, cached_attention(): pl.pallas_call(functools.partial(cached_kernel, groups=groups, block_len=...  39.6 us
    all_gather x1, waiting for transfers between devices, body(): lax.all_gather(states, 'head', axis=1, tiled=True)  25.9 us
    dot_general x1, matrix products, body(): jnp.einsum('tc,jcw->tjw', lax.all_gather(states, 'head', axis=1, tiled=Tr...  17.8 us
    all_to_all x1, starting transfers between devices, body(): lax.all_to_all(picked, 'bx', split_axis=0, concat_axis=0, tiled=True)  12.7 us
    psum x1, blocking collectives, body(): lax.psum((jnp.sum(queries * queries, axis=1), jnp.sum(key_new * key_new,...  12.4 us
    unnamed x26, local copies, waits for them, and re-layouts  11.1 us
  transfers between devices with their start and end apart: 4, of which 2 were waited for; matrix products, arithmetic and copies ran while one was open for 27% of the time, Pallas kernels for 26%

profile of v6, /device:TPU:110, one launch (start us, length us, event | category | flops | bytes accessed | tf_op | source)
XLA Modules:
  0.0 302.4 jit_solution(1904619740706210775)
XLA Ops:
  7.2 5.5 %copy.28 = bf16[2,40,64,512]{3,2,1,0:T(8,128)(2,1)} copy(bf16[2,40,64,512]{3,2,1,0:T(8,128)(2,1)} %param.11) | data formatting | bytes 10485760
  15.0 9.0 %gather_fusion.2 = bf16[128,64,512]{2,1,0:T(8,128)(2,1)} fusion(bf16[80,64,512]{2,1,0:T(8,128)(2,1)} %bitcast.46, s32[1024]{0:T(1024)S(1)} %pad_clamp_fusion.2), kind=kCustom, calls=%fused_computation.2 | custom fusion | bytes 16777728 | tf_op jit(solution)/shard_map/jit(_take)/gather | solution.py:251
  24.0 7.0 %all-to-all-start = ((bf16[16,2,4,64,512]{4,3,2,1,0:T(8,128)(2,1)}), bf16[16,2,4,64,512]{4,3,2,1,0:T(8,128)(2,1)}, u32[]{:S(2)}, u32[]{:S(2)}) async-start(bf16[16,2,4,64,512]{4,3,2,1,0:T(8,128)(2,1)} %bitcast.49), calls=%async_computation | async-start | bytes 16777216 | tf_op jit(solution)/shard_map/all_to_all | solution.py:254
  33.3 3.1 %multiply_cosine_fusion = (f32[1024,64]{1,0:T(8,128)}, f32[1024,64]{1,0:T(8,128)}) fusion(f32[64]{0:T(128)S(1)} %multiply_power_fusion, f32[1024]{0:T(1024)S(1)} %fusion.15), kind=kLoop, calls=%fused_computation.26 | loop fusion | flops 65536 | bytes 528640 | tf_op jit(solution)/shard_map/cos | solution.py:25
  37.0 25.9 %all-gather.2.cloned.1.call-done = bf16[1024,4096]{1,0:T(8,128)(2,1)} async-done(((bf16[1024,512]{1,0:T(8,128)(2,1)}), bf16[1024,4096]{1,0:T(8,128)(2,1)}) %all-gather.2.cloned.1.call-update) | async-done | bytes 8388624 | tf_op jit(solution)/shard_map/all_gather | solution.py:260
  62.9 17.8 %fusion = f32[1024,3,512]{0,2,1:T(8,128)S(1)} fusion(bf16[3,4096,512]{2,1,0:T(8,128)(2,1)} %param.9, bf16[1024,4096]{1,0:T(8,128)(2,1)} %all-gather.2.cloned.1.call-done), kind=kOutput, calls=%fused_computation.7 | convolution fusion | flops 12884901888 | bytes 27262976 | tf_op jit(solution)/shard_map/tc,jcw->tjw/dot_general | solution.py:258
  80.7 2.6 copy-done.8
  84.0 4.6 %multiply_reduce_fusion = (f32[1024]{0:T(1024)S(1)}, f32[1024]{0:T(1024)S(1)}, f32[1024,1,512]{0,2,1:T(8,128)S(1)}, f32[1024,1,512]{0,2,1:T(8,128)}) fusion(f32[1024,3,512]{0,2,1:T(8,128)} %copy-done.8), kind=kLoop, calls=%fused_computation.15 | loop fusion | flops 2095104 | bytes 8396800 | tf_op jit(solution)/shard_map/reduce_sum | solution.py:268
  88.6 1.9 copy.16
  90.5 12.4 %all-reduce = (f32[1024]{0:T(1024)S(1)}, f32[1024]{0:T(1024)S(1)}) all-reduce(f32[1024]{0:T(1024)S(1)} %get-tuple-element.15, f32[1024]{0:T(1024)S(1)} %get-tuple-element.14), channel_id=1, replica_groups=mesh['head'=8,'bx'=8,'bp'=2] {'head'}, use_global_device_ids=true, to_apply=%region_1.2 | all-reduce | flops 2048 | bytes 16384 | tf_op jit(solution)/shard_map/psum | solution.py:267
  102.9 4.2 %multiply_multiply_fusion = f32[1024,4,128]{2,1,0:T(4,128)S(1)} fusion(f32[1024,4,128]{2,1,0:T(4,128)} %copy.16, f32[4,128]{1,0:T(4,128)S(1)} %bitcast.65, f32[1024]{0:T(1024)S(1)} %get-tuple-element.34), kind=kLoop, calls=%fused_computation.14 | loop fusion | flops 1048576 | bytes 4200448 | tf_op jit(solution)/shard_map/mul | solution.py:272
  115.9 2.0 pad_add_fusion.meta_ref
  119.0 2.9 copy.15
  121.9 56.0 %collective-permute-done = bf16[2,1024,512]{2,1,0:T(8,128)(2,1)} collective-permute-done((bf16[2,1024,512]{2,1,0:T(8,128)(2,1)}, bf16[2,1024,512]{2,1,0:T(8,128)(2,1)}, u32[]{:S(2)}, u32[]{:S(2)}) %collective-permute-start) | collective-permute-done | bytes 2097184 | tf_op jit(solution)/shard_map/ppermute | solution.py:292
  178.0 4.3 %maximum_select_fusion = bf16[2,2048,512]{2,1,0:T(8,128)(2,1)} fusion(bf16[2,1024,512]{2,1,0:T(8,128)(2,1)} %collective-permute-done, bf16[1,1024,512]{2,1,0:T(8,128)(2,1)S(1)} %bitcast.56, bf16[1,1024,512]{2,1,0:T(8,128)(2,1)S(1)} %convert_element_type.32, pred[]{:T(512)S(6)} %eq.10), kind=kLoop, calls=%fused_computation.9 | loop fusion | flops 27262976 | bytes 8388609 | tf_op jit(solution)/shard_map/jit(_where)/select_n | solution.py:297
  182.3 4.2 %gather_fusion.5 = bf16[32,64,512]{2,1,0:T(8,128)(2,1)} fusion(bf16[64,64,512]{2,1,0:T(8,128)(2,1)} %bitcast.54, s32[1024]{0:T(1024)S(1)} %pad_clamp_fusion), kind=kCustom, calls=%fused_computation.5 | custom fusion | bytes 4194432 | tf_op jit(solution)/shard_map/jit(_take)/gather | solution.py:312
  186.5 12.7 %all-to-all-start.1 = ((bf16[8,2,2,64,512]{4,3,2,1,0:T(8,128)(2,1)}), bf16[8,2,2,64,512]{4,3,2,1,0:T(8,128)(2,1)S(1)}, u32[]{:S(2)}, u32[]{:S(2)}) async-start(bf16[8,2,2,64,512]{4,3,2,1,0:T(8,128)(2,1)} %bitcast.61), calls=%async_computation.1 | async-start | bytes 4194304 | tf_op jit(solution)/shard_map/all_to_all | solution.py:315
  199.1 4.2 %multiply_multiply_fusion.1 = f32[1024,4,128]{2,1,0:T(4,128)S(1)} fusion(f32[1024,4,128]{2,1,0:T(4,128)} %copy.15, f32[4,128]{1,0:T(4,128)S(1)} %bitcast.64, f32[1024]{0:T(1024)S(1)} %get-tuple-element.35), kind=kLoop, calls=%fused_computation.18 | loop fusion | flops 1048576 | bytes 4200448 | tf_op jit(solution)/shard_map/mul | solution.py:271
  203.3 1.7 subtract_convert_fusion
  207.7 18.3 %shard_map.95 = (f32[1024,512]{1,0:T(8,128)}, f32[1024,512]{1,0:T(8,128)}, f32[1024,512]{1,0:T(8,128)}) custom-call(s32[4]{0:T(128)} %pad_add_fusion.meta_ref, bf16[1024,512]{1,0:T(8,128)(2,1)} %bitcast.50, bf16[1024,512]{1,0:T(8,128)(2,1)} %bitcast.63, bf16[1024,512]{1,0:T(8,128)(2,1)} %bitcast.57), custom_call_target="tpu_custom_call" | custom-call | flops 1610612736 | bytes 15728640 | tf_op jit(solution)/shard_map/pallas_call | solution.py:151
  226.1 3.0 slice_bitcast_fusion
  229.0 21.6 %shard_map.96 = (f32[1024,512]{1,0:T(8,128)}, f32[1024,512]{1,0:T(8,128)}, f32[1024,512]{1,0:T(8,128)}) custom-call(s32[4]{0:T(128)} %pad_add_fusion.meta_ref, bf16[1024,512]{1,0:T(8,128)(2,1)} %bitcast.51, bf16[1024,512]{1,0:T(8,128)(2,1)} %get-tuple-element.29.k_ref, bf16[1024,512]{1,0:T(8,128)(2,1)} %get-tuple-element.28.v_ref, ...), custom_call_target="tpu_custom_call" | custom-call | flops 1610612736 | bytes 15728640 | tf_op jit(solution)/shard_map/pallas_call | solution.py:151
  250.6 39.6 %shard_map.97 = bf16[1024,512]{1,0:T(8,128)(2,1)} custom-call(s32[4]{0:T(128)} %pad_add_fusion.meta_ref, bf16[1024,512]{1,0:T(8,128)(2,1)} %bitcast.52, bf16[16,2,4,64,512]{4,3,2,1,0:T(8,128)(2,1)} %all-to-all-done.k_ref.v_ref, bf16[16,2,4,64,512]{4,3,2,1,0:T(8,128)(2,1)} %all-to-all-done.k_ref.v_ref, f32[1024,512]{1,0:T(8,128)} %get-tuple-element.11.acc_in, ...), custom_call_target="tpu_custom_call" | custom-call | flops 4294967296 | bytes 12582912 | tf_op jit(solution)/shard_map/pallas_call | solution.py:191
  290.2 5.3 %scatter_fusion = bf16[80,64,512]{2,1,0:T(8,128)(2,1)} fusion(bf16[80,64,512]{2,1,0:T(8,128)(2,1)} %bitcast.47, s32[32]{0:T(128)S(1)} %fusion.31, bf16[32,64,512]{2,1,0:T(8,128)(2,1)S(1)} %bitcast.59), kind=kCustom, calls=%fused_computation.6 | custom fusion | bytes 6291584 | tf_op jit(solution)/shard_map/scatter | solution.py:324
  (83 shorter events, 18.4 us)
Async XLA Ops:
  7.2 5.6 %copy-start.1 = (s32[8,64]{1,0:T(8,128)S(1)}, s32[8,64]{1,0:T(8,128)}, u32[]{:S(2)}) copy-start(s32[8,64]{1,0:T(8,128)} %param.13) | copy-start | bytes 6148
  7.2 55.7 %all-gather.2.cloned.1.call-start = ((), (), s32[]{:S(2)}) async-start(), calls=%async_computation.2 | async-start | bytes 9437184 | tf_op jit(solution)/shard_map/all_gather | solution.py:260
  24.0 7.0 %copy-start.10 = (s32[8]{0:T(128)S(1)}, s32[8]{0:T(128)}, u32[]{:S(2)}) copy-start(s32[8]{0:T(128)} %param.12) | copy-start | bytes 100
  24.0 7.7 %copy-start.2 = (s32[8,32]{1,0:T(8,128)S(1)}, s32[8,32]{1,0:T(8,128)}, u32[]{:S(2)}) copy-start(s32[8,32]{1,0:T(8,128)} %param.14) | copy-start | bytes 3076
  24.0 9.3 %copy-start.9 = (bf16[2,512]{1,0:T(2,128)(2,1)S(1)}, bf16[2,512]{1,0:T(2,128)(2,1)}, u32[]{:S(2)}) copy-start(bf16[2,512]{1,0:T(2,128)(2,1)} %param.10) | copy-start | bytes 6148
  24.0 162.5 %all-to-all-start = ((bf16[16,2,4,64,512]{4,3,2,1,0:T(8,128)(2,1)}), bf16[16,2,4,64,512]{4,3,2,1,0:T(8,128)(2,1)}, u32[]{:S(2)}, u32[]{:S(2)}) async-start(bf16[16,2,4,64,512]{4,3,2,1,0:T(8,128)(2,1)} %bitcast.49), calls=%async_computation | async-start | bytes 16777216 | tf_op jit(solution)/shard_map/all_to_all | solution.py:254
  80.6 2.7 copy-start.8
  84.0 93.9 %copy-start.3 = (bf16[1024,1,512]{2,0,1:T(8,128)(2,1)}, bf16[1024,1,512]{2,0,1:T(8,128)(2,1)S(1)}, u32[]{:S(2)}) copy-start(bf16[1024,1,512]{2,0,1:T(8,128)(2,1)S(1)} %copy.19) | copy-start | bytes 3145732
  102.9 4.2 %copy-start.4 = (f32[1024,64]{1,0:T(8,128)S(1)}, f32[1024,64]{1,0:T(8,128)}, u32[]{:S(2)}) copy-start(f32[1024,64]{1,0:T(8,128)} %get-tuple-element.30) | copy-start | bytes 786436
  102.9 4.2 %copy-start.6 = (f32[1024,64]{1,0:T(8,128)S(1)}, f32[1024,64]{1,0:T(8,128)}, u32[]{:S(2)}) copy-start(f32[1024,64]{1,0:T(8,128)} %get-tuple-element.31) | copy-start | bytes 786436
  110.7 3.1 %copy-start = (s32[4]{0:T(128)S(1)}, s32[4]{0:T(128)}, u32[]{:S(2)}) copy-start(s32[4]{0:T(128)} %constant.143.clone) | copy-start | bytes 52
  112.3 65.7 %collective-permute-start = (bf16[2,1024,512]{2,1,0:T(8,128)(2,1)}, bf16[2,1024,512]{2,1,0:T(8,128)(2,1)}, u32[]{:S(2)}, u32[]{:S(2)}) collective-permute-start(bf16[2,1024,512]{2,1,0:T(8,128)(2,1)} %pad_maximum_fusion), channel_id=1, source_target_pairs={{0,1},{1,0},{2,3},{3,2},{4,5},{5,4},{6,7},{7,6},{8,9},{9,8},{10,11... | collective-permute-start | bytes 6291464 | tf_op jit(solution)/shard_map/ppermute | solution.py:292
  186.5 103.7 %all-to-all-start.1 = ((bf16[8,2,2,64,512]{4,3,2,1,0:T(8,128)(2,1)}), bf16[8,2,2,64,512]{4,3,2,1,0:T(8,128)(2,1)S(1)}, u32[]{:S(2)}, u32[]{:S(2)}) async-start(bf16[8,2,2,64,512]{4,3,2,1,0:T(8,128)(2,1)} %bitcast.61), calls=%async_computation.1 | async-start | bytes 4194304 | tf_op jit(solution)/shard_map/all_to_all | solution.py:315
  199.1 4.2 %copy-start.5 = (f32[1024,64]{1,0:T(8,128)S(1)}, f32[1024,64]{1,0:T(8,128)}, u32[]{:S(2)}) copy-start(f32[1024,64]{1,0:T(8,128)} %get-tuple-element.30) | copy-start | bytes 786436
  199.1 4.2 %copy-start.7 = (f32[1024,64]{1,0:T(8,128)S(1)}, f32[1024,64]{1,0:T(8,128)}, u32[]{:S(2)}) copy-start(f32[1024,64]{1,0:T(8,128)} %get-tuple-element.31) | copy-start | bytes 786436
Sparse Core Ops, SparseCore 0:
  12.9 49.9 all-gather.1

commit v7 on v6

--- a/solution.py
+++ b/solution.py
@@ -91,6 +91,51 @@
         acc_out[...] = acc_sc[...]
         m_out[...] = m_sc[...]
         l_out[...] = l_sc[...]
+
+
+def partner_kernel(meta_ref, q_ref, k_ref, v_ref, acc_in, m_in, l_in, acc_out, m_out, l_out):
+    member = meta_ref[0]
+    rows = q_ref.shape[0]
+    half = rows // 2
+    acc_out[...] = acc_in[...]
+    m_out[...] = m_in[...]
+    l_out[...] = l_in[...]
+
+    @pl.when(member == 0)
+    def _():
+        s = scores_of(q_ref[pl.ds(half, half), :], k_ref[...])
+        online_update(
+            s, v_ref[...], m_out.at[pl.ds(half, half)], l_out.at[pl.ds(half, half)],
+            acc_out.at[pl.ds(half, half)],
+        )
+
+    @pl.when(member != 0)
+    def _():
+        s = scores_of(q_ref[...], k_ref[pl.ds(0, half), :])
+        online_update(s, v_ref[pl.ds(0, half), :], m_out, l_out, acc_out)
+
+
+def partner_attention(meta, queries, keys, values, state):
+    tok_rows, width = queries.shape
+    heads = width // HS
+    shape = jax.ShapeDtypeStruct((tok_rows, width), jnp.float32)
+    spec = pl.BlockSpec((tok_rows, HS), lambda h, meta: (0, h))
+    return pl.pallas_call(
+        partner_kernel,
+        out_shape=(shape, shape, shape),
+        grid_spec=pltpu.PrefetchScalarGridSpec(
+            num_scalar_prefetch=1,
+            grid=(heads,),
+            in_specs=[spec] * 6,
+            out_specs=[spec] * 3,
+        ),
+        compiler_params=pltpu.CompilerParams(dimension_semantics=("arbitrary",)),
+        cost_estimate=pl.CostEstimate(
+            flops=2 * 2 * tok_rows * tok_rows * width // 2,
+            transcendentals=tok_rows * tok_rows * heads // 2,
+            bytes_accessed=3 * 2 * tok_rows * width + 6 * 4 * tok_rows * width,
+        ),
+    )(meta, queries, keys, values, *state)
 
 
 def cached_kernel(meta_ref, q_ref, k_ref, v_ref, acc_in, m_in, l_in, o_ref, m_sc, l_sc, acc_sc,
@@ -325,7 +370,7 @@
         .reshape(kv_cache.shape)
     )
 
-    state = new_attention(meta, queries, partner_new[0], partner_new[1], state)
+    state = partner_attention(meta, queries, partner_new[0], partner_new[1], state)
     attended = cached_attention(meta, queries, received, *state)
     return (attended, updated_cache)
 

time: 304 us -> 294 us (0.967)
  Pallas kernels: 79.5 us -> 70 us
    pallas_call x2 -> x1, Pallas kernels: 39.9 us -> 18.3 us  [new_attention(): pl.pallas_call(functools.partial(new_kernel, partner=partner), out_shape=...]
    pallas_call x0 -> x1, Pallas kernels: none -> 11.9 us  [partner_attention(): pl.pallas_call(partner_kernel, out_shape=(shape, shape, shape), grid_spec...]
  transfers between devices with their start and end apart: 4 -> 4, of which waited for: 2 -> 2; matrix products, arithmetic and copies ran while one was open for 27% -> 27% of each run, Pallas kernels for 26% -> 24%
where the time goes in v7:
time: 294 us; the launch traced here: 293 us
  waiting for transfers between devices  81.9 us (28%)
  Pallas kernels  70 us (24%)
  local copies, waits for them, and re-layouts  43.4 us (15%)
  other arithmetic  32.6 us (11%)
  starting transfers between devices  20.5 us (7%)
  matrix products  17.8 us (6%)
  between operations  14.4 us (5%)
  blocking collectives  12.4 us (4%)
    ppermute x1, waiting for transfers between devices, body(): partner_new = lax.ppermute(fresh_kv, 'bp', [(0, 1), (1, 0)])  56 us
    pallas_call x1, Pallas kernels, cached_attention(): pl.pallas_call(functools.partial(cached_kernel, groups=groups, block_len=...  39.8 us
    all_gather x1, waiting for transfers between devices, body(): lax.all_gather(states, 'head', axis=1, tiled=True)  25.9 us
    pallas_call x1, Pallas kernels, new_attention(): pl.pallas_call(functools.partial(new_kernel, partner=partner), out_shape=...  18.3 us
    dot_general x1, matrix products, body(): jnp.einsum('tc,jcw->tjw', lax.all_gather(states, 'head', axis=1, tiled=Tr...  17.8 us
    all_to_all x1, starting transfers between devices, body(): lax.all_to_all(picked, 'bx', split_axis=0, concat_axis=0, tiled=True)  12.7 us
    psum x1, blocking collectives, body(): lax.psum((jnp.sum(queries * queries, axis=1), jnp.sum(key_new * key_new,...  12.4 us
    pallas_call x1, Pallas kernels, partner_attention(): pl.pallas_call(partner_kernel, out_shape=(shape, shape, shape), grid_spec...  11.9 us
  transfers between devices with their start and end apart: 4, of which 2 were waited for; matrix products, arithmetic and copies ran while one was open for 27% of the time, Pallas kernels for 24%

profile of v7, /device:TPU:110, one launch (start us, length us, event | category | flops | bytes accessed | tf_op | source)
XLA Modules:
  0.0 292.9 jit_solution(12300048467684189519)
XLA Ops:
  7.2 5.5 %copy.28 = bf16[2,40,64,512]{3,2,1,0:T(8,128)(2,1)} copy(bf16[2,40,64,512]{3,2,1,0:T(8,128)(2,1)} %param.11) | data formatting | bytes 10485760
  15.0 9.0 %gather_fusion.2 = bf16[128,64,512]{2,1,0:T(8,128)(2,1)} fusion(bf16[80,64,512]{2,1,0:T(8,128)(2,1)} %bitcast.46, s32[1024]{0:T(1024)S(1)} %pad_clamp_fusion.2), kind=kCustom, calls=%fused_computation.2 | custom fusion | bytes 16777728 | tf_op jit(solution)/shard_map/jit(_take)/gather | solution.py:296
  24.0 7.0 %all-to-all-start = ((bf16[16,2,4,64,512]{4,3,2,1,0:T(8,128)(2,1)}), bf16[16,2,4,64,512]{4,3,2,1,0:T(8,128)(2,1)}, u32[]{:S(2)}, u32[]{:S(2)}) async-start(bf16[16,2,4,64,512]{4,3,2,1,0:T(8,128)(2,1)} %bitcast.49), calls=%async_computation | async-start | bytes 16777216 | tf_op jit(solution)/shard_map/all_to_all | solution.py:299
  33.3 3.1 %multiply_cosine_fusion = (f32[1024,64]{1,0:T(8,128)}, f32[1024,64]{1,0:T(8,128)}) fusion(f32[64]{0:T(128)S(1)} %multiply_power_fusion, f32[1024]{0:T(1024)S(1)} %fusion.15), kind=kLoop, calls=%fused_computation.26 | loop fusion | flops 65536 | bytes 528640 | tf_op jit(solution)/shard_map/cos | solution.py:25
  37.0 25.9 %all-gather.2.cloned.1.call-done = bf16[1024,4096]{1,0:T(8,128)(2,1)} async-done(((bf16[1024,512]{1,0:T(8,128)(2,1)}), bf16[1024,4096]{1,0:T(8,128)(2,1)}) %all-gather.2.cloned.1.call-update) | async-done | bytes 8388624 | tf_op jit(solution)/shard_map/all_gather | solution.py:305
  62.9 17.8 %fusion = f32[1024,3,512]{0,2,1:T(8,128)S(1)} fusion(bf16[3,4096,512]{2,1,0:T(8,128)(2,1)} %param.9, bf16[1024,4096]{1,0:T(8,128)(2,1)} %all-gather.2.cloned.1.call-done), kind=kOutput, calls=%fused_computation.7 | convolution fusion | flops 12884901888 | bytes 27262976 | tf_op jit(solution)/shard_map/tc,jcw->tjw/dot_general | solution.py:303
  80.7 2.6 copy-done.8
  84.0 4.6 %multiply_reduce_fusion = (f32[1024]{0:T(1024)S(1)}, f32[1024]{0:T(1024)S(1)}, f32[1024,1,512]{0,2,1:T(8,128)S(1)}, f32[1024,1,512]{0,2,1:T(8,128)}) fusion(f32[1024,3,512]{0,2,1:T(8,128)} %copy-done.8), kind=kLoop, calls=%fused_computation.15 | loop fusion | flops 2095104 | bytes 8396800 | tf_op jit(solution)/shard_map/reduce_sum | solution.py:313
  88.6 1.9 copy.16
  90.5 12.4 %all-reduce = (f32[1024]{0:T(1024)S(1)}, f32[1024]{0:T(1024)S(1)}) all-reduce(f32[1024]{0:T(1024)S(1)} %get-tuple-element.15, f32[1024]{0:T(1024)S(1)} %get-tuple-element.14), channel_id=1, replica_groups=mesh['head'=8,'bx'=8,'bp'=2] {'head'}, use_global_device_ids=true, to_apply=%region_1.2 | all-reduce | flops 2048 | bytes 16384 | tf_op jit(solution)/shard_map/psum | solution.py:312
  102.9 4.2 %multiply_multiply_fusion = f32[1024,4,128]{2,1,0:T(4,128)S(1)} fusion(f32[1024,4,128]{2,1,0:T(4,128)} %copy.16, f32[4,128]{1,0:T(4,128)S(1)} %bitcast.65, f32[1024]{0:T(1024)S(1)} %get-tuple-element.34), kind=kLoop, calls=%fused_computation.14 | loop fusion | flops 1048576 | bytes 4200448 | tf_op jit(solution)/shard_map/mul | solution.py:317
  115.9 2.0 pad_add_fusion.meta_ref
  119.0 2.9 copy.15
  121.9 56.0 %collective-permute-done = bf16[2,1024,512]{2,1,0:T(8,128)(2,1)} collective-permute-done((bf16[2,1024,512]{2,1,0:T(8,128)(2,1)}, bf16[2,1024,512]{2,1,0:T(8,128)(2,1)}, u32[]{:S(2)}, u32[]{:S(2)}) %collective-permute-start) | collective-permute-done | bytes 2097184 | tf_op jit(solution)/shard_map/ppermute | solution.py:337
  178.0 4.3 %maximum_select_fusion = bf16[2,2048,512]{2,1,0:T(8,128)(2,1)} fusion(bf16[2,1024,512]{2,1,0:T(8,128)(2,1)} %collective-permute-done, bf16[1,1024,512]{2,1,0:T(8,128)(2,1)S(1)} %bitcast.56, bf16[1,1024,512]{2,1,0:T(8,128)(2,1)S(1)} %convert_element_type.32, pred[]{:T(512)S(6)} %eq.10), kind=kLoop, calls=%fused_computation.9 | loop fusion | flops 27262976 | bytes 8388609 | tf_op jit(solution)/shard_map/jit(_where)/select_n | solution.py:342
  182.3 4.2 %gather_fusion.5 = bf16[32,64,512]{2,1,0:T(8,128)(2,1)} fusion(bf16[64,64,512]{2,1,0:T(8,128)(2,1)} %bitcast.54, s32[1024]{0:T(1024)S(1)} %pad_clamp_fusion), kind=kCustom, calls=%fused_computation.5 | custom fusion | bytes 4194432 | tf_op jit(solution)/shard_map/jit(_take)/gather | solution.py:357
  186.5 12.7 %all-to-all-start.1 = ((bf16[8,2,2,64,512]{4,3,2,1,0:T(8,128)(2,1)}), bf16[8,2,2,64,512]{4,3,2,1,0:T(8,128)(2,1)S(1)}, u32[]{:S(2)}, u32[]{:S(2)}) async-start(bf16[8,2,2,64,512]{4,3,2,1,0:T(8,128)(2,1)} %bitcast.61), calls=%async_computation.1 | async-start | bytes 4194304 | tf_op jit(solution)/shard_map/all_to_all | solution.py:360
  199.1 4.2 %multiply_multiply_fusion.1 = f32[1024,4,128]{2,1,0:T(4,128)S(1)} fusion(f32[1024,4,128]{2,1,0:T(4,128)} %copy.15, f32[4,128]{1,0:T(4,128)S(1)} %bitcast.64, f32[1024]{0:T(1024)S(1)} %get-tuple-element.35), kind=kLoop, calls=%fused_computation.18 | loop fusion | flops 1048576 | bytes 4200448 | tf_op jit(solution)/shard_map/mul | solution.py:316
  203.3 1.7 subtract_convert_fusion
  207.7 18.3 %shard_map.95 = (f32[1024,512]{1,0:T(8,128)}, f32[1024,512]{1,0:T(8,128)}, f32[1024,512]{1,0:T(8,128)}) custom-call(s32[4]{0:T(128)} %pad_add_fusion.meta_ref, bf16[1024,512]{1,0:T(8,128)(2,1)} %bitcast.50, bf16[1024,512]{1,0:T(8,128)(2,1)} %bitcast.63, bf16[1024,512]{1,0:T(8,128)(2,1)} %bitcast.57), custom_call_target="tpu_custom_call" | custom-call | flops 1610612736 | bytes 15728640 | tf_op jit(solution)/shard_map/pallas_call | solution.py:196
  226.1 3.0 %slice_bitcast_fusion = (bf16[1024,512]{1,0:T(8,128)(2,1)}, bf16[1024,512]{1,0:T(8,128)(2,1)}) fusion(bf16[2,1024,512]{2,1,0:T(8,128)(2,1)} %collective-permute-done), kind=kLoop, calls=%fused_computation.22 | loop fusion | bytes 4194304 | tf_op jit(solution)/shard_map/squeeze | solution.py:373
  229.0 11.9 %shard_map.96 = (f32[1024,512]{1,0:T(8,128)}, f32[1024,512]{1,0:T(8,128)}, f32[1024,512]{1,0:T(8,128)}) custom-call(s32[4]{0:T(128)} %pad_add_fusion.meta_ref, bf16[1024,512]{1,0:T(8,128)(2,1)} %bitcast.51, bf16[1024,512]{1,0:T(8,128)(2,1)} %get-tuple-element.29.k_ref, bf16[1024,512]{1,0:T(8,128)(2,1)} %get-tuple-element.28.v_ref, ...), custom_call_target="tpu_custom_call" | custom-call | flops 1073741824 | bytes 15728640 | tf_op jit(solution)/shard_map/pallas_call | solution.py:123
  240.9 39.8 %shard_map.97 = bf16[1024,512]{1,0:T(8,128)(2,1)} custom-call(s32[4]{0:T(128)} %pad_add_fusion.meta_ref, bf16[1024,512]{1,0:T(8,128)(2,1)} %bitcast.52, bf16[16,2,4,64,512]{4,3,2,1,0:T(8,128)(2,1)} %all-to-all-done.k_ref.v_ref, bf16[16,2,4,64,512]{4,3,2,1,0:T(8,128)(2,1)} %all-to-all-done.k_ref.v_ref, f32[1024,512]{1,0:T(8,128)} %get-tuple-element.11.acc_in, ...), custom_call_target="tpu_custom_call" | custom-call | flops 4294967296 | bytes 12582912 | tf_op jit(solution)/shard_map/pallas_call | solution.py:236
  280.7 5.3 %scatter_fusion = bf16[80,64,512]{2,1,0:T(8,128)(2,1)} fusion(bf16[80,64,512]{2,1,0:T(8,128)(2,1)} %bitcast.47, s32[32]{0:T(128)S(1)} %fusion.31, bf16[32,64,512]{2,1,0:T(8,128)(2,1)S(1)} %bitcast.59), kind=kCustom, calls=%fused_computation.6 | custom fusion | bytes 6291584 | tf_op jit(solution)/shard_map/scatter | solution.py:369
  (83 shorter events, 18.4 us)
Async XLA Ops:
  7.2 5.6 %copy-start.1 = (s32[8,64]{1,0:T(8,128)S(1)}, s32[8,64]{1,0:T(8,128)}, u32[]{:S(2)}) copy-start(s32[8,64]{1,0:T(8,128)} %param.13) | copy-start | bytes 6148
  7.2 55.7 %all-gather.2.cloned.1.call-start = ((), (), s32[]{:S(2)}) async-start(), calls=%async_computation.2 | async-start | bytes 9437184 | tf_op jit(solution)/shard_map/all_gather | solution.py:305
  24.0 7.0 %copy-start.10 = (s32[8]{0:T(128)S(1)}, s32[8]{0:T(128)}, u32[]{:S(2)}) copy-start(s32[8]{0:T(128)} %param.12) | copy-start | bytes 100
  24.0 7.7 %copy-start.2 = (s32[8,32]{1,0:T(8,128)S(1)}, s32[8,32]{1,0:T(8,128)}, u32[]{:S(2)}) copy-start(s32[8,32]{1,0:T(8,128)} %param.14) | copy-start | bytes 3076
  24.0 9.3 %copy-start.9 = (bf16[2,512]{1,0:T(2,128)(2,1)S(1)}, bf16[2,512]{1,0:T(2,128)(2,1)}, u32[]{:S(2)}) copy-start(bf16[2,512]{1,0:T(2,128)(2,1)} %param.10) | copy-start | bytes 6148
  24.0 162.5 %all-to-all-start = ((bf16[16,2,4,64,512]{4,3,2,1,0:T(8,128)(2,1)}), bf16[16,2,4,64,512]{4,3,2,1,0:T(8,128)(2,1)}, u32[]{:S(2)}, u32[]{:S(2)}) async-start(bf16[16,2,4,64,512]{4,3,2,1,0:T(8,128)(2,1)} %bitcast.49), calls=%async_computation | async-start | bytes 16777216 | tf_op jit(solution)/shard_map/all_to_all | solution.py:299
  80.6 2.7 copy-start.8
  84.0 93.9 %copy-start.3 = (bf16[1024,1,512]{2,0,1:T(8,128)(2,1)}, bf16[1024,1,512]{2,0,1:T(8,128)(2,1)S(1)}, u32[]{:S(2)}) copy-start(bf16[1024,1,512]{2,0,1:T(8,128)(2,1)S(1)} %copy.19) | copy-start | bytes 3145732
  102.9 4.2 %copy-start.4 = (f32[1024,64]{1,0:T(8,128)S(1)}, f32[1024,64]{1,0:T(8,128)}, u32[]{:S(2)}) copy-start(f32[1024,64]{1,0:T(8,128)} %get-tuple-element.30) | copy-start | bytes 786436
  102.9 4.2 %copy-start.6 = (f32[1024,64]{1,0:T(8,128)S(1)}, f32[1024,64]{1,0:T(8,128)}, u32[]{:S(2)}) copy-start(f32[1024,64]{1,0:T(8,128)} %get-tuple-element.31) | copy-start | bytes 786436
  110.7 3.1 %copy-start = (s32[4]{0:T(128)S(1)}, s32[4]{0:T(128)}, u32[]{:S(2)}) copy-start(s32[4]{0:T(128)} %constant.143.clone) | copy-start | bytes 52
  112.3 65.7 %collective-permute-start = (bf16[2,1024,512]{2,1,0:T(8,128)(2,1)}, bf16[2,1024,512]{2,1,0:T(8,128)(2,1)}, u32[]{:S(2)}, u32[]{:S(2)}) collective-permute-start(bf16[2,1024,512]{2,1,0:T(8,128)(2,1)} %pad_maximum_fusion), channel_id=1, source_target_pairs={{0,1},{1,0},{2,3},{3,2},{4,5},{5,4},{6,7},{7,6},{8,9},{9,8},{10,11... | collective-permute-start | bytes 6291464 | tf_op jit(solution)/shard_map/ppermute | solution.py:337
  186.5 94.3 %all-to-all-start.1 = ((bf16[8,2,2,64,512]{4,3,2,1,0:T(8,128)(2,1)}), bf16[8,2,2,64,512]{4,3,2,1,0:T(8,128)(2,1)S(1)}, u32[]{:S(2)}, u32[]{:S(2)}) async-start(bf16[8,2,2,64,512]{4,3,2,1,0:T(8,128)(2,1)} %bitcast.61), calls=%async_computation.1 | async-start | bytes 4194304 | tf_op jit(solution)/shard_map/all_to_all | solution.py:360
  199.1 4.2 %copy-start.5 = (f32[1024,64]{1,0:T(8,128)S(1)}, f32[1024,64]{1,0:T(8,128)}, u32[]{:S(2)}) copy-start(f32[1024,64]{1,0:T(8,128)} %get-tuple-element.30) | copy-start | bytes 786436
  199.1 4.2 %copy-start.7 = (f32[1024,64]{1,0:T(8,128)S(1)}, f32[1024,64]{1,0:T(8,128)}, u32[]{:S(2)}) copy-start(f32[1024,64]{1,0:T(8,128)} %get-tuple-element.31) | copy-start | bytes 786436
Sparse Core Ops, SparseCore 0:
  12.9 49.9 all-gather.1

commit v8 on v7

--- a/solution.py
+++ b/solution.py
@@ -37,10 +37,11 @@
     m_cur = jnp.max(s, axis=1, keepdims=True) * scale2
     m_next = jnp.maximum(m_prev, m_cur)
     alpha = jnp.exp2(m_prev - m_next)
-    p = jnp.exp2(s * scale2 - m_next[:, :1])
-    l_sc[...] = alpha * l_sc[...] + jnp.sum(p, axis=1, keepdims=True)
-    pv = jnp.dot(p.astype(jnp.bfloat16), v, preferred_element_type=jnp.float32)
-    acc_sc[...] = acc_sc[...] * alpha + pv
+    p = jnp.exp2(s * scale2 - m_next[:, :1]).astype(jnp.bfloat16)
+    v_ext = jnp.concatenate([v, jnp.ones(v.shape, v.dtype)], axis=1)
+    pv = jnp.dot(p, v_ext, preferred_element_type=jnp.float32)
+    acc_sc[...] = acc_sc[...] * alpha + pv[:, :HS]
+    l_sc[...] = l_sc[...] * alpha + pv[:, HS:]
     m_sc[...] = m_next
 
 
@@ -73,17 +74,12 @@
             l_sc[...] = jnp.zeros(l_sc.shape, jnp.float32)
             acc_sc[...] = jnp.zeros(acc_sc.shape, jnp.float32)
 
-    @pl.when(k_chunk < q_chunk)
-    def _():
-        s = scores_of(q_ref[...], k_ref[...])
-        online_update(s, v_ref[...], m_sc, l_sc, acc_sc)
-
-    @pl.when(k_chunk == q_chunk)
+    @pl.when(k_chunk <= q_chunk)
     def _():
         s = scores_of(q_ref[...], k_ref[...])
         rows = lax.broadcasted_iota(jnp.int32, s.shape, 0)
         cols = lax.broadcasted_iota(jnp.int32, s.shape, 1)
-        s = jnp.where(cols <= rows, s, -jnp.inf)
+        s = jnp.where((k_chunk < q_chunk) | (cols <= rows), s, -jnp.inf)
         online_update(s, v_ref[...], m_sc, l_sc, acc_sc)
 
     @pl.when(kj == pl.num_programs(2) - 1)
@@ -94,6 +90,8 @@
 
 
 def partner_kernel(meta_ref, q_ref, k_ref, v_ref, acc_in, m_in, l_in, acc_out, m_out, l_out):
+    k_ref = k_ref.at[0]
+    v_ref = v_ref.at[0]
     member = meta_ref[0]
     rows = q_ref.shape[0]
     half = rows // 2
@@ -115,18 +113,20 @@
         online_update(s, v_ref[pl.ds(0, half), :], m_out, l_out, acc_out)
 
 
-def partner_attention(meta, queries, keys, values, state):
+def partner_attention(meta, queries, partner_new, state):
     tok_rows, width = queries.shape
     heads = width // HS
     shape = jax.ShapeDtypeStruct((tok_rows, width), jnp.float32)
     spec = pl.BlockSpec((tok_rows, HS), lambda h, meta: (0, h))
+    key_spec = pl.BlockSpec((1, tok_rows, HS), lambda h, meta: (0, 0, h))
+    value_spec = pl.BlockSpec((1, tok_rows, HS), lambda h, meta: (1, 0, h))
     return pl.pallas_call(
         partner_kernel,
         out_shape=(shape, shape, shape),
         grid_spec=pltpu.PrefetchScalarGridSpec(
             num_scalar_prefetch=1,
             grid=(heads,),
-            in_specs=[spec] * 6,
+            in_specs=[spec, key_spec, value_spec, spec, spec, spec],
             out_specs=[spec] * 3,
         ),
         compiler_params=pltpu.CompilerParams(dimension_semantics=("arbitrary",)),
@@ -135,7 +135,7 @@
             transcendentals=tok_rows * tok_rows * heads // 2,
             bytes_accessed=3 * 2 * tok_rows * width + 6 * 4 * tok_rows * width,
         ),
-    )(meta, queries, keys, values, *state)
+    )(meta, queries, partner_new, partner_new, *state)
 
 
 def cached_kernel(meta_ref, q_ref, k_ref, v_ref, acc_in, m_in, l_in, o_ref, m_sc, l_sc, acc_sc,
@@ -339,23 +339,26 @@
 
     blocks_dev = tok_rows // block_len
     chunk_blocks = blocks_dev // 2
-    collected = jnp.where(
-        member == 0,
-        jnp.concatenate([fresh_kv, partner_new], axis=1),
-        jnp.concatenate([partner_new, fresh_kv], axis=1),
-    )
-    new_blocks = 2 * blocks_dev
-    collected_flat = collected.reshape(2 * new_blocks, block_len, local_width)
-    chunk_place = jnp.array([0, 2, 3, 1], dtype=jnp.int32)
     new_home = new_table[:, 0] // slot_count
     pair_index = jnp.arange(2, dtype=jnp.int32)
     reqs = jnp.arange(groups // pair, dtype=jnp.int32)
     dest = reqs * pair + member
     wanted_out = 2 * ((dest - new_home[request]) % groups)[:, None] + pair_index[None, :]
-    place = chunk_place[wanted_out // chunk_blocks] * chunk_blocks + wanted_out % chunk_blocks
-    pick_ids = kv_ids[None, :, None] * new_blocks + place[:, None, :]
-    picked = jnp.take(collected_flat, pick_ids.reshape(-1), axis=0, mode="clip").reshape(
-        groups // pair, 2, 2, block_len, local_width
+    chunk = wanted_out // chunk_blocks
+    within = wanted_out % chunk_blocks
+    own_place = jnp.where(chunk == member, 0, 1) * chunk_blocks + within
+    partner_place = jnp.where(chunk == 1 - member, 0, 1) * chunk_blocks + within
+    is_own = (chunk == member) | (chunk == 3 - member)
+
+    def pick(source, place):
+        ids = kv_ids[None, :, None] * blocks_dev + place[:, None, :]
+        return jnp.take(
+            source.reshape(2 * blocks_dev, block_len, local_width), ids.reshape(-1), axis=0,
+            mode="clip",
+        ).reshape(groups // pair, 2, 2, block_len, local_width)
+
+    picked = jnp.where(
+        is_own[:, None, :, None, None], pick(fresh_kv, own_place), pick(partner_new, partner_place)
     )
     arrived = lax.all_to_all(picked, "bx", split_axis=0, concat_axis=0, tiled=True)
     wanted_in = 2 * ((my_index - new_home) % groups)[:, None] + pair_index[None, :]
@@ -370,7 +373,7 @@
         .reshape(kv_cache.shape)
     )
 
-    state = partner_attention(meta, queries, partner_new[0], partner_new[1], state)
+    state = partner_attention(meta, queries, partner_new, state)
     attended = cached_attention(meta, queries, received, *state)
     return (attended, updated_cache)
 

time: 294 us -> 310 us (1.054)
  Pallas kernels: 70 us -> 86.2 us
  waiting for transfers between devices: 81.9 us -> 85.9 us
    pallas_call x1, Pallas kernels: 39.8 us -> 53.1 us  [cached_attention(): pl.pallas_call(functools.partial(cached_kernel, groups=groups, block_len=...]
    pallas_call x1, Pallas kernels: 18.3 us -> 21.7 us  [new_attention(): pl.pallas_call(functools.partial(new_kernel, partner=partner), out_shape=...]
    unnamed x26 -> x28, local copies, waits for them, and re-layouts: 11.1 us -> 11.9 us
  transfers between devices with their start and end apart: 4 -> 4, of which waited for: 2 -> 2; matrix products, arithmetic and copies ran while one was open for 27% -> 24% of each run, Pallas kernels for 24% -> 28%
where the time goes in v8:
time: 310 us; the launch traced here: 309 us
  Pallas kernels  86.2 us (28%)
  waiting for transfers between devices  85.9 us (28%)
  local copies, waits for them, and re-layouts  41.7 us (13%)
  other arithmetic  30.4 us (10%)
  starting transfers between devices  20.5 us (7%)
  matrix products  17.8 us (6%)
  between operations  14.4 us (5%)
  blocking collectives  12.4 us (4%)
    ppermute x1, waiting for transfers between devices, body(): partner_new = lax.ppermute(fresh_kv, 'bp', [(0, 1), (1, 0)])  57.9 us
    pallas_call x1, Pallas kernels, cached_attention(): pl.pallas_call(functools.partial(cached_kernel, groups=groups, block_len=...  53.1 us
    all_gather x1, waiting for transfers between devices, body(): lax.all_gather(states, 'head', axis=1, tiled=True)  28 us
    pallas_call x1, Pallas kernels, new_attention(): pl.pallas_call(functools.partial(new_kernel, partner=partner), out_shape=...  21.7 us
    dot_general x1, matrix products, body(): jnp.einsum('tc,jcw->tjw', lax.all_gather(states, 'head', axis=1, tiled=Tr...  17.8 us
    all_to_all x1, starting transfers between devices, body(): lax.all_to_all(picked, 'bx', split_axis=0, concat_axis=0, tiled=True)  12.7 us
    psum x1, blocking collectives, body(): lax.psum((jnp.sum(queries * queries, axis=1), jnp.sum(key_new * key_new,...  12.4 us
    unnamed x28, local copies, waits for them, and re-layouts  11.9 us
  transfers between devices with their start and end apart: 4, of which 2 were waited for; matrix products, arithmetic and copies ran while one was open for 24% of the time, Pallas kernels for 28%

profile of v8, /device:TPU:110, one launch (start us, length us, event | category | flops | bytes accessed | tf_op | source)
XLA Modules:
  0.0 309.3 jit_solution(1920239044570991680)
XLA Ops:
  7.2 5.5 %copy.27 = bf16[2,40,64,512]{3,2,1,0:T(8,128)(2,1)} copy(bf16[2,40,64,512]{3,2,1,0:T(8,128)(2,1)} %param.10) | data formatting | bytes 10485760
  15.0 9.0 %gather_fusion.2 = bf16[128,64,512]{2,1,0:T(8,128)(2,1)} fusion(bf16[80,64,512]{2,1,0:T(8,128)(2,1)} %bitcast.42, s32[1024]{0:T(1024)S(1)} %pad_clamp_fusion.2), kind=kCustom, calls=%fused_computation.2 | custom fusion | bytes 16777728 | tf_op jit(solution)/shard_map/jit(_take)/gather | solution.py:296
  24.0 7.0 %all-to-all-start = ((bf16[16,2,4,64,512]{4,3,2,1,0:T(8,128)(2,1)}), bf16[16,2,4,64,512]{4,3,2,1,0:T(8,128)(2,1)}, u32[]{:S(2)}, u32[]{:S(2)}) async-start(bf16[16,2,4,64,512]{4,3,2,1,0:T(8,128)(2,1)} %bitcast.45), calls=%async_computation | async-start | bytes 16777216 | tf_op jit(solution)/shard_map/all_to_all | solution.py:299
  33.0 1.9 multiply_cosine_fusion
  34.9 28.0 %all-gather.2.cloned.1.call-done = bf16[1024,4096]{1,0:T(8,128)(2,1)} async-done(((bf16[1024,512]{1,0:T(8,128)(2,1)}), bf16[1024,4096]{1,0:T(8,128)(2,1)}) %all-gather.2.cloned.1.call-update) | async-done | bytes 8388624 | tf_op jit(solution)/shard_map/all_gather | solution.py:305
  62.9 17.8 %fusion = f32[1024,3,512]{0,2,1:T(8,128)S(1)} fusion(bf16[3,4096,512]{2,1,0:T(8,128)(2,1)} %param.8, bf16[1024,4096]{1,0:T(8,128)(2,1)} %all-gather.2.cloned.1.call-done), kind=kOutput, calls=%fused_computation.7 | convolution fusion | flops 12884901888 | bytes 27262976 | tf_op jit(solution)/shard_map/tc,jcw->tjw/dot_general | solution.py:303
  80.7 2.7 copy-done.8
  84.8 4.2 %multiply_reduce_fusion = (f32[1024]{0:T(1024)S(1)}, f32[1024]{0:T(1024)S(1)}, f32[1024,1,512]{0,2,1:T(8,128)S(1)}, f32[1024,1,512]{0,2,1:T(8,128)}) fusion(f32[1024,3,512]{0,2,1:T(8,128)} %copy-done.8), kind=kLoop, calls=%fused_computation.14 | loop fusion | flops 2095104 | bytes 8396800 | tf_op jit(solution)/shard_map/reduce_sum | solution.py:313
  89.0 1.9 copy.15
  90.9 12.4 %all-reduce = (f32[1024]{0:T(1024)S(1)}, f32[1024]{0:T(1024)S(1)}) all-reduce(f32[1024]{0:T(1024)S(1)} %get-tuple-element.15, f32[1024]{0:T(1024)S(1)} %get-tuple-element.14), channel_id=1, replica_groups=mesh['head'=8,'bx'=8,'bp'=2] {'head'}, use_global_device_ids=true, to_apply=%region_1.2 | all-reduce | flops 2048 | bytes 16384 | tf_op jit(solution)/shard_map/psum | solution.py:312
  103.3 4.1 %multiply_multiply_fusion = f32[1024,4,128]{2,1,0:T(4,128)S(1)} fusion(f32[1024,4,128]{2,1,0:T(4,128)} %copy.15, f32[4,128]{1,0:T(4,128)S(1)} %bitcast.60, f32[1024]{0:T(1024)S(1)} %get-tuple-element.36), kind=kLoop, calls=%fused_computation.13 | loop fusion | flops 1048576 | bytes 4200448 | tf_op jit(solution)/shard_map/mul | solution.py:317
  116.4 3.6 %gather_fusion.4 = bf16[32,64,512]{2,1,0:T(8,128)(2,1)} fusion(bf16[32,64,512]{2,1,0:T(8,128)(2,1)} %bitcast.14, s32[1024]{0:T(1024)S(1)} %pad_clamp_fusion.1), kind=kCustom, calls=%fused_computation.4 | custom fusion | bytes 4194432 | tf_op jit(solution)/shard_map/jit(_take)/gather | solution.py:355
  120.0 57.9 %collective-permute-done.k_ref.v_ref = bf16[2,1024,512]{2,1,0:T(8,128)(2,1)S(1)} collective-permute-done((bf16[2,1024,512]{2,1,0:T(8,128)(2,1)}, bf16[2,1024,512]{2,1,0:T(8,128)(2,1)S(1)}, u32[]{:S(2)}, u32[]{:S(2)}) %collective-permute-start) | collective-permute-done | bytes 2097184 | tf_op jit(solution)/shard_map/ppermute | solution.py:337
  177.9 2.1 gather_fusion.5
  179.9 3.8 %broadcast_select_fusion = bf16[8,2,2,64,512]{4,3,2,1,0:T(8,128)(2,1)} fusion(bf16[8,2,2,64,512]{4,3,2,1,0:T(8,128)(2,1)} %bitcast.53, bf16[8,2,2,64,512]{4,3,2,1,0:T(8,128)(2,1)} %bitcast.54, pred[8,2]{1,0:T(8,128)(4,1)S(1)} %compare_or_fusion), kind=kLoop, calls=%fused_computation.19 | loop fusion | flops 1048576 | bytes 6291472 | tf_op jit(solution)/shard_map/jit(_where)/select_n | solution.py:360
  183.8 12.7 %all-to-all-start.1 = ((bf16[8,2,2,64,512]{4,3,2,1,0:T(8,128)(2,1)}), bf16[8,2,2,64,512]{4,3,2,1,0:T(8,128)(2,1)}, u32[]{:S(2)}, u32[]{:S(2)}) async-start(bf16[8,2,2,64,512]{4,3,2,1,0:T(8,128)(2,1)} %broadcast_select_fusion), calls=%async_computation.1 | async-start | bytes 4194304 | tf_op jit(solution)/shard_map/all_to_all | solution.py:363
  196.4 2.0 pad_add_fusion.meta_ref
  199.6 1.8 copy.14
  201.5 4.2 %multiply_multiply_fusion.1 = f32[1024,4,128]{2,1,0:T(4,128)S(1)} fusion(f32[1024,4,128]{2,1,0:T(4,128)} %copy.14, f32[4,128]{1,0:T(4,128)S(1)} %bitcast.59, f32[1024]{0:T(1024)S(1)} %get-tuple-element.37), kind=kLoop, calls=%fused_computation.17 | loop fusion | flops 1048576 | bytes 4200448 | tf_op jit(solution)/shard_map/mul | solution.py:316
  205.7 1.7 subtract_convert_fusion
  210.0 21.7 %shard_map.86 = (f32[1024,512]{1,0:T(8,128)}, f32[1024,512]{1,0:T(8,128)}, f32[1024,512]{1,0:T(8,128)}) custom-call(s32[4]{0:T(128)} %pad_add_fusion.meta_ref, bf16[1024,512]{1,0:T(8,128)(2,1)} %bitcast.47, bf16[1024,512]{1,0:T(8,128)(2,1)} %bitcast.58, bf16[1024,512]{1,0:T(8,128)(2,1)} %bitcast.56), custom_call_target="tpu_custom_call" | custom-call | flops 1610612736 | bytes 15728640 | tf_op jit(solution)/shard_map/pallas_call | solution.py:196
  231.7 11.4 %shard_map.87 = (f32[1024,512]{1,0:T(8,128)}, f32[1024,512]{1,0:T(8,128)}, f32[1024,512]{1,0:T(8,128)}) custom-call(s32[4]{0:T(128)} %pad_add_fusion.meta_ref, bf16[1024,512]{1,0:T(8,128)(2,1)} %bitcast.48, bf16[2,1024,512]{2,1,0:T(8,128)(2,1)} %copy-done.2, bf16[2,1024,512]{2,1,0:T(8,128)(2,1)} %copy-done.2, f32[1024,512]{1,0:T(8,128)} %get-tuple-element.8.acc_in, ...), custom_call_target="tpu_custom_call" | custom-call | flops 1073741824 | bytes 15728640 | tf_op jit(solution)/shard_map/pallas_call | solution.py:123
  243.1 53.1 %shard_map.88 = bf16[1024,512]{1,0:T(8,128)(2,1)} custom-call(s32[4]{0:T(128)} %pad_add_fusion.meta_ref, bf16[1024,512]{1,0:T(8,128)(2,1)} %bitcast.49, bf16[16,2,4,64,512]{4,3,2,1,0:T(8,128)(2,1)} %all-to-all-done.k_ref.v_ref, bf16[16,2,4,64,512]{4,3,2,1,0:T(8,128)(2,1)} %all-to-all-done.k_ref.v_ref, f32[1024,512]{1,0:T(8,128)} %get-tuple-element.11.acc_in, ...), custom_call_target="tpu_custom_call" | custom-call | flops 4294967296 | bytes 12582912 | tf_op jit(solution)/shard_map/pallas_call | solution.py:236
  296.2 6.2 %scatter_fusion = bf16[80,64,512]{2,1,0:T(8,128)(2,1)} fusion(bf16[80,64,512]{2,1,0:T(8,128)(2,1)} %bitcast.43, s32[32]{0:T(128)S(1)} %fusion.28, bf16[32,64,512]{2,1,0:T(8,128)(2,1)} %bitcast.18), kind=kCustom, calls=%fused_computation.6 | custom fusion | bytes 6291584 | tf_op jit(solution)/shard_map/scatter | solution.py:372
  (83 shorter events, 18.3 us)
Async XLA Ops:
  7.2 5.6 %copy-start = (s32[8,64]{1,0:T(8,128)S(1)}, s32[8,64]{1,0:T(8,128)}, u32[]{:S(2)}) copy-start(s32[8,64]{1,0:T(8,128)} %param.12) | copy-start | bytes 6148
  7.2 55.7 %all-gather.2.cloned.1.call-start = ((), (), s32[]{:S(2)}) async-start(), calls=%async_computation.2 | async-start | bytes 9437184 | tf_op jit(solution)/shard_map/all_gather | solution.py:305
  24.0 7.0 %copy-start.1 = (s32[8,32]{1,0:T(8,128)S(1)}, s32[8,32]{1,0:T(8,128)}, u32[]{:S(2)}) copy-start(s32[8,32]{1,0:T(8,128)} %param.13) | copy-start | bytes 3076
  24.0 7.2 %copy-start.10 = (bf16[2,512]{1,0:T(2,128)(2,1)S(1)}, bf16[2,512]{1,0:T(2,128)(2,1)}, u32[]{:S(2)}) copy-start(bf16[2,512]{1,0:T(2,128)(2,1)} %param.9) | copy-start | bytes 6148
  24.0 7.8 %copy-start.11 = (s32[8]{0:T(128)S(1)}, s32[8]{0:T(128)}, u32[]{:S(2)}) copy-start(s32[8]{0:T(128)} %param.11) | copy-start | bytes 100
  24.0 159.8 %all-to-all-start = ((bf16[16,2,4,64,512]{4,3,2,1,0:T(8,128)(2,1)}), bf16[16,2,4,64,512]{4,3,2,1,0:T(8,128)(2,1)}, u32[]{:S(2)}, u32[]{:S(2)}) async-start(bf16[16,2,4,64,512]{4,3,2,1,0:T(8,128)(2,1)} %bitcast.45), calls=%async_computation | async-start | bytes 16777216 | tf_op jit(solution)/shard_map/all_to_all | solution.py:299
  34.9 72.5 %copy-start.4 = (f32[1024,64]{1,0:T(8,128)}, f32[1024,64]{1,0:T(8,128)S(1)}, u32[]{:S(2)}) copy-start(f32[1024,64]{1,0:T(8,128)S(1)} %get-tuple-element.28) | copy-start | bytes 786436
  34.9 72.5 %copy-start.6 = (f32[1024,64]{1,0:T(8,128)}, f32[1024,64]{1,0:T(8,128)S(1)}, u32[]{:S(2)}) copy-start(f32[1024,64]{1,0:T(8,128)S(1)} %get-tuple-element.29) | copy-start | bytes 786436
  80.7 2.7 copy-start.8
  109.1 1.9 copy-start.9
  112.6 65.3 %collective-permute-start = (bf16[2,1024,512]{2,1,0:T(8,128)(2,1)}, bf16[2,1024,512]{2,1,0:T(8,128)(2,1)S(1)}, u32[]{:S(2)}, u32[]{:S(2)}) collective-permute-start(bf16[2,1024,512]{2,1,0:T(8,128)(2,1)} %pad_maximum_fusion), channel_id=1, source_target_pairs={{0,1},{1,0},{2,3},{3,2},{4,5},{5,4},{6,7},{7,6},{8,9},{9,8},{10,11... | collective-permute-start | bytes 6291464 | tf_op jit(solution)/shard_map/ppermute | solution.py:337
  177.8 2.1 copy-start.2
  183.8 112.5 %all-to-all-start.1 = ((bf16[8,2,2,64,512]{4,3,2,1,0:T(8,128)(2,1)}), bf16[8,2,2,64,512]{4,3,2,1,0:T(8,128)(2,1)}, u32[]{:S(2)}, u32[]{:S(2)}) async-start(bf16[8,2,2,64,512]{4,3,2,1,0:T(8,128)(2,1)} %broadcast_select_fusion), calls=%async_computation.1 | async-start | bytes 4194304 | tf_op jit(solution)/shard_map/all_to_all | solution.py:363
  196.4 3.2 %copy-start.3 = (f32[1024,1,512]{0,2,1:T(8,128)S(1)}, f32[1024,1,512]{0,2,1:T(8,128)}, u32[]{:S(2)}) copy-start(f32[1024,1,512]{0,2,1:T(8,128)} %get-tuple-element.23) | copy-start | bytes 6291460
  201.5 4.2 %copy-start.5 = (f32[1024,64]{1,0:T(8,128)S(1)}, f32[1024,64]{1,0:T(8,128)}, u32[]{:S(2)}) copy-start(f32[1024,64]{1,0:T(8,128)} %copy-done.4) | copy-start | bytes 786436
  201.5 4.2 %copy-start.7 = (f32[1024,64]{1,0:T(8,128)S(1)}, f32[1024,64]{1,0:T(8,128)}, u32[]{:S(2)}) copy-start(f32[1024,64]{1,0:T(8,128)} %copy-done.6) | copy-start | bytes 786436
Sparse Core Ops, SparseCore 0:
  12.9 49.9 all-gather.1

commit v9 on v8

--- a/solution.py
+++ b/solution.py
@@ -37,11 +37,10 @@
     m_cur = jnp.max(s, axis=1, keepdims=True) * scale2
     m_next = jnp.maximum(m_prev, m_cur)
     alpha = jnp.exp2(m_prev - m_next)
-    p = jnp.exp2(s * scale2 - m_next[:, :1]).astype(jnp.bfloat16)
-    v_ext = jnp.concatenate([v, jnp.ones(v.shape, v.dtype)], axis=1)
-    pv = jnp.dot(p, v_ext, preferred_element_type=jnp.float32)
-    acc_sc[...] = acc_sc[...] * alpha + pv[:, :HS]
-    l_sc[...] = l_sc[...] * alpha + pv[:, HS:]
+    p = jnp.exp2(s * scale2 - m_next[:, :1])
+    l_sc[...] = alpha * l_sc[...] + jnp.sum(p, axis=1, keepdims=True)
+    pv = jnp.dot(p.astype(jnp.bfloat16), v, preferred_element_type=jnp.float32)
+    acc_sc[...] = acc_sc[...] * alpha + pv
     m_sc[...] = m_next
 
 

time: 310 us -> 294 us (0.948)
  Pallas kernels: 86.2 us -> 70.2 us
    pallas_call x1, Pallas kernels: 53.1 us -> 39.8 us  [cached_attention(): pl.pallas_call(functools.partial(cached_kernel, groups=groups, block_len=...]
    pallas_call x1, Pallas kernels: 21.7 us -> 18.5 us  [new_attention(): pl.pallas_call(functools.partial(new_kernel, partner=partner), out_shape=...]
  transfers between devices with their start and end apart: 4 -> 4, of which waited for: 2 -> 2; matrix products, arithmetic and copies ran while one was open for 24% -> 26% of each run, Pallas kernels for 28% -> 24%
where the time goes in v9:
time: 294 us; the launch traced here: 293 us
  waiting for transfers between devices  85.9 us (29%)
  Pallas kernels  70.2 us (24%)
  local copies, waits for them, and re-layouts  41.7 us (14%)
  other arithmetic  30.4 us (10%)
  starting transfers between devices  20.5 us (7%)
  matrix products  17.8 us (6%)
  between operations  14.4 us (5%)
  blocking collectives  12.4 us (4%)
    ppermute x1, waiting for transfers between devices, body(): partner_new = lax.ppermute(fresh_kv, 'bp', [(0, 1), (1, 0)])  57.9 us
    pallas_call x1, Pallas kernels, cached_attention(): pl.pallas_call(functools.partial(cached_kernel, groups=groups, block_len=...  39.8 us
    all_gather x1, waiting for transfers between devices, body(): lax.all_gather(states, 'head', axis=1, tiled=True)  28 us
    pallas_call x1, Pallas kernels, new_attention(): pl.pallas_call(functools.partial(new_kernel, partner=partner), out_shape=...  18.5 us
    dot_general x1, matrix products, body(): jnp.einsum('tc,jcw->tjw', lax.all_gather(states, 'head', axis=1, tiled=Tr...  17.8 us
    all_to_all x1, starting transfers between devices, body(): lax.all_to_all(picked, 'bx', split_axis=0, concat_axis=0, tiled=True)  12.7 us
    psum x1, blocking collectives, body(): lax.psum((jnp.sum(queries * queries, axis=1), jnp.sum(key_new * key_new,...  12.4 us
    unnamed x28, local copies, waits for them, and re-layouts  11.9 us
  transfers between devices with their start and end apart: 4, of which 2 were waited for; matrix products, arithmetic and copies ran while one was open for 26% of the time, Pallas kernels for 24%

profile of v9, /device:TPU:110, one launch (start us, length us, event | category | flops | bytes accessed | tf_op | source)
XLA Modules:
  0.0 293.2 jit_solution(9585180318595682620)
XLA Ops:
  7.2 5.5 %copy.27 = bf16[2,40,64,512]{3,2,1,0:T(8,128)(2,1)} copy(bf16[2,40,64,512]{3,2,1,0:T(8,128)(2,1)} %param.10) | data formatting | bytes 10485760
  15.0 9.0 %gather_fusion.2 = bf16[128,64,512]{2,1,0:T(8,128)(2,1)} fusion(bf16[80,64,512]{2,1,0:T(8,128)(2,1)} %bitcast.42, s32[1024]{0:T(1024)S(1)} %pad_clamp_fusion.2), kind=kCustom, calls=%fused_computation.2 | custom fusion | bytes 16777728 | tf_op jit(solution)/shard_map/jit(_take)/gather | solution.py:295
  24.0 7.0 %all-to-all-start = ((bf16[16,2,4,64,512]{4,3,2,1,0:T(8,128)(2,1)}), bf16[16,2,4,64,512]{4,3,2,1,0:T(8,128)(2,1)}, u32[]{:S(2)}, u32[]{:S(2)}) async-start(bf16[16,2,4,64,512]{4,3,2,1,0:T(8,128)(2,1)} %bitcast.45), calls=%async_computation | async-start | bytes 16777216 | tf_op jit(solution)/shard_map/all_to_all | solution.py:298
  33.0 1.9 multiply_cosine_fusion
  34.9 28.0 %all-gather.2.cloned.1.call-done = bf16[1024,4096]{1,0:T(8,128)(2,1)} async-done(((bf16[1024,512]{1,0:T(8,128)(2,1)}), bf16[1024,4096]{1,0:T(8,128)(2,1)}) %all-gather.2.cloned.1.call-update) | async-done | bytes 8388624 | tf_op jit(solution)/shard_map/all_gather | solution.py:304
  62.9 17.8 %fusion = f32[1024,3,512]{0,2,1:T(8,128)S(1)} fusion(bf16[3,4096,512]{2,1,0:T(8,128)(2,1)} %param.8, bf16[1024,4096]{1,0:T(8,128)(2,1)} %all-gather.2.cloned.1.call-done), kind=kOutput, calls=%fused_computation.7 | convolution fusion | flops 12884901888 | bytes 27262976 | tf_op jit(solution)/shard_map/tc,jcw->tjw/dot_general | solution.py:302
  80.7 2.7 copy-done.8
  84.8 4.2 %multiply_reduce_fusion = (f32[1024]{0:T(1024)S(1)}, f32[1024]{0:T(1024)S(1)}, f32[1024,1,512]{0,2,1:T(8,128)S(1)}, f32[1024,1,512]{0,2,1:T(8,128)}) fusion(f32[1024,3,512]{0,2,1:T(8,128)} %copy-done.8), kind=kLoop, calls=%fused_computation.14 | loop fusion | flops 2095104 | bytes 8396800 | tf_op jit(solution)/shard_map/reduce_sum | solution.py:312
  89.0 1.9 copy.15
  90.9 12.4 %all-reduce = (f32[1024]{0:T(1024)S(1)}, f32[1024]{0:T(1024)S(1)}) all-reduce(f32[1024]{0:T(1024)S(1)} %get-tuple-element.15, f32[1024]{0:T(1024)S(1)} %get-tuple-element.14), channel_id=1, replica_groups=mesh['head'=8,'bx'=8,'bp'=2] {'head'}, use_global_device_ids=true, to_apply=%region_1.2 | all-reduce | flops 2048 | bytes 16384 | tf_op jit(solution)/shard_map/psum | solution.py:311
  103.3 4.1 %multiply_multiply_fusion = f32[1024,4,128]{2,1,0:T(4,128)S(1)} fusion(f32[1024,4,128]{2,1,0:T(4,128)} %copy.15, f32[4,128]{1,0:T(4,128)S(1)} %bitcast.60, f32[1024]{0:T(1024)S(1)} %get-tuple-element.36), kind=kLoop, calls=%fused_computation.13 | loop fusion | flops 1048576 | bytes 4200448 | tf_op jit(solution)/shard_map/mul | solution.py:316
  116.4 3.6 %gather_fusion.4 = bf16[32,64,512]{2,1,0:T(8,128)(2,1)} fusion(bf16[32,64,512]{2,1,0:T(8,128)(2,1)} %bitcast.14, s32[1024]{0:T(1024)S(1)} %pad_clamp_fusion.1), kind=kCustom, calls=%fused_computation.4 | custom fusion | bytes 4194432 | tf_op jit(solution)/shard_map/jit(_take)/gather | solution.py:354
  120.0 57.9 %collective-permute-done.k_ref.v_ref = bf16[2,1024,512]{2,1,0:T(8,128)(2,1)S(1)} collective-permute-done((bf16[2,1024,512]{2,1,0:T(8,128)(2,1)}, bf16[2,1024,512]{2,1,0:T(8,128)(2,1)S(1)}, u32[]{:S(2)}, u32[]{:S(2)}) %collective-permute-start) | collective-permute-done | bytes 2097184 | tf_op jit(solution)/shard_map/ppermute | solution.py:336
  177.9 2.1 gather_fusion.5
  179.9 3.8 %broadcast_select_fusion = bf16[8,2,2,64,512]{4,3,2,1,0:T(8,128)(2,1)} fusion(bf16[8,2,2,64,512]{4,3,2,1,0:T(8,128)(2,1)} %bitcast.53, bf16[8,2,2,64,512]{4,3,2,1,0:T(8,128)(2,1)} %bitcast.54, pred[8,2]{1,0:T(8,128)(4,1)S(1)} %compare_or_fusion), kind=kLoop, calls=%fused_computation.19 | loop fusion | flops 1048576 | bytes 6291472 | tf_op jit(solution)/shard_map/jit(_where)/select_n | solution.py:359
  183.8 12.7 %all-to-all-start.1 = ((bf16[8,2,2,64,512]{4,3,2,1,0:T(8,128)(2,1)}), bf16[8,2,2,64,512]{4,3,2,1,0:T(8,128)(2,1)}, u32[]{:S(2)}, u32[]{:S(2)}) async-start(bf16[8,2,2,64,512]{4,3,2,1,0:T(8,128)(2,1)} %broadcast_select_fusion), calls=%async_computation.1 | async-start | bytes 4194304 | tf_op jit(solution)/shard_map/all_to_all | solution.py:362
  196.4 2.0 pad_add_fusion.meta_ref
  199.6 1.8 copy.14
  201.5 4.2 %multiply_multiply_fusion.1 = f32[1024,4,128]{2,1,0:T(4,128)S(1)} fusion(f32[1024,4,128]{2,1,0:T(4,128)} %copy.14, f32[4,128]{1,0:T(4,128)S(1)} %bitcast.59, f32[1024]{0:T(1024)S(1)} %get-tuple-element.37), kind=kLoop, calls=%fused_computation.17 | loop fusion | flops 1048576 | bytes 4200448 | tf_op jit(solution)/shard_map/mul | solution.py:315
  205.7 1.7 subtract_convert_fusion
  210.0 18.5 %shard_map.86 = (f32[1024,512]{1,0:T(8,128)}, f32[1024,512]{1,0:T(8,128)}, f32[1024,512]{1,0:T(8,128)}) custom-call(s32[4]{0:T(128)} %pad_add_fusion.meta_ref, bf16[1024,512]{1,0:T(8,128)(2,1)} %bitcast.47, bf16[1024,512]{1,0:T(8,128)(2,1)} %bitcast.58, bf16[1024,512]{1,0:T(8,128)(2,1)} %bitcast.56), custom_call_target="tpu_custom_call" | custom-call | flops 1610612736 | bytes 15728640 | tf_op jit(solution)/shard_map/pallas_call | solution.py:195
  228.5 11.9 %shard_map.87 = (f32[1024,512]{1,0:T(8,128)}, f32[1024,512]{1,0:T(8,128)}, f32[1024,512]{1,0:T(8,128)}) custom-call(s32[4]{0:T(128)} %pad_add_fusion.meta_ref, bf16[1024,512]{1,0:T(8,128)(2,1)} %bitcast.48, bf16[2,1024,512]{2,1,0:T(8,128)(2,1)} %copy-done.2, bf16[2,1024,512]{2,1,0:T(8,128)(2,1)} %copy-done.2, f32[1024,512]{1,0:T(8,128)} %get-tuple-element.8.acc_in, ...), custom_call_target="tpu_custom_call" | custom-call | flops 1073741824 | bytes 15728640 | tf_op jit(solution)/shard_map/pallas_call | solution.py:122
  240.4 39.8 %shard_map.88 = bf16[1024,512]{1,0:T(8,128)(2,1)} custom-call(s32[4]{0:T(128)} %pad_add_fusion.meta_ref, bf16[1024,512]{1,0:T(8,128)(2,1)} %bitcast.49, bf16[16,2,4,64,512]{4,3,2,1,0:T(8,128)(2,1)} %all-to-all-done.k_ref.v_ref, bf16[16,2,4,64,512]{4,3,2,1,0:T(8,128)(2,1)} %all-to-all-done.k_ref.v_ref, f32[1024,512]{1,0:T(8,128)} %get-tuple-element.11.acc_in, ...), custom_call_target="tpu_custom_call" | custom-call | flops 4294967296 | bytes 12582912 | tf_op jit(solution)/shard_map/pallas_call | solution.py:235
  280.2 6.2 %scatter_fusion = bf16[80,64,512]{2,1,0:T(8,128)(2,1)} fusion(bf16[80,64,512]{2,1,0:T(8,128)(2,1)} %bitcast.43, s32[32]{0:T(128)S(1)} %fusion.28, bf16[32,64,512]{2,1,0:T(8,128)(2,1)} %bitcast.18), kind=kCustom, calls=%fused_computation.6 | custom fusion | bytes 6291584 | tf_op jit(solution)/shard_map/scatter | solution.py:371
  (83 shorter events, 18.3 us)
Async XLA Ops:
  7.2 5.6 %copy-start = (s32[8,64]{1,0:T(8,128)S(1)}, s32[8,64]{1,0:T(8,128)}, u32[]{:S(2)}) copy-start(s32[8,64]{1,0:T(8,128)} %param.12) | copy-start | bytes 6148
  7.2 55.7 %all-gather.2.cloned.1.call-start = ((), (), s32[]{:S(2)}) async-start(), calls=%async_computation.2 | async-start | bytes 9437184 | tf_op jit(solution)/shard_map/all_gather | solution.py:304
  24.0 7.0 %copy-start.1 = (s32[8,32]{1,0:T(8,128)S(1)}, s32[8,32]{1,0:T(8,128)}, u32[]{:S(2)}) copy-start(s32[8,32]{1,0:T(8,128)} %param.13) | copy-start | bytes 3076
  24.0 7.2 %copy-start.10 = (bf16[2,512]{1,0:T(2,128)(2,1)S(1)}, bf16[2,512]{1,0:T(2,128)(2,1)}, u32[]{:S(2)}) copy-start(bf16[2,512]{1,0:T(2,128)(2,1)} %param.9) | copy-start | bytes 6148
  24.0 7.8 %copy-start.11 = (s32[8]{0:T(128)S(1)}, s32[8]{0:T(128)}, u32[]{:S(2)}) copy-start(s32[8]{0:T(128)} %param.11) | copy-start | bytes 100
  24.0 159.8 %all-to-all-start = ((bf16[16,2,4,64,512]{4,3,2,1,0:T(8,128)(2,1)}), bf16[16,2,4,64,512]{4,3,2,1,0:T(8,128)(2,1)}, u32[]{:S(2)}, u32[]{:S(2)}) async-start(bf16[16,2,4,64,512]{4,3,2,1,0:T(8,128)(2,1)} %bitcast.45), calls=%async_computation | async-start | bytes 16777216 | tf_op jit(solution)/shard_map/all_to_all | solution.py:298
  34.9 72.5 %copy-start.4 = (f32[1024,64]{1,0:T(8,128)}, f32[1024,64]{1,0:T(8,128)S(1)}, u32[]{:S(2)}) copy-start(f32[1024,64]{1,0:T(8,128)S(1)} %get-tuple-element.28) | copy-start | bytes 786436
  34.9 72.5 %copy-start.6 = (f32[1024,64]{1,0:T(8,128)}, f32[1024,64]{1,0:T(8,128)S(1)}, u32[]{:S(2)}) copy-start(f32[1024,64]{1,0:T(8,128)S(1)} %get-tuple-element.29) | copy-start | bytes 786436
  80.7 2.7 copy-start.8
  109.1 1.9 copy-start.9
  112.6 65.3 %collective-permute-start = (bf16[2,1024,512]{2,1,0:T(8,128)(2,1)}, bf16[2,1024,512]{2,1,0:T(8,128)(2,1)S(1)}, u32[]{:S(2)}, u32[]{:S(2)}) collective-permute-start(bf16[2,1024,512]{2,1,0:T(8,128)(2,1)} %pad_maximum_fusion), channel_id=1, source_target_pairs={{0,1},{1,0},{2,3},{3,2},{4,5},{5,4},{6,7},{7,6},{8,9},{9,8},{10,11... | collective-permute-start | bytes 6291464 | tf_op jit(solution)/shard_map/ppermute | solution.py:336
  177.8 2.1 copy-start.2
  183.8 96.4 %all-to-all-start.1 = ((bf16[8,2,2,64,512]{4,3,2,1,0:T(8,128)(2,1)}), bf16[8,2,2,64,512]{4,3,2,1,0:T(8,128)(2,1)}, u32[]{:S(2)}, u32[]{:S(2)}) async-start(bf16[8,2,2,64,512]{4,3,2,1,0:T(8,128)(2,1)} %broadcast_select_fusion), calls=%async_computation.1 | async-start | bytes 4194304 | tf_op jit(solution)/shard_map/all_to_all | solution.py:362
  196.4 3.2 %copy-start.3 = (f32[1024,1,512]{0,2,1:T(8,128)S(1)}, f32[1024,1,512]{0,2,1:T(8,128)}, u32[]{:S(2)}) copy-start(f32[1024,1,512]{0,2,1:T(8,128)} %get-tuple-element.23) | copy-start | bytes 6291460
  201.5 4.2 %copy-start.5 = (f32[1024,64]{1,0:T(8,128)S(1)}, f32[1024,64]{1,0:T(8,128)}, u32[]{:S(2)}) copy-start(f32[1024,64]{1,0:T(8,128)} %copy-done.4) | copy-start | bytes 786436
  201.5 4.2 %copy-start.7 = (f32[1024,64]{1,0:T(8,128)S(1)}, f32[1024,64]{1,0:T(8,128)}, u32[]{:S(2)}) copy-start(f32[1024,64]{1,0:T(8,128)} %copy-done.6) | copy-start | bytes 786436
Sparse Core Ops, SparseCore 0:
  12.9 49.9 all-gather.1

commit v10 on v9

--- a/solution.py
+++ b/solution.py
@@ -138,7 +138,7 @@
 
 
 def cached_kernel(meta_ref, q_ref, k_ref, v_ref, acc_in, m_in, l_in, o_ref, m_sc, l_sc, acc_sc,
-                  *, groups, block_len):
+                  *, groups, block_len, side):
     c = pl.program_id(1)
     length = meta_ref[1]
     first = meta_ref[2]
@@ -163,7 +163,11 @@
         v = v_ref[...].reshape(tile, HS)
         s = scores_of(q_ref[...], k)
         cols = lax.broadcasted_iota(jnp.int32, (1, tile), 1)
-        src = cols // block_len
+        shift = cols // block_len
+        me = meta_ref[3]
+        src = ((me // side - shift // side + side) % side) * side + (
+            me % side - shift % side + side
+        ) % side
         block = (src - first + groups) % groups + groups * c
         visible = block * block_len + cols % block_len < length
         s = jnp.where(visible, s, -jnp.inf)
@@ -217,7 +221,7 @@
     )(*operands)
 
 
-def cached_attention(meta, queries, received, acc, m, l):
+def cached_attention(meta, queries, received, acc, m, l, side):
     tok_rows, width = queries.shape
     heads = width // HS
     groups, _, per_dev, block_len, _ = received.shape
@@ -234,7 +238,7 @@
     keys_total = groups * per_dev * block_len
     return pl.pallas_call(
         functools.partial(
-            cached_kernel, groups=groups, block_len=block_len
+            cached_kernel, groups=groups, block_len=block_len, side=side
         ),
         out_shape=jax.ShapeDtypeStruct((tok_rows, width), jnp.bfloat16),
         grid_spec=pltpu.PrefetchScalarGridSpec(
@@ -283,6 +287,11 @@
     kv_flat = kv_cache.reshape(2 * slot_count, block_len, local_width)
 
     first_dev = old_table[:, 0] // slot_count
+    side = 4
+    shift_x = targets // side
+    shift_z = targets % side
+    dest_of = lambda src: ((src // side + shift_x) % side) * side + (src + shift_z) % side
+    targets = dest_of(my_index)
     target_req = targets // pair
     c_index = jnp.arange(per_dev, dtype=jnp.int32)
     block_index = ((my_index - first_dev[target_req]) % groups)[:, None] + groups * c_index[None, :]
@@ -295,9 +304,14 @@
     outgoing = jnp.take(kv_flat, out_ids.reshape(-1), axis=0, mode="clip").reshape(
         groups, 2, per_dev, block_len, local_width
     )
-    received = lax.all_to_all(
-        outgoing, ("bx", "bp"), split_axis=0, concat_axis=0, tiled=True
-    )
+    pieces = [outgoing[0]]
+    for k in range(1, groups):
+        route = [
+            (src, ((src // side + k // side) % side) * side + (src + k % side) % side)
+            for src in range(groups)
+        ]
+        pieces.append(lax.ppermute(outgoing[k], ("bx", "bp"), route))
+    received = jnp.stack(pieces)
 
     projected = jnp.einsum(
         "tc,jcw->tjw",
@@ -331,7 +345,7 @@
     )
     value_new = value_new.astype(jnp.bfloat16)
     fresh_kv = jnp.stack([key_new, value_new])
-    meta = jnp.stack([member, cached_len[request], first_dev[request], 0]).astype(jnp.int32)
+    meta = jnp.stack([member, cached_len[request], first_dev[request], my_index]).astype(jnp.int32)
 
     partner_new = lax.ppermute(fresh_kv, "bp", [(0, 1), (1, 0)])
     state = new_attention(meta, queries, fresh_kv[0], fresh_kv[1])
@@ -373,7 +387,7 @@
     )
 
     state = partner_attention(meta, queries, partner_new, state)
-    attended = cached_attention(meta, queries, received, *state)
+    attended = cached_attention(meta, queries, received, *state, side)
     return (attended, updated_cache)
 
 

time: 294 us -> 329 us (1.12)
  the two profiles are of different devices: /device:TPU:110 before, /device:TPU:102 now
where the time goes in v10:
time: 329 us; the launch traced here: 327 us
  waiting for transfers between devices  78.7 us (24%)
  local copies, waits for them, and re-layouts  71.2 us (22%)
  Pallas kernels  70.3 us (21%)
  starting transfers between devices  32.8 us (10%)
  other arithmetic  28.1 us (9%)
  matrix products  17.8 us (5%)
  between operations  14.4 us (4%)
  blocking collectives  14 us (4%)
    ppermute x15, waiting for transfers between devices, body(): pieces.append(lax.ppermute(outgoing[k], ('bx', 'bp'), route))  66.5 us
    pallas_call x1, Pallas kernels, cached_attention(): pl.pallas_call(functools.partial(cached_kernel, groups=groups, block_len=...  39.8 us
    unnamed x51, local copies, waits for them, and re-layouts  31.3 us
    ppermute x15, starting transfers between devices, body(): pieces.append(lax.ppermute(outgoing[k], ('bx', 'bp'), route))  24.9 us
    pallas_call x1, Pallas kernels, new_attention(): pl.pallas_call(functools.partial(new_kernel, partner=partner), out_shape=...  18.5 us
    dot_general x1, matrix products, body(): jnp.einsum('tc,jcw->tjw', lax.all_gather(states, 'head', axis=1, tiled=Tr...  17.8 us
    psum x1, blocking collectives, body(): lax.psum((jnp.sum(queries * queries, axis=1), jnp.sum(key_new * key_new,...  14 us
    ppermute x1, waiting for transfers between devices, body(): partner_new = lax.ppermute(fresh_kv, 'bp', [(0, 1), (1, 0)])  12.2 us
  transfers between devices with their start and end apart: 18, of which 9 were waited for; matrix products, arithmetic and copies ran while one was open for 32% of the time, Pallas kernels for 21%

profile of v10, /device:TPU:102, one launch (start us, length us, event | category | flops | bytes accessed | tf_op | source)
XLA Modules:
  0.0 327.3 jit_solution(17428655023788992604)
XLA Ops:
  7.2 5.5 %copy.42 = bf16[2,40,64,512]{3,2,1,0:T(8,128)(2,1)} copy(bf16[2,40,64,512]{3,2,1,0:T(8,128)(2,1)} %param.10) | data formatting | bytes 10485760
  15.0 9.0 %gather_fusion.2 = bf16[128,64,512]{2,1,0:T(8,128)(2,1)} fusion(bf16[80,64,512]{2,1,0:T(8,128)(2,1)} %bitcast.88, s32[1024]{0:T(1024)S(1)} %pad_clamp_fusion.2), kind=kCustom, calls=%fused_computation.2 | custom fusion | bytes 16777728 | tf_op jit(solution)/shard_map/jit(_take)/gather | solution.py:304
  24.0 7.2 %fusion.43 = (bf16[8,64,512]{2,1,0:T(8,128)(2,1)}, bf16[8,64,512]{2,1,0:T(8,128)(2,1)}, bf16[8,64,512]{2,1,0:T(8,128)(2,1)}, bf16[8,64,512]{2,1,0:T(8,128)(2,1)}...) fusion(bf16[128,64,512]{2,1,0:T(8,128)(2,1)} %gather_fusion.2), kind=kLoop, calls=%fused_computation.167 | loop fusion | bytes 16777216 | tf_op jit(solution)/shard_map/slice | solution.py:313
  33.3 4.0 %collective-permute-start.1 = (bf16[2,4,64,512]{3,2,1,0:T(8,128)(2,1)}, bf16[2,4,64,512]{3,2,1,0:T(8,128)(2,1)}, u32[]{:S(2)}, u32[]{:S(2)}) collective-permute-start(bf16[2,4,64,512]{3,2,1,0:T(8,128)(2,1)} %bitcast.11), channel_id=1, source_target_pairs={{0,2},{1,3},{2,0},{3,1},{4,6},{5,7},{6,4},{7,5},{8,10},{9,11},{10,... | collective-permute-start | bytes 1572872 | tf_op jit(solution)/shard_map/ppermute | solution.py:313
  48.9 18.8 %collective-permute-done = bf16[2,4,64,512]{3,2,1,0:T(8,128)(2,1)} collective-permute-done((bf16[2,4,64,512]{3,2,1,0:T(8,128)(2,1)}, bf16[2,4,64,512]{3,2,1,0:T(8,128)(2,1)}, u32[]{:S(2)}, u32[]{:S(2)}) %collective-permute-start) | collective-permute-done | bytes 524320 | tf_op jit(solution)/shard_map/ppermute | solution.py:313
  79.2 3.3 %collective-permute-done.3 = bf16[2,4,64,512]{3,2,1,0:T(8,128)(2,1)S(1)} collective-permute-done((bf16[2,4,64,512]{3,2,1,0:T(8,128)(2,1)S(1)}, bf16[2,4,64,512]{3,2,1,0:T(8,128)(2,1)S(1)}, u32[]{:S(2)}, u32[]{:S(2)}) %collective-permute-start.3) | collective-permute-done | bytes 524320 | tf_op jit(solution)/shard_map/ppermute | solution.py:313
  82.5 3.5 %collective-permute-start.4 = (bf16[2,4,64,512]{3,2,1,0:T(8,128)(2,1)}, bf16[2,4,64,512]{3,2,1,0:T(8,128)(2,1)}, u32[]{:S(2)}, u32[]{:S(2)}) collective-permute-start(bf16[2,4,64,512]{3,2,1,0:T(8,128)(2,1)} %bitcast.17), channel_id=1, source_target_pairs={{0,5},{1,6},{2,7},{3,4},{4,9},{5,10},{6,11},{7,8},{8,13},{9,14},{1... | collective-permute-start | bytes 1572872 | tf_op jit(solution)/shard_map/ppermute | solution.py:313
  86.8 17.8 %fusion = f32[1024,3,512]{0,2,1:T(8,128)S(1)} fusion(bf16[3,4096,512]{2,1,0:T(8,128)(2,1)} %param.8, bf16[1024,4096]{1,0:T(8,128)(2,1)} %all-gather.2.cloned.1.call-done), kind=kOutput, calls=%fused_computation.7 | convolution fusion | flops 12884901888 | bytes 27262976 | tf_op jit(solution)/shard_map/tc,jcw->tjw/dot_general | solution.py:316
  111.7 14.0 %all-reduce = (f32[1024]{0:T(1024)S(1)}, f32[1024]{0:T(1024)S(1)}) all-reduce(f32[1024]{0:T(1024)S(1)} %get-tuple-element.15, f32[1024]{0:T(1024)S(1)} %get-tuple-element.14), channel_id=1, replica_groups=mesh['head'=8,'bx'=8,'bp'=2] {'head'}, use_global_device_ids=true, to_apply=%region_1.2 | all-reduce | flops 2048 | bytes 16384 | tf_op jit(solution)/shard_map/psum | solution.py:325
  125.8 4.1 %multiply_multiply_fusion = f32[1024,4,128]{2,1,0:T(4,128)S(1)} fusion(f32[1024,4,128]{2,1,0:T(4,128)} %copy.15, f32[4,128]{1,0:T(4,128)S(1)} %bitcast.113, f32[1024]{0:T(1024)S(1)} %get-tuple-element.54), kind=kLoop, calls=%fused_computation.13 | loop fusion | flops 1048576 | bytes 4200448 | tf_op jit(solution)/shard_map/mul | solution.py:330
  150.0 4.8 %collective-permute-done.8 = bf16[2,4,64,512]{3,2,1,0:T(8,128)(2,1)S(1)} collective-permute-done((bf16[2,4,64,512]{3,2,1,0:T(8,128)(2,1)S(1)}, bf16[2,4,64,512]{3,2,1,0:T(8,128)(2,1)S(1)}, u32[]{:S(2)}, u32[]{:S(2)}) %collective-permute-start.8) | collective-permute-done | bytes 524320 | tf_op jit(solution)/shard_map/ppermute | solution.py:313
  155.7 12.0 %collective-permute-done.9 = bf16[2,4,64,512]{3,2,1,0:T(8,128)(2,1)S(1)} collective-permute-done((bf16[2,4,64,512]{3,2,1,0:T(8,128)(2,1)S(1)}, bf16[2,4,64,512]{3,2,1,0:T(8,128)(2,1)S(1)}, u32[]{:S(2)}, u32[]{:S(2)}) %collective-permute-start.9) | collective-permute-done | bytes 524320 | tf_op jit(solution)/shard_map/ppermute | solution.py:313
  170.8 8.7 %collective-permute-done.10 = bf16[2,4,64,512]{3,2,1,0:T(8,128)(2,1)S(1)} collective-permute-done((bf16[2,4,64,512]{3,2,1,0:T(8,128)(2,1)S(1)}, bf16[2,4,64,512]{3,2,1,0:T(8,128)(2,1)S(1)}, u32[]{:S(2)}, u32[]{:S(2)}) %collective-permute-start.10) | collective-permute-done | bytes 524320 | tf_op jit(solution)/shard_map/ppermute | solution.py:313
  180.3 7.7 %collective-permute-done.11 = bf16[2,4,64,512]{3,2,1,0:T(8,128)(2,1)S(1)} collective-permute-done((bf16[2,4,64,512]{3,2,1,0:T(8,128)(2,1)S(1)}, bf16[2,4,64,512]{3,2,1,0:T(8,128)(2,1)S(1)}, u32[]{:S(2)}, u32[]{:S(2)}) %collective-permute-start.11) | collective-permute-done | bytes 524320 | tf_op jit(solution)/shard_map/ppermute | solution.py:313
  188.8 10.0 %collective-permute-done.12 = bf16[2,4,64,512]{3,2,1,0:T(8,128)(2,1)S(1)} collective-permute-done((bf16[2,4,64,512]{3,2,1,0:T(8,128)(2,1)S(1)}, bf16[2,4,64,512]{3,2,1,0:T(8,128)(2,1)S(1)}, u32[]{:S(2)}, u32[]{:S(2)}) %collective-permute-start.12) | collective-permute-done | bytes 524320 | tf_op jit(solution)/shard_map/ppermute | solution.py:313
  199.7 3.6 %gather_fusion.4 = bf16[32,64,512]{2,1,0:T(8,128)(2,1)} fusion(bf16[32,64,512]{2,1,0:T(8,128)(2,1)} %bitcast.45, s32[1024]{0:T(1024)S(1)} %pad_clamp_fusion.1), kind=kCustom, calls=%fused_computation.4 | custom fusion | bytes 4194432 | tf_op jit(solution)/shard_map/jit(_take)/gather | solution.py:368
  203.3 12.2 %collective-permute-done.15.k_ref.v_ref = bf16[2,1024,512]{2,1,0:T(8,128)(2,1)S(1)} collective-permute-done((bf16[2,1024,512]{2,1,0:T(8,128)(2,1)}, bf16[2,1024,512]{2,1,0:T(8,128)(2,1)S(1)}, u32[]{:S(2)}, u32[]{:S(2)}) %collective-permute-start.15) | collective-permute-done | bytes 2097184 | tf_op jit(solution)/shard_map/ppermute | solution.py:350
  217.5 3.8 %broadcast_select_fusion = bf16[8,2,2,64,512]{4,3,2,1,0:T(8,128)(2,1)} fusion(bf16[8,2,2,64,512]{4,3,2,1,0:T(8,128)(2,1)} %bitcast.98, bf16[8,2,2,64,512]{4,3,2,1,0:T(8,128)(2,1)} %bitcast.99, pred[8,2]{1,0:T(8,128)(4,1)S(1)} %compare_or_fusion), kind=kLoop, calls=%fused_computation.19 | loop fusion | flops 1048576 | bytes 6291472 | tf_op jit(solution)/shard_map/jit(_where)/select_n | solution.py:373
  221.3 7.3 %all-to-all-start = ((bf16[8,2,2,64,512]{4,3,2,1,0:T(8,128)(2,1)}), bf16[8,2,2,64,512]{4,3,2,1,0:T(8,128)(2,1)}, u32[]{:S(2)}, u32[]{:S(2)}) async-start(bf16[8,2,2,64,512]{4,3,2,1,0:T(8,128)(2,1)} %broadcast_select_fusion), calls=%async_computation | async-start | bytes 4194304 | tf_op jit(solution)/shard_map/all_to_all | solution.py:376
  235.5 4.2 %multiply_multiply_fusion.1 = f32[1024,4,128]{2,1,0:T(4,128)S(1)} fusion(f32[1024,4,128]{2,1,0:T(4,128)} %copy.14, f32[4,128]{1,0:T(4,128)S(1)} %bitcast.112, f32[1024]{0:T(1024)S(1)} %get-tuple-element.55), kind=kLoop, calls=%fused_computation.17 | loop fusion | flops 1048576 | bytes 4200448 | tf_op jit(solution)/shard_map/mul | solution.py:329
  244.0 18.5 %shard_map.86 = (f32[1024,512]{1,0:T(8,128)}, f32[1024,512]{1,0:T(8,128)}, f32[1024,512]{1,0:T(8,128)}) custom-call(s32[4]{0:T(128)} %pad_add_fusion.meta_ref, bf16[1024,512]{1,0:T(8,128)(2,1)} %bitcast.92, bf16[1024,512]{1,0:T(8,128)(2,1)} %bitcast.104, bf16[1024,512]{1,0:T(8,128)(2,1)} %bitcast.101), custom_call_target="tpu_custom_call" | custom-call | flops 1610612736 | bytes 15728640 | tf_op jit(solution)/shard_map/pallas_call | solution.py:199
  262.5 11.9 %shard_map.87 = (f32[1024,512]{1,0:T(8,128)}, f32[1024,512]{1,0:T(8,128)}, f32[1024,512]{1,0:T(8,128)}) custom-call(s32[4]{0:T(128)} %pad_add_fusion.meta_ref, bf16[1024,512]{1,0:T(8,128)(2,1)} %bitcast.93, bf16[2,1024,512]{2,1,0:T(8,128)(2,1)} %copy-done.2, bf16[2,1024,512]{2,1,0:T(8,128)(2,1)} %copy-done.2, f32[1024,512]{1,0:T(8,128)} %get-tuple-element.8.acc_in, ...), custom_call_target="tpu_custom_call" | custom-call | flops 1073741824 | bytes 15728640 | tf_op jit(solution)/shard_map/pallas_call | solution.py:122
  274.4 39.8 %shard_map.88 = bf16[1024,512]{1,0:T(8,128)(2,1)} custom-call(s32[4]{0:T(128)} %pad_add_fusion.meta_ref, bf16[1024,512]{1,0:T(8,128)(2,1)} %bitcast.94, bf16[16,2,4,64,512]{4,3,2,1,0:T(8,128)(2,1)} %bitcast_dynamic-update-slice_fusion.k_ref.v_ref, bf16[16,2,4,64,512]{4,3,2,1,0:T(8,128)(2,1)} %bitcast_dynamic-update-slice_fusion.k_ref.v_ref, ...), custom_call_target="tpu_custom_call" | custom-call | flops 4294967296 | bytes 12582912 | tf_op jit(solution)/shard_map/pallas_call | solution.py:239
  314.3 6.2 %scatter_fusion = bf16[80,64,512]{2,1,0:T(8,128)(2,1)} fusion(bf16[80,64,512]{2,1,0:T(8,128)(2,1)} %bitcast.89, s32[32]{0:T(128)S(1)} %fusion.40, bf16[32,64,512]{2,1,0:T(8,128)(2,1)} %bitcast.49), kind=kCustom, calls=%fused_computation.6 | custom fusion | bytes 6291584 | tf_op jit(solution)/shard_map/scatter | solution.py:385
  (135 shorter events, 74.9 us)
Async XLA Ops:
  7.2 79.6 %all-gather.2.cloned.1.call-start = ((), (), s32[]{:S(2)}) async-start(), calls=%async_computation.1 | async-start | bytes 9437184 | tf_op jit(solution)/shard_map/all_gather | solution.py:318
  24.0 14.9 %copy-start.15 = (s32[8]{0:T(128)S(1)}, s32[8]{0:T(128)}, u32[]{:S(2)}) copy-start(s32[8]{0:T(128)} %param.11) | copy-start | bytes 100
  24.0 15.5 %copy-start.1 = (s32[8,32]{1,0:T(8,128)S(1)}, s32[8,32]{1,0:T(8,128)}, u32[]{:S(2)}) copy-start(s32[8,32]{1,0:T(8,128)} %param.13) | copy-start | bytes 3076
  31.3 197.3 %collective-permute-start.13 = (bf16[2,4,64,512]{3,2,1,0:T(8,128)(2,1)}, bf16[2,4,64,512]{3,2,1,0:T(8,128)(2,1)}, u32[]{:S(2)}, u32[]{:S(2)}) collective-permute-start(bf16[2,4,64,512]{3,2,1,0:T(8,128)(2,1)} %bitcast.35), channel_id=1, source_target_pairs={{0,14},{1,15},{2,12},{3,13},{4,2},{5,3},{6,0},{7,1},{8,6},{9,7},{1... | collective-permute-start | bytes 1572872 | tf_op jit(solution)/shard_map/ppermute | solution.py:313
  32.1 115.2 %collective-permute-start.7 = (bf16[2,4,64,512]{3,2,1,0:T(8,128)(2,1)}, bf16[2,4,64,512]{3,2,1,0:T(8,128)(2,1)}, u32[]{:S(2)}, u32[]{:S(2)}) collective-permute-start(bf16[2,4,64,512]{3,2,1,0:T(8,128)(2,1)} %bitcast.23), channel_id=1, source_target_pairs={{0,8},{1,9},{2,10},{3,11},{4,12},{5,13},{6,14},{7,15},{8,0},{9,1},... | collective-permute-start | bytes 1572872 | tf_op jit(solution)/shard_map/ppermute | solution.py:313
  33.2 42.5 %collective-permute-start.2 = (bf16[2,4,64,512]{3,2,1,0:T(8,128)(2,1)S(1)}, bf16[2,4,64,512]{3,2,1,0:T(8,128)(2,1)}, u32[]{:S(2)}, u32[]{:S(2)}) collective-permute-start(bf16[2,4,64,512]{3,2,1,0:T(8,128)(2,1)S(1)} %bitcast.111), channel_id=1, source_target_pairs={{0,3},{1,0},{2,1},{3,2},{4,7},{5,4},{6,5},{7,6},{8,11},{9,8},{10,9... | collective-permute-start | bytes 1572872 | tf_op jit(solution)/shard_map/ppermute | solution.py:313
  33.3 37.6 %collective-permute-start.1 = (bf16[2,4,64,512]{3,2,1,0:T(8,128)(2,1)}, bf16[2,4,64,512]{3,2,1,0:T(8,128)(2,1)}, u32[]{:S(2)}, u32[]{:S(2)}) collective-permute-start(bf16[2,4,64,512]{3,2,1,0:T(8,128)(2,1)} %bitcast.11), channel_id=1, source_target_pairs={{0,2},{1,3},{2,0},{3,1},{4,6},{5,7},{6,4},{7,5},{8,10},{9,11},{10,... | collective-permute-start | bytes 1572872 | tf_op jit(solution)/shard_map/ppermute | solution.py:313
  37.2 30.4 %collective-permute-start = (bf16[2,4,64,512]{3,2,1,0:T(8,128)(2,1)}, bf16[2,4,64,512]{3,2,1,0:T(8,128)(2,1)}, u32[]{:S(2)}, u32[]{:S(2)}) collective-permute-start(bf16[2,4,64,512]{3,2,1,0:T(8,128)(2,1)} %bitcast.9), channel_id=1, source_target_pairs={{0,1},{1,2},{2,3},{3,0},{4,5},{5,6},{6,7},{7,4},{8,9},{9,10},{10,1... | collective-permute-start | bytes 1572872 | tf_op jit(solution)/shard_map/ppermute | solution.py:313
  45.3 84.6 %copy-start.4 = (f32[1024,64]{1,0:T(8,128)}, f32[1024,64]{1,0:T(8,128)S(1)}, u32[]{:S(2)}) copy-start(f32[1024,64]{1,0:T(8,128)S(1)} %get-tuple-element.44) | copy-start | bytes 786436
  45.3 84.6 %copy-start.6 = (f32[1024,64]{1,0:T(8,128)}, f32[1024,64]{1,0:T(8,128)S(1)}, u32[]{:S(2)}) copy-start(f32[1024,64]{1,0:T(8,128)S(1)} %get-tuple-element.45) | copy-start | bytes 786436
  67.7 14.8 %collective-permute-start.3 = (bf16[2,4,64,512]{3,2,1,0:T(8,128)(2,1)S(1)}, bf16[2,4,64,512]{3,2,1,0:T(8,128)(2,1)S(1)}, u32[]{:S(2)}, u32[]{:S(2)}) collective-permute-start(bf16[2,4,64,512]{3,2,1,0:T(8,128)(2,1)S(1)} %bitcast.110), channel_id=1, source_target_pairs={{0,4},{1,5},{2,6},{3,7},{4,8},{5,9},{6,10},{7,11},{8,12},{9,13},{1... | collective-permute-start | bytes 1572872 | tf_op jit(solution)/shard_map/ppermute | solution.py:313
  70.9 71.4 %collective-permute-start.6 = (bf16[2,4,64,512]{3,2,1,0:T(8,128)(2,1)}, bf16[2,4,64,512]{3,2,1,0:T(8,128)(2,1)}, u32[]{:S(2)}, u32[]{:S(2)}) collective-permute-start(bf16[2,4,64,512]{3,2,1,0:T(8,128)(2,1)} %bitcast.21), channel_id=1, source_target_pairs={{0,7},{1,4},{2,5},{3,6},{4,11},{5,8},{6,9},{7,10},{8,15},{9,12},{1... | collective-permute-start | bytes 1572872 | tf_op jit(solution)/shard_map/ppermute | solution.py:313
  75.7 61.7 %collective-permute-start.5 = (bf16[2,4,64,512]{3,2,1,0:T(8,128)(2,1)}, bf16[2,4,64,512]{3,2,1,0:T(8,128)(2,1)}, u32[]{:S(2)}, u32[]{:S(2)}) collective-permute-start(bf16[2,4,64,512]{3,2,1,0:T(8,128)(2,1)} %bitcast.19), channel_id=1, source_target_pairs={{0,6},{1,7},{2,4},{3,5},{4,10},{5,11},{6,8},{7,9},{8,14},{9,15},{1... | collective-permute-start | bytes 1572872 | tf_op jit(solution)/shard_map/ppermute | solution.py:313
  82.5 52.6 %collective-permute-start.4 = (bf16[2,4,64,512]{3,2,1,0:T(8,128)(2,1)}, bf16[2,4,64,512]{3,2,1,0:T(8,128)(2,1)}, u32[]{:S(2)}, u32[]{:S(2)}) collective-permute-start(bf16[2,4,64,512]{3,2,1,0:T(8,128)(2,1)} %bitcast.17), channel_id=1, source_target_pairs={{0,5},{1,6},{2,7},{3,4},{4,9},{5,10},{6,11},{7,8},{8,13},{9,14},{1... | collective-permute-start | bytes 1572872 | tf_op jit(solution)/shard_map/ppermute | solution.py:313
  135.0 19.8 %copy-start.10 = (bf16[8,64,512]{2,1,0:T(8,128)(2,1)S(1)}, bf16[8,64,512]{2,1,0:T(8,128)(2,1)}, u32[]{:S(2)}) copy-start(bf16[8,64,512]{2,1,0:T(8,128)(2,1)} %get-tuple-element.25) | copy-start | bytes 1572868
  135.0 80.4 %collective-permute-start.15 = (bf16[2,1024,512]{2,1,0:T(8,128)(2,1)}, bf16[2,1024,512]{2,1,0:T(8,128)(2,1)S(1)}, u32[]{:S(2)}, u32[]{:S(2)}) collective-permute-start(bf16[2,1024,512]{2,1,0:T(8,128)(2,1)} %pad_maximum_fusion), channel_id=1, source_target_pairs={{0,1},{1,0},{2,3},{3,2},{4,5},{5,4},{6,7},{7,6},{8,9},{9,8},{10,11... | collective-permute-start | bytes 6291464 | tf_op jit(solution)/shard_map/ppermute | solution.py:350
  137.4 30.2 %copy-start.9 = (bf16[8,64,512]{2,1,0:T(8,128)(2,1)S(1)}, bf16[8,64,512]{2,1,0:T(8,128)(2,1)}, u32[]{:S(2)}) copy-start(bf16[8,64,512]{2,1,0:T(8,128)(2,1)} %get-tuple-element.24) | copy-start | bytes 1572868
  137.5 17.4 %collective-permute-start.8 = (bf16[2,4,64,512]{3,2,1,0:T(8,128)(2,1)S(1)}, bf16[2,4,64,512]{3,2,1,0:T(8,128)(2,1)S(1)}, u32[]{:S(2)}, u32[]{:S(2)}) collective-permute-start(bf16[2,4,64,512]{3,2,1,0:T(8,128)(2,1)S(1)} %bitcast.109), channel_id=1, source_target_pairs={{0,9},{1,10},{2,11},{3,8},{4,13},{5,14},{6,15},{7,12},{8,1},{9,2},... | collective-permute-start | bytes 1572872 | tf_op jit(solution)/shard_map/ppermute | solution.py:313
  142.3 25.4 %collective-permute-start.9 = (bf16[2,4,64,512]{3,2,1,0:T(8,128)(2,1)S(1)}, bf16[2,4,64,512]{3,2,1,0:T(8,128)(2,1)S(1)}, u32[]{:S(2)}, u32[]{:S(2)}) collective-permute-start(bf16[2,4,64,512]{3,2,1,0:T(8,128)(2,1)S(1)} %bitcast.108), channel_id=1, source_target_pairs={{0,10},{1,11},{2,8},{3,9},{4,14},{5,15},{6,12},{7,13},{8,2},{9,3},... | collective-permute-start | bytes 1572872 | tf_op jit(solution)/shard_map/ppermute | solution.py:313
  147.3 32.1 %collective-permute-start.10 = (bf16[2,4,64,512]{3,2,1,0:T(8,128)(2,1)S(1)}, bf16[2,4,64,512]{3,2,1,0:T(8,128)(2,1)S(1)}, u32[]{:S(2)}, u32[]{:S(2)}) collective-permute-start(bf16[2,4,64,512]{3,2,1,0:T(8,128)(2,1)S(1)} %bitcast.107), channel_id=1, source_target_pairs={{0,11},{1,8},{2,9},{3,10},{4,15},{5,12},{6,13},{7,14},{8,3},{9,0},... | collective-permute-start | bytes 1572872 | tf_op jit(solution)/shard_map/ppermute | solution.py:313
  154.8 33.1 %collective-permute-start.11 = (bf16[2,4,64,512]{3,2,1,0:T(8,128)(2,1)S(1)}, bf16[2,4,64,512]{3,2,1,0:T(8,128)(2,1)S(1)}, u32[]{:S(2)}, u32[]{:S(2)}) collective-permute-start(bf16[2,4,64,512]{3,2,1,0:T(8,128)(2,1)S(1)} %bitcast.106), channel_id=1, source_target_pairs={{0,12},{1,13},{2,14},{3,15},{4,0},{5,1},{6,2},{7,3},{8,4},{9,5},{1... | collective-permute-start | bytes 1572872 | tf_op jit(solution)/shard_map/ppermute | solution.py:313
  167.7 31.2 %collective-permute-start.12 = (bf16[2,4,64,512]{3,2,1,0:T(8,128)(2,1)S(1)}, bf16[2,4,64,512]{3,2,1,0:T(8,128)(2,1)S(1)}, u32[]{:S(2)}, u32[]{:S(2)}) collective-permute-start(bf16[2,4,64,512]{3,2,1,0:T(8,128)(2,1)S(1)} %bitcast.105), channel_id=1, source_target_pairs={{0,13},{1,14},{2,15},{3,12},{4,1},{5,2},{6,3},{7,0},{8,5},{9,6},{1... | collective-permute-start | bytes 1572872 | tf_op jit(solution)/shard_map/ppermute | solution.py:313
  179.5 51.2 %collective-permute-start.14 = (bf16[2,4,64,512]{3,2,1,0:T(8,128)(2,1)}, bf16[2,4,64,512]{3,2,1,0:T(8,128)(2,1)}, u32[]{:S(2)}, u32[]{:S(2)}) collective-permute-start(bf16[2,4,64,512]{3,2,1,0:T(8,128)(2,1)} %bitcast.37), channel_id=1, source_target_pairs={{0,15},{1,12},{2,13},{3,14},{4,3},{5,0},{6,1},{7,2},{8,7},{9,4},{1... | collective-permute-start | bytes 1572872 | tf_op jit(solution)/shard_map/ppermute | solution.py:313
  221.3 93.0 %all-to-all-start = ((bf16[8,2,2,64,512]{4,3,2,1,0:T(8,128)(2,1)}), bf16[8,2,2,64,512]{4,3,2,1,0:T(8,128)(2,1)}, u32[]{:S(2)}, u32[]{:S(2)}) async-start(bf16[8,2,2,64,512]{4,3,2,1,0:T(8,128)(2,1)} %broadcast_select_fusion), calls=%async_computation | async-start | bytes 4194304 | tf_op jit(solution)/shard_map/all_to_all | solution.py:376
  (10 other events, 49.2 us)
Sparse Core Ops, SparseCore 0:
  12.9 50.8 all-gather.1

commit v11 on v9

--- a/solution.py
+++ b/solution.py
@@ -264,6 +264,24 @@
     )(meta, queries, received, received, acc, m, l)
 
 
+def copy_kernel(src_ref, dst_ref):
+    dst_ref[...] = src_ref[...]
+
+
+def cache_copy(cache):
+    kinds, slots, rows, width = cache.shape
+    step = 8
+    spec = pl.BlockSpec((1, step, rows, width), lambda k, i: (k, i, 0, 0))
+    return pl.pallas_call(
+        copy_kernel,
+        out_shape=jax.ShapeDtypeStruct(cache.shape, cache.dtype),
+        grid=(kinds, slots // step),
+        in_specs=[spec],
+        out_specs=spec,
+        cost_estimate=pl.CostEstimate(flops=0, transcendentals=0, bytes_accessed=2 * cache.size * 2),
+    )(cache)
+
+
 def body(states, qkv_weight, norm_gains, kv_cache, cached_len, old_table, new_table):
     tok_rows = states.shape[0]
     half_rows = tok_rows // 2
@@ -366,8 +384,9 @@
         - my_index * slot_count
     )
     target_ids = kv_ids[None, :, None] * slot_count + target_slot[:, None, :]
+    base = cache_copy(kv_cache).reshape(kv_flat.shape)
     updated_cache = (
-        kv_flat.at[target_ids.reshape(-1)]
+        base.at[target_ids.reshape(-1)]
         .set(arrived.reshape(-1, block_len, local_width), mode="drop")
         .reshape(kv_cache.shape)
     )

time: 294 us -> 291 us (0.990)
  the two profiles are of different devices: /device:TPU:110 before, /device:TPU:118 now
where the time goes in v11:
time: 291 us; the launch traced here: 290 us
  waiting for transfers between devices  79.1 us (27%)
  Pallas kernels  78.2 us (27%)
  local copies, waits for them, and re-layouts  36.1 us (12%)
  other arithmetic  31.6 us (11%)
  starting transfers between devices  20.6 us (7%)
  matrix products  17.8 us (6%)
  between operations  14.4 us (5%)
  blocking collectives  11.9 us (4%)
    ppermute x1, waiting for transfers between devices, body(): partner_new = lax.ppermute(fresh_kv, 'bp', [(0, 1), (1, 0)])  58.4 us
    pallas_call x1, Pallas kernels, cached_attention(): pl.pallas_call(functools.partial(cached_kernel, groups=groups, block_len=...  39.8 us
    all_gather x1, waiting for transfers between devices, body(): lax.all_gather(states, 'head', axis=1, tiled=True)  19.9 us
    pallas_call x1, Pallas kernels, new_attention(): pl.pallas_call(functools.partial(new_kernel, partner=partner), out_shape=...  18.5 us
    dot_general x1, matrix products, body(): jnp.einsum('tc,jcw->tjw', lax.all_gather(states, 'head', axis=1, tiled=Tr...  17.8 us
    all_to_all x1, starting transfers between devices, body(): lax.all_to_all(picked, 'bx', split_axis=0, concat_axis=0, tiled=True)  12.8 us
    pallas_call x1, Pallas kernels, partner_attention(): pl.pallas_call(partner_kernel, out_shape=(shape, shape, shape), grid_spec...  11.9 us
    psum x1, blocking collectives, body(): lax.psum((jnp.sum(queries * queries, axis=1), jnp.sum(key_new * key_new,...  11.9 us
  transfers between devices with their start and end apart: 4, of which 2 were waited for; matrix products, arithmetic and copies ran while one was open for 26% of the time, Pallas kernels for 27%

profile of v11, /device:TPU:118, one launch (start us, length us, event | category | flops | bytes accessed | tf_op | source)
XLA Modules:
  0.0 289.7 jit_solution(2303943177658466708)
XLA Ops:
  11.5 9.0 %gather_fusion.2 = bf16[128,64,512]{2,1,0:T(8,128)(2,1)} fusion(bf16[80,64,512]{2,1,0:T(8,128)(2,1)} %bitcast.42, s32[1024]{0:T(1024)S(1)} %pad_clamp_fusion.2), kind=kCustom, calls=%fused_computation.2 | custom fusion | bytes 16777728 | tf_op jit(solution)/shard_map/jit(_take)/gather | solution.py:313
  20.5 7.0 %all-to-all-start = ((bf16[16,2,4,64,512]{4,3,2,1,0:T(8,128)(2,1)}), bf16[16,2,4,64,512]{4,3,2,1,0:T(8,128)(2,1)}, u32[]{:S(2)}, u32[]{:S(2)}) async-start(bf16[16,2,4,64,512]{4,3,2,1,0:T(8,128)(2,1)} %bitcast.43), calls=%async_computation | async-start | bytes 16777216 | tf_op jit(solution)/shard_map/all_to_all | solution.py:316
  27.7 8.0 %shard_map.89 = bf16[2,40,64,512]{3,2,1,0:T(8,128)(2,1)} custom-call(bf16[2,40,64,512]{3,2,1,0:T(8,128)(2,1)} %src_ref.1), custom_call_target="tpu_custom_call" | custom-call | bytes 10485760 | tf_op jit(solution)/shard_map/pallas_call | solution.py:275
  37.5 1.9 multiply_cosine_fusion
  39.4 19.9 %all-gather.2.cloned.1.call-done = bf16[1024,4096]{1,0:T(8,128)(2,1)} async-done(((bf16[1024,512]{1,0:T(8,128)(2,1)}), bf16[1024,4096]{1,0:T(8,128)(2,1)}) %all-gather.2.cloned.1.call-update) | async-done | bytes 8388624 | tf_op jit(solution)/shard_map/all_gather | solution.py:322
  59.3 17.8 %fusion = f32[1024,3,512]{0,2,1:T(8,128)S(1)} fusion(bf16[3,4096,512]{2,1,0:T(8,128)(2,1)} %param.8, bf16[1024,4096]{1,0:T(8,128)(2,1)} %all-gather.2.cloned.1.call-done), kind=kOutput, calls=%fused_computation.7 | convolution fusion | flops 12884901888 | bytes 27262976 | tf_op jit(solution)/shard_map/tc,jcw->tjw/dot_general | solution.py:320
  77.1 2.7 copy-done.8
  81.3 4.2 %multiply_reduce_fusion = (f32[1024]{0:T(1024)S(1)}, f32[1024]{0:T(1024)S(1)}, f32[1024,1,512]{0,2,1:T(8,128)S(1)}, f32[1024,1,512]{0,2,1:T(8,128)}) fusion(f32[1024,3,512]{0,2,1:T(8,128)} %copy-done.8), kind=kLoop, calls=%fused_computation.14 | loop fusion | flops 2095104 | bytes 8396800 | tf_op jit(solution)/shard_map/reduce_sum | solution.py:330
  85.5 1.9 copy.15
  87.3 11.9 %all-reduce = (f32[1024]{0:T(1024)S(1)}, f32[1024]{0:T(1024)S(1)}) all-reduce(f32[1024]{0:T(1024)S(1)} %get-tuple-element.15, f32[1024]{0:T(1024)S(1)} %get-tuple-element.14), channel_id=1, replica_groups=mesh['head'=8,'bx'=8,'bp'=2] {'head'}, use_global_device_ids=true, to_apply=%region_1.2 | all-reduce | flops 2048 | bytes 16384 | tf_op jit(solution)/shard_map/psum | solution.py:329
  99.2 4.1 %multiply_multiply_fusion = f32[1024,4,128]{2,1,0:T(4,128)S(1)} fusion(f32[1024,4,128]{2,1,0:T(4,128)} %copy.15, f32[4,128]{1,0:T(4,128)S(1)} %bitcast.60, f32[1024]{0:T(1024)S(1)} %get-tuple-element.36), kind=kLoop, calls=%fused_computation.13 | loop fusion | flops 1048576 | bytes 4200448 | tf_op jit(solution)/shard_map/mul | solution.py:334
  103.3 1.7 multiply_subtract_fusion
  112.3 3.6 %gather_fusion.4 = bf16[32,64,512]{2,1,0:T(8,128)(2,1)} fusion(bf16[32,64,512]{2,1,0:T(8,128)(2,1)} %bitcast.15, s32[1024]{0:T(1024)S(1)} %pad_clamp_fusion.1), kind=kCustom, calls=%fused_computation.4 | custom fusion | bytes 4194432 | tf_op jit(solution)/shard_map/jit(_take)/gather | solution.py:372
  115.9 58.4 %collective-permute-done.k_ref.v_ref = bf16[2,1024,512]{2,1,0:T(8,128)(2,1)S(1)} collective-permute-done((bf16[2,1024,512]{2,1,0:T(8,128)(2,1)}, bf16[2,1024,512]{2,1,0:T(8,128)(2,1)S(1)}, u32[]{:S(2)}, u32[]{:S(2)}) %collective-permute-start) | collective-permute-done | bytes 2097184 | tf_op jit(solution)/shard_map/ppermute | solution.py:354
  174.4 2.1 gather_fusion.5
  176.4 3.8 %broadcast_select_fusion = bf16[8,2,2,64,512]{4,3,2,1,0:T(8,128)(2,1)} fusion(bf16[8,2,2,64,512]{4,3,2,1,0:T(8,128)(2,1)} %bitcast.53, bf16[8,2,2,64,512]{4,3,2,1,0:T(8,128)(2,1)} %bitcast.54, pred[8,2]{1,0:T(8,128)(4,1)S(1)} %compare_or_fusion), kind=kLoop, calls=%fused_computation.19 | loop fusion | flops 1048576 | bytes 6291472 | tf_op jit(solution)/shard_map/jit(_where)/select_n | solution.py:377
  180.3 12.8 %all-to-all-start.1 = ((bf16[8,2,2,64,512]{4,3,2,1,0:T(8,128)(2,1)}), bf16[8,2,2,64,512]{4,3,2,1,0:T(8,128)(2,1)}, u32[]{:S(2)}, u32[]{:S(2)}) async-start(bf16[8,2,2,64,512]{4,3,2,1,0:T(8,128)(2,1)} %broadcast_select_fusion), calls=%async_computation.1 | async-start | bytes 4194304 | tf_op jit(solution)/shard_map/all_to_all | solution.py:380
  193.1 1.8 pad_add_fusion.meta_ref
  194.9 1.8 copy.14
  196.8 4.2 %multiply_multiply_fusion.1 = f32[1024,4,128]{2,1,0:T(4,128)S(1)} fusion(f32[1024,4,128]{2,1,0:T(4,128)} %copy.14, f32[4,128]{1,0:T(4,128)S(1)} %bitcast.59, f32[1024]{0:T(1024)S(1)} %get-tuple-element.37), kind=kLoop, calls=%fused_computation.17 | loop fusion | flops 1048576 | bytes 4200448 | tf_op jit(solution)/shard_map/mul | solution.py:333
  206.4 18.5 %shard_map.86 = (f32[1024,512]{1,0:T(8,128)}, f32[1024,512]{1,0:T(8,128)}, f32[1024,512]{1,0:T(8,128)}) custom-call(s32[4]{0:T(128)} %pad_add_fusion.meta_ref, bf16[1024,512]{1,0:T(8,128)(2,1)} %bitcast.47, bf16[1024,512]{1,0:T(8,128)(2,1)} %bitcast.58, bf16[1024,512]{1,0:T(8,128)(2,1)} %bitcast.56), custom_call_target="tpu_custom_call" | custom-call | flops 1610612736 | bytes 15728640 | tf_op jit(solution)/shard_map/pallas_call | solution.py:195
  224.9 11.9 %shard_map.87 = (f32[1024,512]{1,0:T(8,128)}, f32[1024,512]{1,0:T(8,128)}, f32[1024,512]{1,0:T(8,128)}) custom-call(s32[4]{0:T(128)} %pad_add_fusion.meta_ref, bf16[1024,512]{1,0:T(8,128)(2,1)} %bitcast.48, bf16[2,1024,512]{2,1,0:T(8,128)(2,1)} %copy-done.2, bf16[2,1024,512]{2,1,0:T(8,128)(2,1)} %copy-done.2, f32[1024,512]{1,0:T(8,128)} %get-tuple-element.8.acc_in, ...), custom_call_target="tpu_custom_call" | custom-call | flops 1073741824 | bytes 15728640 | tf_op jit(solution)/shard_map/pallas_call | solution.py:122
  236.8 39.8 %shard_map.88 = bf16[1024,512]{1,0:T(8,128)(2,1)} custom-call(s32[4]{0:T(128)} %pad_add_fusion.meta_ref, bf16[1024,512]{1,0:T(8,128)(2,1)} %bitcast.49, bf16[16,2,4,64,512]{4,3,2,1,0:T(8,128)(2,1)} %all-to-all-done.k_ref.v_ref, bf16[16,2,4,64,512]{4,3,2,1,0:T(8,128)(2,1)} %all-to-all-done.k_ref.v_ref, f32[1024,512]{1,0:T(8,128)} %get-tuple-element.11.acc_in, ...), custom_call_target="tpu_custom_call" | custom-call | flops 4294967296 | bytes 12582912 | tf_op jit(solution)/shard_map/pallas_call | solution.py:235
  276.7 6.2 %scatter_fusion = bf16[80,64,512]{2,1,0:T(8,128)(2,1)} fusion(bf16[80,64,512]{2,1,0:T(8,128)(2,1)} %bitcast.45, s32[32]{0:T(128)S(1)} %fusion.28, bf16[32,64,512]{2,1,0:T(8,128)(2,1)} %bitcast.19), kind=kCustom, calls=%fused_computation.6 | custom fusion | bytes 6291584 | tf_op jit(solution)/shard_map/scatter | solution.py:390
  (83 shorter events, 20.3 us)
Async XLA Ops:
  7.2 3.3 %copy-start = (s32[8,64]{1,0:T(8,128)S(1)}, s32[8,64]{1,0:T(8,128)}, u32[]{:S(2)}) copy-start(s32[8,64]{1,0:T(8,128)} %param.12) | copy-start | bytes 6148
  7.2 52.2 %all-gather.2.cloned.1.call-start = ((), (), s32[]{:S(2)}) async-start(), calls=%async_computation.2 | async-start | bytes 9437184 | tf_op jit(solution)/shard_map/all_gather | solution.py:322
  20.5 7.0 %copy-start.1 = (s32[8,32]{1,0:T(8,128)S(1)}, s32[8,32]{1,0:T(8,128)}, u32[]{:S(2)}) copy-start(s32[8,32]{1,0:T(8,128)} %param.13) | copy-start | bytes 3076
  20.5 7.2 %copy-start.10 = (bf16[2,512]{1,0:T(2,128)(2,1)S(1)}, bf16[2,512]{1,0:T(2,128)(2,1)}, u32[]{:S(2)}) copy-start(bf16[2,512]{1,0:T(2,128)(2,1)} %param.9) | copy-start | bytes 6148
  20.5 159.8 %all-to-all-start = ((bf16[16,2,4,64,512]{4,3,2,1,0:T(8,128)(2,1)}), bf16[16,2,4,64,512]{4,3,2,1,0:T(8,128)(2,1)}, u32[]{:S(2)}, u32[]{:S(2)}) async-start(bf16[16,2,4,64,512]{4,3,2,1,0:T(8,128)(2,1)} %bitcast.43), calls=%async_computation | async-start | bytes 16777216 | tf_op jit(solution)/shard_map/all_to_all | solution.py:316
  27.7 8.6 %copy-start.11 = (s32[8]{0:T(128)S(1)}, s32[8]{0:T(128)}, u32[]{:S(2)}) copy-start(s32[8]{0:T(128)} %param.11) | copy-start | bytes 100
  39.4 63.9 %copy-start.4 = (f32[1024,64]{1,0:T(8,128)}, f32[1024,64]{1,0:T(8,128)S(1)}, u32[]{:S(2)}) copy-start(f32[1024,64]{1,0:T(8,128)S(1)} %get-tuple-element.28) | copy-start | bytes 786436
  39.4 63.9 %copy-start.6 = (f32[1024,64]{1,0:T(8,128)}, f32[1024,64]{1,0:T(8,128)S(1)}, u32[]{:S(2)}) copy-start(f32[1024,64]{1,0:T(8,128)S(1)} %get-tuple-element.29) | copy-start | bytes 786436
  77.1 2.7 copy-start.8
  105.1 1.9 copy-start.9
  108.5 65.9 %collective-permute-start = (bf16[2,1024,512]{2,1,0:T(8,128)(2,1)}, bf16[2,1024,512]{2,1,0:T(8,128)(2,1)S(1)}, u32[]{:S(2)}, u32[]{:S(2)}) collective-permute-start(bf16[2,1024,512]{2,1,0:T(8,128)(2,1)} %pad_maximum_fusion), channel_id=1, source_target_pairs={{0,1},{1,0},{2,3},{3,2},{4,5},{5,4},{6,7},{7,6},{8,9},{9,8},{10,11... | collective-permute-start | bytes 6291464 | tf_op jit(solution)/shard_map/ppermute | solution.py:354
  174.4 2.1 copy-start.2
  180.3 14.7 %copy-start.3 = (f32[1024,1,512]{0,2,1:T(8,128)S(1)}, f32[1024,1,512]{0,2,1:T(8,128)}, u32[]{:S(2)}) copy-start(f32[1024,1,512]{0,2,1:T(8,128)} %get-tuple-element.23) | copy-start | bytes 6291460
  180.3 96.4 %all-to-all-start.1 = ((bf16[8,2,2,64,512]{4,3,2,1,0:T(8,128)(2,1)}), bf16[8,2,2,64,512]{4,3,2,1,0:T(8,128)(2,1)}, u32[]{:S(2)}, u32[]{:S(2)}) async-start(bf16[8,2,2,64,512]{4,3,2,1,0:T(8,128)(2,1)} %broadcast_select_fusion), calls=%async_computation.1 | async-start | bytes 4194304 | tf_op jit(solution)/shard_map/all_to_all | solution.py:380
  196.8 4.2 %copy-start.5 = (f32[1024,64]{1,0:T(8,128)S(1)}, f32[1024,64]{1,0:T(8,128)}, u32[]{:S(2)}) copy-start(f32[1024,64]{1,0:T(8,128)} %copy-done.4) | copy-start | bytes 786436
  196.8 4.2 %copy-start.7 = (f32[1024,64]{1,0:T(8,128)S(1)}, f32[1024,64]{1,0:T(8,128)}, u32[]{:S(2)}) copy-start(f32[1024,64]{1,0:T(8,128)} %copy-done.6) | copy-start | bytes 786436
Sparse Core Ops, SparseCore 0:
  9.7 49.6 all-gather.1

commit v12 on v11

--- a/solution.py
+++ b/solution.py
@@ -88,67 +88,33 @@
         l_out[...] = l_sc[...]
 
 
-def partner_kernel(meta_ref, q_ref, k_ref, v_ref, acc_in, m_in, l_in, acc_out, m_out, l_out):
-    k_ref = k_ref.at[0]
-    v_ref = v_ref.at[0]
-    member = meta_ref[0]
-    rows = q_ref.shape[0]
-    half = rows // 2
-    acc_out[...] = acc_in[...]
-    m_out[...] = m_in[...]
-    l_out[...] = l_in[...]
-
-    @pl.when(member == 0)
-    def _():
-        s = scores_of(q_ref[pl.ds(half, half), :], k_ref[...])
-        online_update(
-            s, v_ref[...], m_out.at[pl.ds(half, half)], l_out.at[pl.ds(half, half)],
-            acc_out.at[pl.ds(half, half)],
-        )
-
-    @pl.when(member != 0)
-    def _():
-        s = scores_of(q_ref[...], k_ref[pl.ds(0, half), :])
-        online_update(s, v_ref[pl.ds(0, half), :], m_out, l_out, acc_out)
-
-
-def partner_attention(meta, queries, partner_new, state):
-    tok_rows, width = queries.shape
-    heads = width // HS
-    shape = jax.ShapeDtypeStruct((tok_rows, width), jnp.float32)
-    spec = pl.BlockSpec((tok_rows, HS), lambda h, meta: (0, h))
-    key_spec = pl.BlockSpec((1, tok_rows, HS), lambda h, meta: (0, 0, h))
-    value_spec = pl.BlockSpec((1, tok_rows, HS), lambda h, meta: (1, 0, h))
-    return pl.pallas_call(
-        partner_kernel,
-        out_shape=(shape, shape, shape),
-        grid_spec=pltpu.PrefetchScalarGridSpec(
-            num_scalar_prefetch=1,
-            grid=(heads,),
-            in_specs=[spec, key_spec, value_spec, spec, spec, spec],
-            out_specs=[spec] * 3,
-        ),
-        compiler_params=pltpu.CompilerParams(dimension_semantics=("arbitrary",)),
-        cost_estimate=pl.CostEstimate(
-            flops=2 * 2 * tok_rows * tok_rows * width // 2,
-            transcendentals=tok_rows * tok_rows * heads // 2,
-            bytes_accessed=3 * 2 * tok_rows * width + 6 * 4 * tok_rows * width,
-        ),
-    )(meta, queries, partner_new, partner_new, *state)
-
-
-def cached_kernel(meta_ref, q_ref, k_ref, v_ref, acc_in, m_in, l_in, o_ref, m_sc, l_sc, acc_sc,
-                  *, groups, block_len):
+def cached_kernel(meta_ref, q_ref, pk_ref, pv_ref, k_ref, v_ref, acc_in, m_in, l_in, o_ref,
+                  m_sc, l_sc, acc_sc, *, groups, block_len):
     c = pl.program_id(1)
     length = meta_ref[1]
     first = meta_ref[2]
     tile = groups * block_len
+    member = meta_ref[0]
+    half = q_ref.shape[0] // 2
 
     @pl.when(c == 0)
     def _():
         m_sc[...] = m_in[...]
         l_sc[...] = l_in[...]
         acc_sc[...] = acc_in[...]
+
+    @pl.when((c == 0) & (member == 0))
+    def _():
+        s = scores_of(q_ref[pl.ds(half, half), :], pk_ref[0])
+        online_update(
+            s, pv_ref[0], m_sc.at[pl.ds(half, half)], l_sc.at[pl.ds(half, half)],
+            acc_sc.at[pl.ds(half, half)],
+        )
+
+    @pl.when((c == 0) & (member != 0))
+    def _():
+        s = scores_of(q_ref[...], pk_ref[0, pl.ds(0, half), :])
+        online_update(s, pv_ref[0, pl.ds(0, half), :], m_sc, l_sc, acc_sc)
 
     @pl.when((c + 1) * groups * block_len <= length)
     def _():
@@ -217,7 +183,7 @@
     )(*operands)
 
 
-def cached_attention(meta, queries, received, acc, m, l):
+def cached_attention(meta, queries, partner_new, received, acc, m, l):
     tok_rows, width = queries.shape
     heads = width // HS
     groups, _, per_dev, block_len, _ = received.shape
@@ -242,6 +208,8 @@
             grid=(heads, per_dev),
             in_specs=[
                 pl.BlockSpec((tok_rows, HS), lambda h, c, meta: (0, h)),
+                pl.BlockSpec((1, tok_rows, HS), lambda h, c, meta: (0, 0, h)),
+                pl.BlockSpec((1, tok_rows, HS), lambda h, c, meta: (1, 0, h)),
                 pl.BlockSpec(kv_block, kv_map(0)),
                 pl.BlockSpec(kv_block, kv_map(1)),
                 state_spec,
@@ -261,7 +229,7 @@
             transcendentals=tok_rows * keys_total * heads // 2,
             bytes_accessed=2 * keys_total * width + 2 * tok_rows * width * 2 + 3 * 4 * tok_rows * width,
         ),
-    )(meta, queries, received, received, acc, m, l)
+    )(meta, queries, partner_new, partner_new, received, received, acc, m, l)
 
 
 def copy_kernel(src_ref, dst_ref):
@@ -391,8 +359,7 @@
         .reshape(kv_cache.shape)
     )
 
-    state = partner_attention(meta, queries, partner_new, state)
-    attended = cached_attention(meta, queries, received, *state)
+    attended = cached_attention(meta, queries, partner_new, received, *state)
     return (attended, updated_cache)
 
 

time: 291 us -> 296 us (1.017)
  waiting for transfers between devices: 79.1 us -> 87.7 us
  Pallas kernels: 78.2 us -> 74.5 us
    pallas_call x1 -> x0, Pallas kernels: 11.9 us -> none  [partner_attention(): pl.pallas_call(partner_kernel, out_shape=(shape, shape, shape), grid_spec...]
    all_gather x1, waiting for transfers between devices: 19.9 us -> 28.5 us  [body(): lax.all_gather(states, 'head', axis=1, tiled=True)]
    pallas_call x1, Pallas kernels: 39.8 us -> 48.1 us  [cached_attention(): pl.pallas_call(functools.partial(cached_kernel, groups=groups, block_len=...]
  transfers between devices with their start and end apart: 4 -> 4, of which waited for: 2 -> 2; matrix products, arithmetic and copies ran while one was open for 26% -> 26% of each run, Pallas kernels for 27% -> 25%
where the time goes in v12:
time: 296 us; the launch traced here: 295 us
  waiting for transfers between devices  87.7 us (30%)
  Pallas kernels  74.5 us (25%)
  local copies, waits for them, and re-layouts  36.1 us (12%)
  other arithmetic  31.8 us (11%)
  starting transfers between devices  20.5 us (7%)
  matrix products  17.8 us (6%)
  between operations  14.4 us (5%)
  blocking collectives  11.9 us (4%)
    ppermute x1, waiting for transfers between devices, body(): partner_new = lax.ppermute(fresh_kv, 'bp', [(0, 1), (1, 0)])  58.6 us
    pallas_call x1, Pallas kernels, cached_attention(): pl.pallas_call(functools.partial(cached_kernel, groups=groups, block_len=...  48.1 us
    all_gather x1, waiting for transfers between devices, body(): lax.all_gather(states, 'head', axis=1, tiled=True)  28.5 us
    pallas_call x1, Pallas kernels, new_attention(): pl.pallas_call(functools.partial(new_kernel, partner=partner), out_shape=...  18.4 us
    dot_general x1, matrix products, body(): jnp.einsum('tc,jcw->tjw', lax.all_gather(states, 'head', axis=1, tiled=Tr...  17.8 us
    all_to_all x1, starting transfers between devices, body(): lax.all_to_all(picked, 'bx', split_axis=0, concat_axis=0, tiled=True)  12.7 us
    psum x1, blocking collectives, body(): lax.psum((jnp.sum(queries * queries, axis=1), jnp.sum(key_new * key_new,...  11.9 us
    gather x1, local copies, waits for them, and re-layouts, body(): jnp.take(kv_flat, out_ids.reshape(-1), axis=0, mode='clip')  9.01 us
  transfers between devices with their start and end apart: 4, of which 2 were waited for; matrix products, arithmetic and copies ran while one was open for 26% of the time, Pallas kernels for 25%

profile of v12, /device:TPU:118, one launch (start us, length us, event | category | flops | bytes accessed | tf_op | source)
XLA Modules:
  0.0 294.7 jit_solution(7534730856473079019)
XLA Ops:
  11.5 9.0 %gather_fusion.2 = bf16[128,64,512]{2,1,0:T(8,128)(2,1)} fusion(bf16[80,64,512]{2,1,0:T(8,128)(2,1)} %bitcast.42, s32[1024]{0:T(1024)S(1)} %pad_clamp_fusion.2), kind=kCustom, calls=%fused_computation.2 | custom fusion | bytes 16777728 | tf_op jit(solution)/shard_map/jit(_take)/gather | solution.py:281
  20.5 7.0 %all-to-all-start = ((bf16[16,2,4,64,512]{4,3,2,1,0:T(8,128)(2,1)}), bf16[16,2,4,64,512]{4,3,2,1,0:T(8,128)(2,1)}, u32[]{:S(2)}, u32[]{:S(2)}) async-start(bf16[16,2,4,64,512]{4,3,2,1,0:T(8,128)(2,1)} %bitcast.43), calls=%async_computation | async-start | bytes 16777216 | tf_op jit(solution)/shard_map/all_to_all | solution.py:284
  29.0 1.9 multiply_cosine_fusion
  30.9 28.5 %all-gather.2.cloned.1.call-done = bf16[1024,4096]{1,0:T(8,128)(2,1)} async-done(((bf16[1024,512]{1,0:T(8,128)(2,1)}), bf16[1024,4096]{1,0:T(8,128)(2,1)}) %all-gather.2.cloned.1.call-update) | async-done | bytes 8388624 | tf_op jit(solution)/shard_map/all_gather | solution.py:290
  59.3 17.8 %fusion = f32[1024,3,512]{0,2,1:T(8,128)S(1)} fusion(bf16[3,4096,512]{2,1,0:T(8,128)(2,1)} %param.8, bf16[1024,4096]{1,0:T(8,128)(2,1)} %all-gather.2.cloned.1.call-done), kind=kOutput, calls=%fused_computation.7 | convolution fusion | flops 12884901888 | bytes 27262976 | tf_op jit(solution)/shard_map/tc,jcw->tjw/dot_general | solution.py:288
  77.1 2.6 copy-done.8
  81.3 4.2 %multiply_reduce_fusion = (f32[1024]{0:T(1024)S(1)}, f32[1024]{0:T(1024)S(1)}, f32[1024,1,512]{0,2,1:T(8,128)S(1)}, f32[1024,1,512]{0,2,1:T(8,128)}) fusion(f32[1024,3,512]{0,2,1:T(8,128)} %copy-done.8), kind=kLoop, calls=%fused_computation.14 | loop fusion | flops 2095104 | bytes 8396800 | tf_op jit(solution)/shard_map/reduce_sum | solution.py:298
  85.5 1.8 copy.15
  87.3 11.9 %all-reduce = (f32[1024]{0:T(1024)S(1)}, f32[1024]{0:T(1024)S(1)}) all-reduce(f32[1024]{0:T(1024)S(1)} %get-tuple-element.9, f32[1024]{0:T(1024)S(1)} %get-tuple-element.8), channel_id=1, replica_groups=mesh['head'=8,'bx'=8,'bp'=2] {'head'}, use_global_device_ids=true, to_apply=%region_1.2 | all-reduce | flops 2048 | bytes 16384 | tf_op jit(solution)/shard_map/psum | solution.py:297
  99.2 4.1 %multiply_multiply_fusion = f32[1024,4,128]{2,1,0:T(4,128)S(1)} fusion(f32[1024,4,128]{2,1,0:T(4,128)} %copy.15, f32[4,128]{1,0:T(4,128)S(1)} %bitcast.59, f32[1024]{0:T(1024)S(1)} %get-tuple-element.30), kind=kLoop, calls=%fused_computation.13 | loop fusion | flops 1048576 | bytes 4200448 | tf_op jit(solution)/shard_map/mul | solution.py:302
  103.3 1.7 multiply_subtract_fusion
  112.2 3.6 %gather_fusion.4 = bf16[32,64,512]{2,1,0:T(8,128)(2,1)} fusion(bf16[32,64,512]{2,1,0:T(8,128)(2,1)} %bitcast.15, s32[1024]{0:T(1024)S(1)} %pad_clamp_fusion.1), kind=kCustom, calls=%fused_computation.4 | custom fusion | bytes 4194432 | tf_op jit(solution)/shard_map/jit(_take)/gather | solution.py:340
  115.8 58.6 %collective-permute-done.pk_ref.pv_ref = bf16[2,1024,512]{2,1,0:T(8,128)(2,1)S(1)} collective-permute-done((bf16[2,1024,512]{2,1,0:T(8,128)(2,1)}, bf16[2,1024,512]{2,1,0:T(8,128)(2,1)S(1)}, u32[]{:S(2)}, u32[]{:S(2)}) %collective-permute-start) | collective-permute-done | bytes 2097184 | tf_op jit(solution)/shard_map/ppermute | solution.py:322
  174.4 2.0 gather_fusion.5
  176.4 3.8 %broadcast_select_fusion = bf16[8,2,2,64,512]{4,3,2,1,0:T(8,128)(2,1)} fusion(bf16[8,2,2,64,512]{4,3,2,1,0:T(8,128)(2,1)} %bitcast.50, bf16[8,2,2,64,512]{4,3,2,1,0:T(8,128)(2,1)} %bitcast.51, pred[8,2]{1,0:T(8,128)(4,1)S(1)} %compare_or_fusion), kind=kLoop, calls=%fused_computation.19 | loop fusion | flops 1048576 | bytes 6291472 | tf_op jit(solution)/shard_map/jit(_where)/select_n | solution.py:345
  180.3 12.7 %all-to-all-start.1 = ((bf16[8,2,2,64,512]{4,3,2,1,0:T(8,128)(2,1)}), bf16[8,2,2,64,512]{4,3,2,1,0:T(8,128)(2,1)}, u32[]{:S(2)}, u32[]{:S(2)}) async-start(bf16[8,2,2,64,512]{4,3,2,1,0:T(8,128)(2,1)} %broadcast_select_fusion), calls=%async_computation.1 | async-start | bytes 4194304 | tf_op jit(solution)/shard_map/all_to_all | solution.py:348
  193.6 8.1 %shard_map.88 = bf16[2,40,64,512]{3,2,1,0:T(8,128)(2,1)} custom-call(bf16[2,40,64,512]{3,2,1,0:T(8,128)(2,1)} %src_ref.1), custom_call_target="tpu_custom_call" | custom-call | bytes 10485760 | tf_op jit(solution)/shard_map/pallas_call | solution.py:243
  201.7 1.9 pad_add_fusion.meta_ref
  203.6 1.8 copy.14
  205.5 4.2 %multiply_multiply_fusion.1 = f32[1024,4,128]{2,1,0:T(4,128)S(1)} fusion(f32[1024,4,128]{2,1,0:T(4,128)} %copy.14, f32[4,128]{1,0:T(4,128)S(1)} %bitcast.58, f32[1024]{0:T(1024)S(1)} %get-tuple-element.31), kind=kLoop, calls=%fused_computation.17 | loop fusion | flops 1048576 | bytes 4200448 | tf_op jit(solution)/shard_map/mul | solution.py:301
  209.7 1.7 subtract_convert_fusion
  215.1 18.4 %shard_map.86 = (f32[1024,512]{1,0:T(8,128)}, f32[1024,512]{1,0:T(8,128)}, f32[1024,512]{1,0:T(8,128)}) custom-call(s32[4]{0:T(128)} %pad_add_fusion.meta_ref, bf16[1024,512]{1,0:T(8,128)(2,1)} %bitcast.52, bf16[1024,512]{1,0:T(8,128)(2,1)} %bitcast.57, bf16[1024,512]{1,0:T(8,128)(2,1)} %bitcast.55), custom_call_target="tpu_custom_call" | custom-call | flops 1610612736 | bytes 15728640 | tf_op jit(solution)/shard_map/pallas_call | solution.py:161
  233.6 48.1 %shard_map.87 = bf16[1024,512]{1,0:T(8,128)(2,1)} custom-call(s32[4]{0:T(128)} %pad_add_fusion.meta_ref, bf16[1024,512]{1,0:T(8,128)(2,1)} %bitcast.53, bf16[2,1024,512]{2,1,0:T(8,128)(2,1)} %copy-done.2, bf16[2,1024,512]{2,1,0:T(8,128)(2,1)} %copy-done.2, bf16[16,2,4,64,512]{4,3,2,1,0:T(8,128)(2,1)} %all-to-all-done.k_ref.v_ref, ...), custom_call_target="tpu_custom_call" | custom-call | flops 4294967296 | bytes 12582912 | tf_op jit(solution)/shard_map/pallas_call | solution.py:201
  281.6 6.2 %scatter_fusion = bf16[80,64,512]{2,1,0:T(8,128)(2,1)} fusion(bf16[80,64,512]{2,1,0:T(8,128)(2,1)} %bitcast.45, s32[32]{0:T(128)S(1)} %fusion.28, bf16[32,64,512]{2,1,0:T(8,128)(2,1)} %bitcast.19), kind=kCustom, calls=%fused_computation.6 | custom fusion | bytes 6291584 | tf_op jit(solution)/shard_map/scatter | solution.py:358
  (82 shorter events, 18.8 us)
Async XLA Ops:
  7.2 3.3 %copy-start = (s32[8,64]{1,0:T(8,128)S(1)}, s32[8,64]{1,0:T(8,128)}, u32[]{:S(2)}) copy-start(s32[8,64]{1,0:T(8,128)} %param.12) | copy-start | bytes 6148
  7.2 52.2 %all-gather.2.cloned.1.call-start = ((), (), s32[]{:S(2)}) async-start(), calls=%async_computation.2 | async-start | bytes 9437184 | tf_op jit(solution)/shard_map/all_gather | solution.py:290
  20.5 7.0 %copy-start.10 = (bf16[2,512]{1,0:T(2,128)(2,1)S(1)}, bf16[2,512]{1,0:T(2,128)(2,1)}, u32[]{:S(2)}) copy-start(bf16[2,512]{1,0:T(2,128)(2,1)} %param.9) | copy-start | bytes 6148
  20.5 7.1 %copy-start.11 = (s32[8]{0:T(128)S(1)}, s32[8]{0:T(128)}, u32[]{:S(2)}) copy-start(s32[8]{0:T(128)} %param.11) | copy-start | bytes 100
  20.5 159.7 %all-to-all-start = ((bf16[16,2,4,64,512]{4,3,2,1,0:T(8,128)(2,1)}), bf16[16,2,4,64,512]{4,3,2,1,0:T(8,128)(2,1)}, u32[]{:S(2)}, u32[]{:S(2)}) async-start(bf16[16,2,4,64,512]{4,3,2,1,0:T(8,128)(2,1)} %bitcast.43), calls=%async_computation | async-start | bytes 16777216 | tf_op jit(solution)/shard_map/all_to_all | solution.py:284
  30.9 72.4 %copy-start.4 = (f32[1024,64]{1,0:T(8,128)}, f32[1024,64]{1,0:T(8,128)S(1)}, u32[]{:S(2)}) copy-start(f32[1024,64]{1,0:T(8,128)S(1)} %get-tuple-element.22) | copy-start | bytes 786436
  30.9 72.4 %copy-start.6 = (f32[1024,64]{1,0:T(8,128)}, f32[1024,64]{1,0:T(8,128)S(1)}, u32[]{:S(2)}) copy-start(f32[1024,64]{1,0:T(8,128)S(1)} %get-tuple-element.23) | copy-start | bytes 786436
  77.1 2.7 copy-start.8
  105.0 1.9 copy-start.9
  106.9 2.3 copy-start.1
  108.4 66.0 %collective-permute-start = (bf16[2,1024,512]{2,1,0:T(8,128)(2,1)}, bf16[2,1024,512]{2,1,0:T(8,128)(2,1)S(1)}, u32[]{:S(2)}, u32[]{:S(2)}) collective-permute-start(bf16[2,1024,512]{2,1,0:T(8,128)(2,1)} %pad_maximum_fusion), channel_id=1, source_target_pairs={{0,1},{1,0},{2,3},{3,2},{4,5},{5,4},{6,7},{7,6},{8,9},{9,8},{10,11... | collective-permute-start | bytes 6291464 | tf_op jit(solution)/shard_map/ppermute | solution.py:322
  174.4 2.0 copy-start.2
  180.3 101.4 %all-to-all-start.1 = ((bf16[8,2,2,64,512]{4,3,2,1,0:T(8,128)(2,1)}), bf16[8,2,2,64,512]{4,3,2,1,0:T(8,128)(2,1)}, u32[]{:S(2)}, u32[]{:S(2)}) async-start(bf16[8,2,2,64,512]{4,3,2,1,0:T(8,128)(2,1)} %broadcast_select_fusion), calls=%async_computation.1 | async-start | bytes 4194304 | tf_op jit(solution)/shard_map/all_to_all | solution.py:348
  193.6 10.0 %copy-start.3 = (f32[1024,1,512]{0,2,1:T(8,128)S(1)}, f32[1024,1,512]{0,2,1:T(8,128)}, u32[]{:S(2)}) copy-start(f32[1024,1,512]{0,2,1:T(8,128)} %get-tuple-element.17) | copy-start | bytes 6291460
  205.5 4.2 %copy-start.5 = (f32[1024,64]{1,0:T(8,128)S(1)}, f32[1024,64]{1,0:T(8,128)}, u32[]{:S(2)}) copy-start(f32[1024,64]{1,0:T(8,128)} %copy-done.4) | copy-start | bytes 786436
  205.5 4.2 %copy-start.7 = (f32[1024,64]{1,0:T(8,128)S(1)}, f32[1024,64]{1,0:T(8,128)}, u32[]{:S(2)}) copy-start(f32[1024,64]{1,0:T(8,128)} %copy-done.6) | copy-start | bytes 786436
Sparse Core Ops, SparseCore 0:
  9.7 49.6 all-gather.1

commit v13 on v12

--- a/solution.py
+++ b/solution.py
@@ -250,6 +250,35 @@
     )(cache)
 
 
+def place_kernel(ids_ref, blocks_ref, base_ref, out_ref, sems):
+    del base_ref
+    count = blocks_ref.shape[0]
+    copies = [
+        pltpu.make_async_copy(blocks_ref.at[i], out_ref.at[ids_ref[i]], sems.at[i])
+        for i in range(count)
+    ]
+    for copy in copies:
+        copy.start()
+    for copy in copies:
+        copy.wait()
+
+
+def place_blocks(ids, blocks, base):
+    count = blocks.shape[0]
+    return pl.pallas_call(
+        place_kernel,
+        out_shape=jax.ShapeDtypeStruct(base.shape, base.dtype),
+        grid_spec=pltpu.PrefetchScalarGridSpec(
+            num_scalar_prefetch=1,
+            grid=(),
+            in_specs=[pl.BlockSpec(memory_space=pl.ANY), pl.BlockSpec(memory_space=pl.ANY)],
+            out_specs=pl.BlockSpec(memory_space=pl.ANY),
+            scratch_shapes=[pltpu.SemaphoreType.DMA((count,))],
+        ),
+        input_output_aliases={2: 0},
+    )(ids, blocks, base)
+
+
 def body(states, qkv_weight, norm_gains, kv_cache, cached_len, old_table, new_table):
     tok_rows = states.shape[0]
     half_rows = tok_rows // 2
@@ -353,11 +382,9 @@
     )
     target_ids = kv_ids[None, :, None] * slot_count + target_slot[:, None, :]
     base = cache_copy(kv_cache).reshape(kv_flat.shape)
-    updated_cache = (
-        base.at[target_ids.reshape(-1)]
-        .set(arrived.reshape(-1, block_len, local_width), mode="drop")
-        .reshape(kv_cache.shape)
-    )
+    updated_cache = place_blocks(
+        target_ids.reshape(-1), arrived.reshape(-1, block_len, local_width), base
+    ).reshape(kv_cache.shape)
 
     attended = cached_attention(meta, queries, partner_new, received, *state)
     return (attended, updated_cache)

time: 296 us -> 356 us (1.20)
  the two profiles are of different devices: /device:TPU:118 before, /device:TPU:102 now
where the time goes in v13:
time: 356 us; the launch traced here: 355 us
  Pallas kernels  140 us (39%)
  waiting for transfers between devices  85.6 us (24%)
  other arithmetic  31.6 us (9%)
  local copies, waits for them, and re-layouts  30.3 us (9%)
  starting transfers between devices  20.5 us (6%)
  matrix products  17.8 us (5%)
  blocking collectives  14.4 us (4%)
  between operations  14.4 us (4%)
    pallas_call x1, Pallas kernels, place_blocks(): pl.pallas_call(place_kernel, out_shape=jax.ShapeDtypeStruct(base.shape, b...  65.6 us
    ppermute x1, waiting for transfers between devices, body(): partner_new = lax.ppermute(fresh_kv, 'bp', [(0, 1), (1, 0)])  55.1 us
    pallas_call x1, Pallas kernels, cached_attention(): pl.pallas_call(functools.partial(cached_kernel, groups=groups, block_len=...  48 us
    all_gather x1, waiting for transfers between devices, body(): lax.all_gather(states, 'head', axis=1, tiled=True)  29.9 us
    pallas_call x1, Pallas kernels, new_attention(): pl.pallas_call(functools.partial(new_kernel, partner=partner), out_shape=...  18.4 us
    dot_general x1, matrix products, body(): jnp.einsum('tc,jcw->tjw', lax.all_gather(states, 'head', axis=1, tiled=Tr...  17.8 us
    psum x1, blocking collectives, body(): lax.psum((jnp.sum(queries * queries, axis=1), jnp.sum(key_new * key_new,...  14.4 us
    all_to_all x1, starting transfers between devices, body(): lax.all_to_all(picked, 'bx', split_axis=0, concat_axis=0, tiled=True)  12.7 us
  transfers between devices with their start and end apart: 4, of which 2 were waited for; matrix products, arithmetic and copies ran while one was open for 22% of the time, Pallas kernels for 21%

profile of v13, /device:TPU:102, one launch (start us, length us, event | category | flops | bytes accessed | tf_op | source)
XLA Modules:
  0.0 354.7 jit_solution(10023138423513879988)
XLA Ops:
  11.5 9.0 %gather_fusion.2 = bf16[128,64,512]{2,1,0:T(8,128)(2,1)} fusion(bf16[80,64,512]{2,1,0:T(8,128)(2,1)} %bitcast.40, s32[1024]{0:T(1024)S(1)} %pad_clamp_fusion.2), kind=kCustom, calls=%fused_computation.2 | custom fusion | bytes 16777728 | tf_op jit(solution)/shard_map/jit(_take)/gather | solution.py:310
  20.5 7.0 %all-to-all-start = ((bf16[16,2,4,64,512]{4,3,2,1,0:T(8,128)(2,1)}), bf16[16,2,4,64,512]{4,3,2,1,0:T(8,128)(2,1)}, u32[]{:S(2)}, u32[]{:S(2)}) async-start(bf16[16,2,4,64,512]{4,3,2,1,0:T(8,128)(2,1)} %bitcast.41), calls=%async_computation | async-start | bytes 16777216 | tf_op jit(solution)/shard_map/all_to_all | solution.py:313
  28.8 1.9 multiply_cosine_fusion
  30.7 29.9 %all-gather.2.cloned.1.call-done = bf16[1024,4096]{1,0:T(8,128)(2,1)} async-done(((bf16[1024,512]{1,0:T(8,128)(2,1)}), bf16[1024,4096]{1,0:T(8,128)(2,1)}) %all-gather.2.cloned.1.call-update) | async-done | bytes 8388624 | tf_op jit(solution)/shard_map/all_gather | solution.py:319
  60.6 17.8 %fusion = f32[1024,3,512]{0,2,1:T(8,128)S(1)} fusion(bf16[3,4096,512]{2,1,0:T(8,128)(2,1)} %param.8, bf16[1024,4096]{1,0:T(8,128)(2,1)} %all-gather.2.cloned.1.call-done), kind=kOutput, calls=%fused_computation.6 | convolution fusion | flops 12884901888 | bytes 27262976 | tf_op jit(solution)/shard_map/tc,jcw->tjw/dot_general | solution.py:317
  78.4 2.7 copy-done.8
  82.6 4.2 %multiply_reduce_fusion = (f32[1024]{0:T(1024)S(1)}, f32[1024]{0:T(1024)S(1)}, f32[1024,1,512]{0,2,1:T(8,128)S(1)}, f32[1024,1,512]{0,2,1:T(8,128)}) fusion(f32[1024,3,512]{0,2,1:T(8,128)} %copy-done.8), kind=kLoop, calls=%fused_computation.13 | loop fusion | flops 2095104 | bytes 8396800 | tf_op jit(solution)/shard_map/reduce_sum | solution.py:327
  86.8 1.8 copy.16
  88.6 14.4 %all-reduce = (f32[1024]{0:T(1024)S(1)}, f32[1024]{0:T(1024)S(1)}) all-reduce(f32[1024]{0:T(1024)S(1)} %get-tuple-element.9, f32[1024]{0:T(1024)S(1)} %get-tuple-element.8), channel_id=1, replica_groups=mesh['head'=8,'bx'=8,'bp'=2] {'head'}, use_global_device_ids=true, to_apply=%region_1.2 | all-reduce | flops 2048 | bytes 16384 | tf_op jit(solution)/shard_map/psum | solution.py:326
  103.0 4.1 %multiply_multiply_fusion = f32[1024,4,128]{2,1,0:T(4,128)S(1)} fusion(f32[1024,4,128]{2,1,0:T(4,128)} %copy.16, f32[4,128]{1,0:T(4,128)S(1)} %bitcast.57, f32[1024]{0:T(1024)S(1)} %get-tuple-element.30), kind=kLoop, calls=%fused_computation.12 | loop fusion | flops 1048576 | bytes 4200448 | tf_op jit(solution)/shard_map/mul | solution.py:331
  107.1 1.7 multiply_subtract_fusion
  115.7 3.6 %gather_fusion.4 = bf16[32,64,512]{2,1,0:T(8,128)(2,1)} fusion(bf16[32,64,512]{2,1,0:T(8,128)(2,1)} %bitcast.13, s32[1024]{0:T(1024)S(1)} %pad_clamp_fusion.1), kind=kCustom, calls=%fused_computation.4 | custom fusion | bytes 4194432 | tf_op jit(solution)/shard_map/jit(_take)/gather | solution.py:369
  119.3 55.1 %collective-permute-done.pk_ref.pv_ref = bf16[2,1024,512]{2,1,0:T(8,128)(2,1)S(1)} collective-permute-done((bf16[2,1024,512]{2,1,0:T(8,128)(2,1)}, bf16[2,1024,512]{2,1,0:T(8,128)(2,1)S(1)}, u32[]{:S(2)}, u32[]{:S(2)}) %collective-permute-start) | collective-permute-done | bytes 2097184 | tf_op jit(solution)/shard_map/ppermute | solution.py:351
  174.4 2.0 gather_fusion.5
  176.4 3.8 %broadcast_select_fusion = bf16[8,2,2,64,512]{4,3,2,1,0:T(8,128)(2,1)} fusion(bf16[8,2,2,64,512]{4,3,2,1,0:T(8,128)(2,1)} %bitcast.48, bf16[8,2,2,64,512]{4,3,2,1,0:T(8,128)(2,1)} %bitcast.49, pred[8,2]{1,0:T(8,128)(4,1)S(1)} %compare_or_fusion), kind=kLoop, calls=%fused_computation.18 | loop fusion | flops 1048576 | bytes 6291472 | tf_op jit(solution)/shard_map/jit(_where)/select_n | solution.py:374
  180.2 12.7 %all-to-all-start.1 = ((bf16[8,2,2,64,512]{4,3,2,1,0:T(8,128)(2,1)}), bf16[8,2,2,64,512]{4,3,2,1,0:T(8,128)(2,1)}, u32[]{:S(2)}, u32[]{:S(2)}) async-start(bf16[8,2,2,64,512]{4,3,2,1,0:T(8,128)(2,1)} %broadcast_select_fusion), calls=%async_computation.1 | async-start | bytes 4194304 | tf_op jit(solution)/shard_map/all_to_all | solution.py:377
  193.6 8.1 %shard_map.88 = bf16[2,40,64,512]{3,2,1,0:T(8,128)(2,1)} custom-call(bf16[2,40,64,512]{3,2,1,0:T(8,128)(2,1)} %src_ref.1), custom_call_target="tpu_custom_call" | custom-call | bytes 10485760 | tf_op jit(solution)/shard_map/pallas_call | solution.py:243
  202.4 1.9 pad_add_fusion.meta_ref
  204.3 1.8 copy.15
  206.2 4.2 %multiply_multiply_fusion.1 = f32[1024,4,128]{2,1,0:T(4,128)S(1)} fusion(f32[1024,4,128]{2,1,0:T(4,128)} %copy.15, f32[4,128]{1,0:T(4,128)S(1)} %bitcast.56, f32[1024]{0:T(1024)S(1)} %get-tuple-element.31), kind=kLoop, calls=%fused_computation.16 | loop fusion | flops 1048576 | bytes 4200448 | tf_op jit(solution)/shard_map/mul | solution.py:330
  210.3 1.7 subtract_convert_fusion
  215.8 18.4 %shard_map.86 = (f32[1024,512]{1,0:T(8,128)}, f32[1024,512]{1,0:T(8,128)}, f32[1024,512]{1,0:T(8,128)}) custom-call(s32[4]{0:T(128)} %pad_add_fusion.meta_ref, bf16[1024,512]{1,0:T(8,128)(2,1)} %bitcast.50, bf16[1024,512]{1,0:T(8,128)(2,1)} %bitcast.55, bf16[1024,512]{1,0:T(8,128)(2,1)} %bitcast.53), custom_call_target="tpu_custom_call" | custom-call | flops 1610612736 | bytes 15728640 | tf_op jit(solution)/shard_map/pallas_call | solution.py:161
  234.2 48.0 %shard_map.87 = bf16[1024,512]{1,0:T(8,128)(2,1)} custom-call(s32[4]{0:T(128)} %pad_add_fusion.meta_ref, bf16[1024,512]{1,0:T(8,128)(2,1)} %bitcast.51, bf16[2,1024,512]{2,1,0:T(8,128)(2,1)} %copy-done.2, bf16[2,1024,512]{2,1,0:T(8,128)(2,1)} %copy-done.2, bf16[16,2,4,64,512]{4,3,2,1,0:T(8,128)(2,1)} %all-to-all-done.k_ref.v_ref, ...), custom_call_target="tpu_custom_call" | custom-call | flops 4294967296 | bytes 12582912 | tf_op jit(solution)/shard_map/pallas_call | solution.py:201
  282.3 65.6 %shard_map.89 = bf16[80,64,512]{2,1,0:T(8,128)(2,1)} custom-call(s32[32]{0:T(128)} %add.363.ids_ref, bf16[32,64,512]{2,1,0:T(8,128)(2,1)} %bitcast.17.blocks_ref, bf16[80,64,512]{2,1,0:T(8,128)(2,1)} %bitcast.42), custom_call_target="tpu_custom_call", output_to_operand_aliasing={{}: (2, {})} | custom-call | tf_op jit(solution)/shard_map/pallas_call | solution.py:268
  (81 shorter events, 19.0 us)
Async XLA Ops:
  7.2 3.3 copy-start
  7.2 53.4 %all-gather.2.cloned.1.call-start = ((), (), s32[]{:S(2)}) async-start(), calls=%async_computation.2 | async-start | bytes 9437184 | tf_op jit(solution)/shard_map/all_gather | solution.py:319
  20.5 7.0 %copy-start.11 = (s32[8]{0:T(128)S(1)}, s32[8]{0:T(128)}, u32[]{:S(2)}) copy-start(s32[8]{0:T(128)} %param.11) | copy-start | bytes 100
  20.5 8.3 %copy-start.10 = (bf16[2,512]{1,0:T(2,128)(2,1)S(1)}, bf16[2,512]{1,0:T(2,128)(2,1)}, u32[]{:S(2)}) copy-start(bf16[2,512]{1,0:T(2,128)(2,1)} %param.9) | copy-start | bytes 6148
  20.5 159.7 %all-to-all-start = ((bf16[16,2,4,64,512]{4,3,2,1,0:T(8,128)(2,1)}), bf16[16,2,4,64,512]{4,3,2,1,0:T(8,128)(2,1)}, u32[]{:S(2)}, u32[]{:S(2)}) async-start(bf16[16,2,4,64,512]{4,3,2,1,0:T(8,128)(2,1)} %bitcast.41), calls=%async_computation | async-start | bytes 16777216 | tf_op jit(solution)/shard_map/all_to_all | solution.py:313
  30.7 76.4 %copy-start.4 = (f32[1024,64]{1,0:T(8,128)}, f32[1024,64]{1,0:T(8,128)S(1)}, u32[]{:S(2)}) copy-start(f32[1024,64]{1,0:T(8,128)S(1)} %get-tuple-element.22) | copy-start | bytes 786436
  30.7 76.4 %copy-start.6 = (f32[1024,64]{1,0:T(8,128)}, f32[1024,64]{1,0:T(8,128)S(1)}, u32[]{:S(2)}) copy-start(f32[1024,64]{1,0:T(8,128)S(1)} %get-tuple-element.23) | copy-start | bytes 786436
  78.4 2.7 copy-start.8
  108.8 1.9 copy-start.9
  110.7 2.3 copy-start.1
  112.2 62.2 %collective-permute-start = (bf16[2,1024,512]{2,1,0:T(8,128)(2,1)}, bf16[2,1024,512]{2,1,0:T(8,128)(2,1)S(1)}, u32[]{:S(2)}, u32[]{:S(2)}) collective-permute-start(bf16[2,1024,512]{2,1,0:T(8,128)(2,1)} %pad_maximum_fusion), channel_id=1, source_target_pairs={{0,1},{1,0},{2,3},{3,2},{4,5},{5,4},{6,7},{7,6},{8,9},{9,8},{10,11... | collective-permute-start | bytes 6291464 | tf_op jit(solution)/shard_map/ppermute | solution.py:351
  174.4 2.0 copy-start.2
  180.2 102.0 %all-to-all-start.1 = ((bf16[8,2,2,64,512]{4,3,2,1,0:T(8,128)(2,1)}), bf16[8,2,2,64,512]{4,3,2,1,0:T(8,128)(2,1)}, u32[]{:S(2)}, u32[]{:S(2)}) async-start(bf16[8,2,2,64,512]{4,3,2,1,0:T(8,128)(2,1)} %broadcast_select_fusion), calls=%async_computation.1 | async-start | bytes 4194304 | tf_op jit(solution)/shard_map/all_to_all | solution.py:377
  193.6 10.8 %copy-start.3 = (f32[1024,1,512]{0,2,1:T(8,128)S(1)}, f32[1024,1,512]{0,2,1:T(8,128)}, u32[]{:S(2)}) copy-start(f32[1024,1,512]{0,2,1:T(8,128)} %get-tuple-element.17) | copy-start | bytes 6291460
  206.2 4.2 %copy-start.5 = (f32[1024,64]{1,0:T(8,128)S(1)}, f32[1024,64]{1,0:T(8,128)}, u32[]{:S(2)}) copy-start(f32[1024,64]{1,0:T(8,128)} %copy-done.4) | copy-start | bytes 786436
  206.2 4.2 %copy-start.7 = (f32[1024,64]{1,0:T(8,128)S(1)}, f32[1024,64]{1,0:T(8,128)}, u32[]{:S(2)}) copy-start(f32[1024,64]{1,0:T(8,128)} %copy-done.6) | copy-start | bytes 786436
Sparse Core Ops, SparseCore 0:
  9.7 50.9 all-gather.1
